TPU v7x, 32 devices: a whole 2x2x4 slice. The times are simulated.
32 devices in a mesh: grp: 2 (over x), wide: 16 (over z, y, core).
Axes of the slice: x: 2, y: 2, z: 4, core: 2. Of those that a mesh axis runs over, the one named last changes fastest.
Arguments:
- query_maps: bfloat16 [4096, 1024], P(('grp', 'wide')), parts along dimension 0
- source_maps: bfloat16 [4096, 1024], P(('grp', 'wide')), parts along dimension 0
- hubs: int32 [8], P('grp'), parts along dimension 0, may hold values from 0 to 15, as said below
- pick: int32 [32, 2], P(('grp', 'wide')), parts along dimension 0, may hold values from 0 to 3, all different within a row
- weight_first: bfloat16 [16, 1, 3, 3, 3, 3], replicated, may hold values from -0.625 to 0.625
- bias_first: float32 [16], replicated, may hold values from -0.6 to 0.6
- weight_second: bfloat16 [1, 16, 3, 3, 3, 3], replicated, may hold values from -0.15625 to 0.15625
- bias_second: float32 [1], replicated, may hold values from 0 to 0.2
Outputs:
- consensus: float32 [32, 2, 128, 128], P(('grp', 'wide')), parts along dimension 0
There are 2 independent parts, one for each index of `grp`. A program takes and returns all parts, laid end to end along the dimension named above; an argument that names none is the same for every part. Nothing has to cross between parts.
Inputs may be any that keep to these rules, and one draw needn't show every extreme that they name: `hubs`: distinct photo indices of the batch.
All inputs are finite; a program needn't handle non-finite values.
Results may differ from a plain program's by a relative error of at most 0.0063.
Values may be sent and summed in bfloat16 or wider, within the bound.
No kernel may reach another device: no remote copies, remote signals or barrier semaphores. Data moves between devices by JAX's collectives and lax.ppermute only.
A program may use at most 64 MiB of HBM per device.

v0:
```python
import jax
import jax.numpy as jnp
from jax import lax
from jax.sharding import PartitionSpec as P

HQ = 4
WQ = 32
HUBS = 4


def spread(value, axis, source):
    kept = jnp.where(lax.axis_index(axis) == source, value, 0).astype(value.dtype)
    return lax.psum(kept, axis)


def conv_volume(volume, kernel):
    padded = jnp.pad(volume, ((1, 1), (0, 0), (0, 0), (0, 0), (0, 0)))
    height = volume.shape[0]
    result = None
    for offset in range(3):
        term = lax.conv_general_dilated(
            padded[offset : offset + height],
            kernel[:, :, offset],
            (1, 1, 1),
            [(1, 1), (1, 1), (1, 1)],
            preferred_element_type=jnp.float32,
        )
        result = term if result is None else result + term
    return result


def consensus_net(matrix, weight_first, bias_first, weight_second, bias_second):
    cells = matrix.shape[0]
    volume = matrix.reshape(HQ, WQ, HQ, WQ)[:, None]
    preact = conv_volume(volume, weight_first) + bias_first[None, :, None, None, None]
    hidden = jax.nn.relu(preact).astype(jnp.bfloat16)
    result = jax.nn.relu(
        conv_volume(hidden, weight_second) + bias_second[None, :, None, None, None]
    )
    return result.reshape(cells, cells)


def scaled_corr(query, sources):
    query_f = query.astype(jnp.float32)
    sources_f = sources.astype(jnp.float32)
    query_rms = jnp.sqrt(jnp.mean(query_f * query_f, axis=-1) + 1e-06)
    source_rms = jnp.sqrt(jnp.mean(sources_f * sources_f, axis=-1) + 1e-06)
    inner = jnp.einsum("ac,jbc->jab", query, sources, preferred_element_type=jnp.float32)
    scale = jnp.sqrt(jnp.float32(query.shape[1]))
    return (inner / (scale * query_rms[None, :, None] * source_rms[:, None, :])).astype(
        jnp.bfloat16
    )


def per_device(
    query_maps, source_maps, hubs, pick, weight_first, bias_first, weight_second, bias_second
):
    owners = pick[0]
    cells, channels = source_maps.shape
    chosen = jnp.zeros((2, cells, channels), jnp.bfloat16)
    for index in range(HUBS):
        arrived = spread(source_maps, "wide", hubs[index])
        chosen = jnp.where((owners == index)[:, None, None], arrived[None], chosen)
    correlation = scaled_corr(query_maps, chosen)
    volumes = jnp.concatenate([correlation, jnp.swapaxes(correlation, 1, 2)], axis=0)

    def filter_one(matrix):
        return consensus_net(matrix, weight_first, bias_first, weight_second, bias_second)

    filtered = lax.map(filter_one, volumes)
    return (filtered[:2] + jnp.swapaxes(filtered[2:], 1, 2))[None]


def solution(mesh):
    return jax.shard_map(
        per_device,
        mesh=mesh,
        in_specs=(
            P(("grp", "wide"), None),
            P(("grp", "wide"), None),
            P("grp"),
            P(("grp", "wide"), None),
            P(),
            P(),
            P(),
            P(),
        ),
        out_specs=P(("grp", "wide"), None, None, None),
        check_vma=False,
    )
```

profile of v0, /device:TPU:0, one launch (start us, length us, event | category | flops | bytes accessed | tf_op | source)
XLA Modules:
  0.0 569.3 jit_solution(4240992218030931366)
XLA Ops:
  14.3 95.2 %all-reduce.5.cloned.1.call-done = (bf16[128,1024]{1,0:T(8,128)(2,1)}, bf16[128,1024]{1,0:T(8,128)(2,1)}, bf16[128,1024]{1,0:T(8,128)(2,1)}, bf16[128,1024]{1,0:T(8,128)(2,1)}) async-done(((bf16[128,1024]{1,0:T(8,128)(2,1)}, bf16[128,1024]{1,0:T(8,128)(2,1)}, bf16[128,1024]{1,0:T(8,128)(2,1)}, bf16[128,1024]{1,0:T(8,128)(2,1)}), (bf16[128,1024]{1,0:T(8,128)(2,1)}, bf16[128,1024]{1,0:T(8,128)(2,1)}, ...) | async-done | bytes 1048592 | tf_op jit(solution)/shard_map/psum | solution.py:13
  113.0 448.3 %while.12 = (s32[]{:T(128)}, f32[4,128,128]{2,1,0:T(8,128)S(1)}, bf16[4,128,128]{2,1,0:T(8,128)(2,1)S(1)}, bf16[16,1,3,3,3,3]{0,5,4,3,2,1:T(4,128)(2,1)S(1)}, f3...) while((s32[]{:T(128)}, f32[4,128,128]{2,1,0:T(8,128)S(1)}, ...), condition=%wide.region_7.8_spmd, body=%wide.region_6.7_spmd.sunk | while | flops 100311040 | bytes 41547692 | solution.py:70
  114.4 6.2 %fusion.91 = f32[32,4,32,5,16]{2,4,3,1,0:T(8,128)} fusion(bf16[1,32,4,32,7]{3,0,4,2,1:T(2,128)(2,1)S(1)} %copy.115, bf16[16,1,3,3,3]{0,4,3,2,1:T(4,128)(2,1)S(1)} %get-tuple-element.216), kind=kOutput, calls=%fused_computation.45.clone.1 | convolution fusion | flops 14438400 | bytes 1368928 | tf_op jit(solution)/shard_map/while/body/eval_jaxpr/conv_general_dilated | solution.py:21
  121.3 6.1 %fusion.89 = f32[32,4,32,5,16]{2,4,3,1,0:T(8,128)} fusion(bf16[1,32,4,32,7]{3,0,4,2,1:T(2,128)(2,1)S(1)} %copy.113, bf16[16,1,3,3,3]{0,4,3,2,1:T(4,128)(2,1)S(1)} %get-tuple-element.214), kind=kOutput, calls=%fused_computation.43.clone.1 | convolution fusion | flops 14438400 | bytes 1368928 | tf_op jit(solution)/shard_map/while/body/eval_jaxpr/conv_general_dilated | solution.py:21
  128.1 9.4 %broadcast_select_fusion.6 = (bf16[32,4,32,5,16]{2,4,3,1,0:T(8,128)(2,1)}, bf16[32,4,32,5,16]{2,4,3,1,0:T(8,128)(2,1)}) fusion(pred[32,5]{0,1:T(8,128)(4,1)S(1)} %get-tuple-element.254, f32[16]{0:T(128)S(1)} %get-tuple-element.250, bf16[1,32,4,32,7]{3,0,4,2,1:T(2,128)(2,1)S(1)} %copy.111, bf16[16,1,3,3,3]{0,4,3,2,1:T(4,128)(2,1)S(1)} %get-tuple-element.213, ...), kind=kOutput, calls=%fused_computation.14.clone.1 | convolution fusion | flops 17387520 | bytes 3990592 | tf_op jit(solution)/shard_map/while/body/eval_jaxpr/conv_general_dilated | solution.py:21
  137.5 5.5 copy.116
  148.2 10.4 %copy.120 = bf16[16,32,4,32,7]{3,0,4,2,1:T(8,128)(2,1)} copy(bf16[16,32,4,32,7]{1,0,4,3,2:T(8,128)(2,1)} %bitcast.140) | data formatting | bytes 1835008 | tf_op jit(solution)/shard_map/while/body/eval_jaxpr/conv_general_dilated | solution.py:21
  158.6 4.9 copy.118
  166.1 10.6 %copy.119 = bf16[32,4,32,7,16]{2,4,3,1,0:T(8,128)(2,1)} copy(bf16[32,4,32,7,16]{0,4,3,2,1:T(8,128)(2,1)} %bitcast.139) | data formatting | bytes 1835008 | tf_op jit(solution)/shard_map/while/body/eval_jaxpr/convert_element_type | solution.py:36
  177.4 2.3 fusion.93
  179.7 10.4 %copy.117 = bf16[16,32,4,32,7]{3,0,4,2,1:T(8,128)(2,1)} copy(bf16[16,32,4,32,7]{1,0,4,3,2:T(8,128)(2,1)} %bitcast.141) | data formatting | bytes 1835008 | tf_op jit(solution)/shard_map/while/body/eval_jaxpr/conv_general_dilated | solution.py:21
  190.2 11.0 %convolution_select_fusion.3 = f32[32,4,32,5,1]{2,4,3,1,0:T(1,128)S(1)} fusion(bf16[16,32,4,32,7]{3,0,4,2,1:T(8,128)(2,1)} %copy.117, pred[32,5]{0,1:T(8,128)(4,1)S(1)} %get-tuple-element.254, bf16[1,16,3,3,3]{1,4,3,2,0:T(4,128)(2,1)S(1)} %get-tuple-element.219), kind=kOutput, calls=%fused_computation.23.clone.1 | convolution fusion | flops 14458880 | bytes 1000448 | tf_op jit(solution)/shard_map/while/body/eval_jaxpr/conv_general_dilated | solution.py:21
  201.2 8.9 %convolution_add_fusion.2 = f32[32,4,32,5,1]{2,4,3,1,0:T(1,128)S(1)} fusion(f32[32,4,32,5,1]{2,4,3,1,0:T(1,128)S(1)} %convolution_select_fusion.3, bf16[32,4,32,7,16]{2,4,3,1,0:T(8,128)(2,1)S(1)} %copy-done.2, bf16[1,16,3,3,3]{1,4,3,2,0:T(4,128)(2,1)S(1)} %get-tuple-element.223), kind=kOutput, calls=%fused_computation.18.clone.1 | convolution fusion | flops 14458880 | bytes 1082208 | tf_op jit(solution)/shard_map/while/body/eval_jaxpr/conv_general_dilated | solution.py:21
  210.2 9.8 %fusion.97 = f32[32,4,32,5,1]{2,4,3,1,0:T(1,128)S(1)} fusion(f32[32,4,32,5,1]{2,4,3,1,0:T(1,128)S(1)} %convolution_add_fusion.2, bf16[16,32,4,32,7]{3,0,4,2,1:T(8,128)(2,1)S(1)} %copy-done.1, pred[32,5]{0,1:T(8,128)(4,1)S(1)} %get-tuple-element.254, f32[]{:T(128)} %bitcast.137, bf16[1,16,3,3,3]{1,4,3,2,0:T(4,128)(2,1)S(1)} %get-tuple-element.225), kind=kOutput, calls=%fused_computation.22.clone.1 | convolution fusion | flops 14520320 | bytes 1082372 | tf_op jit(solution)/shard_map/while/body/eval_jaxpr/conv_general_dilated | solution.py:21
  226.4 6.2 %fusion.91 = f32[32,4,32,5,16]{2,4,3,1,0:T(8,128)} fusion(bf16[1,32,4,32,7]{3,0,4,2,1:T(2,128)(2,1)S(1)} %copy.115, bf16[16,1,3,3,3]{0,4,3,2,1:T(4,128)(2,1)S(1)} %get-tuple-element.216), kind=kOutput, calls=%fused_computation.45.clone.1 | convolution fusion | flops 14438400 | bytes 1368928 | tf_op jit(solution)/shard_map/while/body/eval_jaxpr/conv_general_dilated | solution.py:21
  233.3 6.1 %fusion.89 = f32[32,4,32,5,16]{2,4,3,1,0:T(8,128)} fusion(bf16[1,32,4,32,7]{3,0,4,2,1:T(2,128)(2,1)S(1)} %copy.113, bf16[16,1,3,3,3]{0,4,3,2,1:T(4,128)(2,1)S(1)} %get-tuple-element.214), kind=kOutput, calls=%fused_computation.43.clone.1 | convolution fusion | flops 14438400 | bytes 1368928 | tf_op jit(solution)/shard_map/while/body/eval_jaxpr/conv_general_dilated | solution.py:21
  240.1 9.4 %broadcast_select_fusion.6 = (bf16[32,4,32,5,16]{2,4,3,1,0:T(8,128)(2,1)}, bf16[32,4,32,5,16]{2,4,3,1,0:T(8,128)(2,1)}) fusion(pred[32,5]{0,1:T(8,128)(4,1)S(1)} %get-tuple-element.254, f32[16]{0:T(128)S(1)} %get-tuple-element.250, bf16[1,32,4,32,7]{3,0,4,2,1:T(2,128)(2,1)S(1)} %copy.111, bf16[16,1,3,3,3]{0,4,3,2,1:T(4,128)(2,1)S(1)} %get-tuple-element.213, ...), kind=kOutput, calls=%fused_computation.14.clone.1 | convolution fusion | flops 17387520 | bytes 3990592 | tf_op jit(solution)/shard_map/while/body/eval_jaxpr/conv_general_dilated | solution.py:21
  249.5 5.1 copy.116
  259.9 10.4 %copy.120 = bf16[16,32,4,32,7]{3,0,4,2,1:T(8,128)(2,1)} copy(bf16[16,32,4,32,7]{1,0,4,3,2:T(8,128)(2,1)} %bitcast.140) | data formatting | bytes 1835008 | tf_op jit(solution)/shard_map/while/body/eval_jaxpr/conv_general_dilated | solution.py:21
  270.3 4.9 copy.118
  277.7 10.6 %copy.119 = bf16[32,4,32,7,16]{2,4,3,1,0:T(8,128)(2,1)} copy(bf16[32,4,32,7,16]{0,4,3,2,1:T(8,128)(2,1)} %bitcast.139) | data formatting | bytes 1835008 | tf_op jit(solution)/shard_map/while/body/eval_jaxpr/convert_element_type | solution.py:36
  289.1 2.3 fusion.93
  291.4 10.4 %copy.117 = bf16[16,32,4,32,7]{3,0,4,2,1:T(8,128)(2,1)} copy(bf16[16,32,4,32,7]{1,0,4,3,2:T(8,128)(2,1)} %bitcast.141) | data formatting | bytes 1835008 | tf_op jit(solution)/shard_map/while/body/eval_jaxpr/conv_general_dilated | solution.py:21
  301.8 11.1 %convolution_select_fusion.3 = f32[32,4,32,5,1]{2,4,3,1,0:T(1,128)S(1)} fusion(bf16[16,32,4,32,7]{3,0,4,2,1:T(8,128)(2,1)} %copy.117, pred[32,5]{0,1:T(8,128)(4,1)S(1)} %get-tuple-element.254, bf16[1,16,3,3,3]{1,4,3,2,0:T(4,128)(2,1)S(1)} %get-tuple-element.219), kind=kOutput, calls=%fused_computation.23.clone.1 | convolution fusion | flops 14458880 | bytes 1000448 | tf_op jit(solution)/shard_map/while/body/eval_jaxpr/conv_general_dilated | solution.py:21
  312.9 8.9 %convolution_add_fusion.2 = f32[32,4,32,5,1]{2,4,3,1,0:T(1,128)S(1)} fusion(f32[32,4,32,5,1]{2,4,3,1,0:T(1,128)S(1)} %convolution_select_fusion.3, bf16[32,4,32,7,16]{2,4,3,1,0:T(8,128)(2,1)S(1)} %copy-done.2, bf16[1,16,3,3,3]{1,4,3,2,0:T(4,128)(2,1)S(1)} %get-tuple-element.223), kind=kOutput, calls=%fused_computation.18.clone.1 | convolution fusion | flops 14458880 | bytes 1082208 | tf_op jit(solution)/shard_map/while/body/eval_jaxpr/conv_general_dilated | solution.py:21
  321.9 10.0 %fusion.97 = f32[32,4,32,5,1]{2,4,3,1,0:T(1,128)S(1)} fusion(f32[32,4,32,5,1]{2,4,3,1,0:T(1,128)S(1)} %convolution_add_fusion.2, bf16[16,32,4,32,7]{3,0,4,2,1:T(8,128)(2,1)S(1)} %copy-done.1, pred[32,5]{0,1:T(8,128)(4,1)S(1)} %get-tuple-element.254, f32[]{:T(128)} %bitcast.137, bf16[1,16,3,3,3]{1,4,3,2,0:T(4,128)(2,1)S(1)} %get-tuple-element.225), kind=kOutput, calls=%fused_computation.22.clone.1 | convolution fusion | flops 14520320 | bytes 1082372 | tf_op jit(solution)/shard_map/while/body/eval_jaxpr/conv_general_dilated | solution.py:21
  338.1 6.2 %fusion.91 = f32[32,4,32,5,16]{2,4,3,1,0:T(8,128)} fusion(bf16[1,32,4,32,7]{3,0,4,2,1:T(2,128)(2,1)S(1)} %copy.115, bf16[16,1,3,3,3]{0,4,3,2,1:T(4,128)(2,1)S(1)} %get-tuple-element.216), kind=kOutput, calls=%fused_computation.45.clone.1 | convolution fusion | flops 14438400 | bytes 1368928 | tf_op jit(solution)/shard_map/while/body/eval_jaxpr/conv_general_dilated | solution.py:21
  345.0 6.1 %fusion.89 = f32[32,4,32,5,16]{2,4,3,1,0:T(8,128)} fusion(bf16[1,32,4,32,7]{3,0,4,2,1:T(2,128)(2,1)S(1)} %copy.113, bf16[16,1,3,3,3]{0,4,3,2,1:T(4,128)(2,1)S(1)} %get-tuple-element.214), kind=kOutput, calls=%fused_computation.43.clone.1 | convolution fusion | flops 14438400 | bytes 1368928 | tf_op jit(solution)/shard_map/while/body/eval_jaxpr/conv_general_dilated | solution.py:21
  351.8 9.4 %broadcast_select_fusion.6 = (bf16[32,4,32,5,16]{2,4,3,1,0:T(8,128)(2,1)}, bf16[32,4,32,5,16]{2,4,3,1,0:T(8,128)(2,1)}) fusion(pred[32,5]{0,1:T(8,128)(4,1)S(1)} %get-tuple-element.254, f32[16]{0:T(128)S(1)} %get-tuple-element.250, bf16[1,32,4,32,7]{3,0,4,2,1:T(2,128)(2,1)S(1)} %copy.111, bf16[16,1,3,3,3]{0,4,3,2,1:T(4,128)(2,1)S(1)} %get-tuple-element.213, ...), kind=kOutput, calls=%fused_computation.14.clone.1 | convolution fusion | flops 17387520 | bytes 3990592 | tf_op jit(solution)/shard_map/while/body/eval_jaxpr/conv_general_dilated | solution.py:21
  361.1 5.2 copy.116
  371.6 10.4 %copy.120 = bf16[16,32,4,32,7]{3,0,4,2,1:T(8,128)(2,1)} copy(bf16[16,32,4,32,7]{1,0,4,3,2:T(8,128)(2,1)} %bitcast.140) | data formatting | bytes 1835008 | tf_op jit(solution)/shard_map/while/body/eval_jaxpr/conv_general_dilated | solution.py:21
  382.0 4.9 copy.118
  389.5 10.6 %copy.119 = bf16[32,4,32,7,16]{2,4,3,1,0:T(8,128)(2,1)} copy(bf16[32,4,32,7,16]{0,4,3,2,1:T(8,128)(2,1)} %bitcast.139) | data formatting | bytes 1835008 | tf_op jit(solution)/shard_map/while/body/eval_jaxpr/convert_element_type | solution.py:36
  403.1 10.4 %copy.117 = bf16[16,32,4,32,7]{3,0,4,2,1:T(8,128)(2,1)} copy(bf16[16,32,4,32,7]{1,0,4,3,2:T(8,128)(2,1)} %bitcast.141) | data formatting | bytes 1835008 | tf_op jit(solution)/shard_map/while/body/eval_jaxpr/conv_general_dilated | solution.py:21
  413.5 11.2 %convolution_select_fusion.3 = f32[32,4,32,5,1]{2,4,3,1,0:T(1,128)S(1)} fusion(bf16[16,32,4,32,7]{3,0,4,2,1:T(8,128)(2,1)} %copy.117, pred[32,5]{0,1:T(8,128)(4,1)S(1)} %get-tuple-element.254, bf16[1,16,3,3,3]{1,4,3,2,0:T(4,128)(2,1)S(1)} %get-tuple-element.219), kind=kOutput, calls=%fused_computation.23.clone.1 | convolution fusion | flops 14458880 | bytes 1000448 | tf_op jit(solution)/shard_map/while/body/eval_jaxpr/conv_general_dilated | solution.py:21
  424.8 8.9 %convolution_add_fusion.2 = f32[32,4,32,5,1]{2,4,3,1,0:T(1,128)S(1)} fusion(f32[32,4,32,5,1]{2,4,3,1,0:T(1,128)S(1)} %convolution_select_fusion.3, bf16[32,4,32,7,16]{2,4,3,1,0:T(8,128)(2,1)S(1)} %copy-done.2, bf16[1,16,3,3,3]{1,4,3,2,0:T(4,128)(2,1)S(1)} %get-tuple-element.223), kind=kOutput, calls=%fused_computation.18.clone.1 | convolution fusion | flops 14458880 | bytes 1082208 | tf_op jit(solution)/shard_map/while/body/eval_jaxpr/conv_general_dilated | solution.py:21
  433.8 9.7 %fusion.97 = f32[32,4,32,5,1]{2,4,3,1,0:T(1,128)S(1)} fusion(f32[32,4,32,5,1]{2,4,3,1,0:T(1,128)S(1)} %convolution_add_fusion.2, bf16[16,32,4,32,7]{3,0,4,2,1:T(8,128)(2,1)S(1)} %copy-done.1, pred[32,5]{0,1:T(8,128)(4,1)S(1)} %get-tuple-element.254, f32[]{:T(128)} %bitcast.137, bf16[1,16,3,3,3]{1,4,3,2,0:T(4,128)(2,1)S(1)} %get-tuple-element.225), kind=kOutput, calls=%fused_computation.22.clone.1 | convolution fusion | flops 14520320 | bytes 1082372 | tf_op jit(solution)/shard_map/while/body/eval_jaxpr/conv_general_dilated | solution.py:21
  449.8 6.2 %fusion.91 = f32[32,4,32,5,16]{2,4,3,1,0:T(8,128)} fusion(bf16[1,32,4,32,7]{3,0,4,2,1:T(2,128)(2,1)S(1)} %copy.115, bf16[16,1,3,3,3]{0,4,3,2,1:T(4,128)(2,1)S(1)} %get-tuple-element.216), kind=kOutput, calls=%fused_computation.45.clone.1 | convolution fusion | flops 14438400 | bytes 1368928 | tf_op jit(solution)/shard_map/while/body/eval_jaxpr/conv_general_dilated | solution.py:21
  456.7 6.1 %fusion.89 = f32[32,4,32,5,16]{2,4,3,1,0:T(8,128)} fusion(bf16[1,32,4,32,7]{3,0,4,2,1:T(2,128)(2,1)S(1)} %copy.113, bf16[16,1,3,3,3]{0,4,3,2,1:T(4,128)(2,1)S(1)} %get-tuple-element.214), kind=kOutput, calls=%fused_computation.43.clone.1 | convolution fusion | flops 14438400 | bytes 1368928 | tf_op jit(solution)/shard_map/while/body/eval_jaxpr/conv_general_dilated | solution.py:21
  463.5 9.4 %broadcast_select_fusion.6 = (bf16[32,4,32,5,16]{2,4,3,1,0:T(8,128)(2,1)}, bf16[32,4,32,5,16]{2,4,3,1,0:T(8,128)(2,1)}) fusion(pred[32,5]{0,1:T(8,128)(4,1)S(1)} %get-tuple-element.254, f32[16]{0:T(128)S(1)} %get-tuple-element.250, bf16[1,32,4,32,7]{3,0,4,2,1:T(2,128)(2,1)S(1)} %copy.111, bf16[16,1,3,3,3]{0,4,3,2,1:T(4,128)(2,1)S(1)} %get-tuple-element.213, ...), kind=kOutput, calls=%fused_computation.14.clone.1 | convolution fusion | flops 17387520 | bytes 3990592 | tf_op jit(solution)/shard_map/while/body/eval_jaxpr/conv_general_dilated | solution.py:21
  472.8 5.3 copy.116
  483.5 10.4 %copy.120 = bf16[16,32,4,32,7]{3,0,4,2,1:T(8,128)(2,1)} copy(bf16[16,32,4,32,7]{1,0,4,3,2:T(8,128)(2,1)} %bitcast.140) | data formatting | bytes 1835008 | tf_op jit(solution)/shard_map/while/body/eval_jaxpr/conv_general_dilated | solution.py:21
  493.9 4.9 copy.118
  501.4 10.6 %copy.119 = bf16[32,4,32,7,16]{2,4,3,1,0:T(8,128)(2,1)} copy(bf16[32,4,32,7,16]{0,4,3,2,1:T(8,128)(2,1)} %bitcast.139) | data formatting | bytes 1835008 | tf_op jit(solution)/shard_map/while/body/eval_jaxpr/convert_element_type | solution.py:36
  515.0 10.4 %copy.117 = bf16[16,32,4,32,7]{3,0,4,2,1:T(8,128)(2,1)} copy(bf16[16,32,4,32,7]{1,0,4,3,2:T(8,128)(2,1)} %bitcast.141) | data formatting | bytes 1835008 | tf_op jit(solution)/shard_map/while/body/eval_jaxpr/conv_general_dilated | solution.py:21
  525.4 11.0 %convolution_select_fusion.3 = f32[32,4,32,5,1]{2,4,3,1,0:T(1,128)S(1)} fusion(bf16[16,32,4,32,7]{3,0,4,2,1:T(8,128)(2,1)} %copy.117, pred[32,5]{0,1:T(8,128)(4,1)S(1)} %get-tuple-element.254, bf16[1,16,3,3,3]{1,4,3,2,0:T(4,128)(2,1)S(1)} %get-tuple-element.219), kind=kOutput, calls=%fused_computation.23.clone.1 | convolution fusion | flops 14458880 | bytes 1000448 | tf_op jit(solution)/shard_map/while/body/eval_jaxpr/conv_general_dilated | solution.py:21
  536.5 8.9 %convolution_add_fusion.2 = f32[32,4,32,5,1]{2,4,3,1,0:T(1,128)S(1)} fusion(f32[32,4,32,5,1]{2,4,3,1,0:T(1,128)S(1)} %convolution_select_fusion.3, bf16[32,4,32,7,16]{2,4,3,1,0:T(8,128)(2,1)S(1)} %copy-done.2, bf16[1,16,3,3,3]{1,4,3,2,0:T(4,128)(2,1)S(1)} %get-tuple-element.223), kind=kOutput, calls=%fused_computation.18.clone.1 | convolution fusion | flops 14458880 | bytes 1082208 | tf_op jit(solution)/shard_map/while/body/eval_jaxpr/conv_general_dilated | solution.py:21
  545.4 9.8 %fusion.97 = f32[32,4,32,5,1]{2,4,3,1,0:T(1,128)S(1)} fusion(f32[32,4,32,5,1]{2,4,3,1,0:T(1,128)S(1)} %convolution_add_fusion.2, bf16[16,32,4,32,7]{3,0,4,2,1:T(8,128)(2,1)S(1)} %copy-done.1, pred[32,5]{0,1:T(8,128)(4,1)S(1)} %get-tuple-element.254, f32[]{:T(128)} %bitcast.137, bf16[1,16,3,3,3]{1,4,3,2,0:T(4,128)(2,1)S(1)} %get-tuple-element.225), kind=kOutput, calls=%fused_computation.22.clone.1 | convolution fusion | flops 14520320 | bytes 1082372 | tf_op jit(solution)/shard_map/while/body/eval_jaxpr/conv_general_dilated | solution.py:21
  (192 shorter events, 61.4 us)
Async XLA Ops:
  6.5 104.6 %copy-start.5 = (bf16[128,1024]{1,0:T(8,128)(2,1)S(1)}, bf16[128,1024]{1,0:T(8,128)(2,1)}, u32[]{:S(2)}) copy-start(bf16[128,1024]{1,0:T(8,128)(2,1)} %param.10) | copy-start | bytes 786436
  6.5 103.0 %all-reduce.5.cloned.1.call-start = ((), (), s32[]{:S(2)}) async-start(), calls=%async_computation | async-start | bytes 2097152 | tf_op jit(solution)/shard_map/psum | solution.py:13
  10.4 102.5 %copy-start.3 = (bf16[16,1,3,3,3,3]{0,5,4,3,2,1:T(4,128)(2,1)S(1)}, bf16[16,1,3,3,3,3]{0,5,4,3,2,1:T(4,128)(2,1)}, u32[]{:S(2)}) copy-start(bf16[16,1,3,3,3,3]{0,5,4,3,2,1:T(4,128)(2,1)} %param.14) | copy-start | bytes 7780
  10.5 102.5 %copy-start.4 = (bf16[1,16,3,3,3,3]{1,5,4,3,2,0:T(4,128)(2,1)S(1)}, bf16[1,16,3,3,3,3]{1,5,4,3,2,0:T(4,128)(2,1)}, u32[]{:S(2)}) copy-start(bf16[1,16,3,3,3,3]{1,5,4,3,2,0:T(4,128)(2,1)} %param.16) | copy-start | bytes 7780
  10.5 102.5 %copy-start.6 = (f32[16]{0:T(128)S(1)}, f32[16]{0:T(128)}, u32[]{:S(2)}) copy-start(f32[16]{0:T(128)} %param.15) | copy-start | bytes 196
  10.5 102.5 %copy-start.7 = (pred[32,5]{0,1:T(8,128)(4,1)S(1)}, pred[32,5]{0,1:T(8,128)(4,1)}, u32[]{:S(2)}) copy-start(pred[32,5]{0,1:T(8,128)(4,1)} %constant.157) | copy-start | bytes 484
  166.1 10.6 %copy-start = (bf16[16,32,4,4,32]{1,0,4,3,2:T(8,128)(2,1)S(1)}, bf16[16,32,4,4,32]{1,0,4,3,2:T(8,128)(2,1)}, u32[]{:S(2)}) copy-start(bf16[16,32,4,4,32]{1,0,4,3,2:T(8,128)(2,1)} %get-tuple-element.218) | copy-start | bytes 1572868 | tf_op jit(solution)/shard_map/while
  190.2 11.0 %copy-start.2 = (bf16[32,4,32,7,16]{2,4,3,1,0:T(8,128)(2,1)S(1)}, bf16[32,4,32,7,16]{2,4,3,1,0:T(8,128)(2,1)}, u32[]{:S(2)}) copy-start(bf16[32,4,32,7,16]{2,4,3,1,0:T(8,128)(2,1)} %copy.119) | copy-start | bytes 2752516 | tf_op jit(solution)/shard_map/while
  201.2 9.0 %copy-start.1 = (bf16[16,32,4,32,7]{3,0,4,2,1:T(8,128)(2,1)S(1)}, bf16[16,32,4,32,7]{3,0,4,2,1:T(8,128)(2,1)}, u32[]{:S(2)}) copy-start(bf16[16,32,4,32,7]{3,0,4,2,1:T(8,128)(2,1)} %copy.120) | copy-start | bytes 2752516 | tf_op jit(solution)/shard_map/while
  277.7 10.6 %copy-start = (bf16[16,32,4,4,32]{1,0,4,3,2:T(8,128)(2,1)S(1)}, bf16[16,32,4,4,32]{1,0,4,3,2:T(8,128)(2,1)}, u32[]{:S(2)}) copy-start(bf16[16,32,4,4,32]{1,0,4,3,2:T(8,128)(2,1)} %get-tuple-element.218) | copy-start | bytes 1572868 | tf_op jit(solution)/shard_map/while
  301.8 11.1 %copy-start.2 = (bf16[32,4,32,7,16]{2,4,3,1,0:T(8,128)(2,1)S(1)}, bf16[32,4,32,7,16]{2,4,3,1,0:T(8,128)(2,1)}, u32[]{:S(2)}) copy-start(bf16[32,4,32,7,16]{2,4,3,1,0:T(8,128)(2,1)} %copy.119) | copy-start | bytes 2752516 | tf_op jit(solution)/shard_map/while
  312.9 9.0 %copy-start.1 = (bf16[16,32,4,32,7]{3,0,4,2,1:T(8,128)(2,1)S(1)}, bf16[16,32,4,32,7]{3,0,4,2,1:T(8,128)(2,1)}, u32[]{:S(2)}) copy-start(bf16[16,32,4,32,7]{3,0,4,2,1:T(8,128)(2,1)} %copy.120) | copy-start | bytes 2752516 | tf_op jit(solution)/shard_map/while
  389.5 10.6 %copy-start = (bf16[16,32,4,4,32]{1,0,4,3,2:T(8,128)(2,1)S(1)}, bf16[16,32,4,4,32]{1,0,4,3,2:T(8,128)(2,1)}, u32[]{:S(2)}) copy-start(bf16[16,32,4,4,32]{1,0,4,3,2:T(8,128)(2,1)} %get-tuple-element.218) | copy-start | bytes 1572868 | tf_op jit(solution)/shard_map/while
  413.5 11.3 %copy-start.2 = (bf16[32,4,32,7,16]{2,4,3,1,0:T(8,128)(2,1)S(1)}, bf16[32,4,32,7,16]{2,4,3,1,0:T(8,128)(2,1)}, u32[]{:S(2)}) copy-start(bf16[32,4,32,7,16]{2,4,3,1,0:T(8,128)(2,1)} %copy.119) | copy-start | bytes 2752516 | tf_op jit(solution)/shard_map/while
  424.8 9.0 %copy-start.1 = (bf16[16,32,4,32,7]{3,0,4,2,1:T(8,128)(2,1)S(1)}, bf16[16,32,4,32,7]{3,0,4,2,1:T(8,128)(2,1)}, u32[]{:S(2)}) copy-start(bf16[16,32,4,32,7]{3,0,4,2,1:T(8,128)(2,1)} %copy.120) | copy-start | bytes 2752516 | tf_op jit(solution)/shard_map/while
  501.4 10.6 %copy-start = (bf16[16,32,4,4,32]{1,0,4,3,2:T(8,128)(2,1)S(1)}, bf16[16,32,4,4,32]{1,0,4,3,2:T(8,128)(2,1)}, u32[]{:S(2)}) copy-start(bf16[16,32,4,4,32]{1,0,4,3,2:T(8,128)(2,1)} %get-tuple-element.218) | copy-start | bytes 1572868 | tf_op jit(solution)/shard_map/while
  525.4 11.0 %copy-start.2 = (bf16[32,4,32,7,16]{2,4,3,1,0:T(8,128)(2,1)S(1)}, bf16[32,4,32,7,16]{2,4,3,1,0:T(8,128)(2,1)}, u32[]{:S(2)}) copy-start(bf16[32,4,32,7,16]{2,4,3,1,0:T(8,128)(2,1)} %copy.119) | copy-start | bytes 2752516 | tf_op jit(solution)/shard_map/while
  536.5 9.0 %copy-start.1 = (bf16[16,32,4,32,7]{3,0,4,2,1:T(8,128)(2,1)S(1)}, bf16[16,32,4,32,7]{3,0,4,2,1:T(8,128)(2,1)}, u32[]{:S(2)}) copy-start(bf16[16,32,4,32,7]{3,0,4,2,1:T(8,128)(2,1)} %copy.120) | copy-start | bytes 2752516 | tf_op jit(solution)/shard_map/while
Sparse Core Ops, SparseCore 0:
  12.6 96.8 all-reduce.4
where the time goes:
time: 572 us; the launch traced here: 569 us
  matrix products  207 us (36%)
  local copies, waits for them, and re-layouts  196 us (34%)
  waiting for transfers between devices  95.2 us (17%)
  other arithmetic  35.3 us (6%)
  loops' own time  19.4 us (3%)
  between operations  16.3 us (3%)
    conv_general_dilated x24, matrix products, conv_volume(): lax.conv_general_dilated(padded[offset:offset + height], kernel[:, :, off...  206 us
    psum x1, waiting for transfers between devices, spread(): return lax.psum(kept, axis)  95.2 us
    conv_general_dilated x52, local copies, waits for them, and re-layouts, conv_volume(): lax.conv_general_dilated(padded[offset:offset + height], kernel[:, :, off...  89.9 us
    convert_element_type x20, local copies, waits for them, and re-layouts, consensus_net(): hidden = jax.nn.relu(preact).astype(jnp.bfloat16)  85.4 us
    conv_general_dilated x20, other arithmetic, conv_volume(): lax.conv_general_dilated(padded[offset:offset + height], kernel[:, :, off...  19.8 us
    another operation x1, loops' own time, per_device(): filtered = lax.map(filter_one, volumes)  19.4 us
    slice x24, local copies, waits for them, and re-layouts, conv_volume(): padded[offset:offset + height]  13.8 us
  transfers between devices with their start and end apart: 1, of which 1 were waited for; matrix products, arithmetic and copies ran while one was open for 0% of the time, Pallas kernels for 0%

commit v1 on v0

v1 whole, which is shorter than its diff:
```python
import numpy as np
import jax
import jax.numpy as jnp
from jax import lax
from jax.sharding import PartitionSpec as P

HQ = 4
WQ = 32
TAPS = 9


def spread(value, axis, source):
    kept = jnp.where(lax.axis_index(axis) == source, value, 0).astype(value.dtype)
    return lax.psum(kept, axis)


def tap_onehot():
    cells = HQ * WQ
    table = np.zeros((TAPS, cells, cells), np.float32)
    for b1 in range(HQ):
        for b2 in range(WQ):
            for e1 in range(3):
                for e2 in range(3):
                    p1, p2 = b1 + e1 - 1, b2 + e2 - 1
                    if 0 <= p1 < HQ and 0 <= p2 < WQ:
                        table[e1 * 3 + e2, p1 * WQ + p2, b1 * WQ + b2] = 1.0
    return jnp.asarray(table, jnp.bfloat16)


def row_shifts(x):
    cells = x.shape[1]
    pad = WQ + 1
    padded = jnp.pad(x, ((0, 0), (pad, pad), (0, 0)))
    col = np.arange(cells) % WQ
    outs = []
    for d in range(TAPS):
        d1, d2 = d // 3 - 1, d % 3 - 1
        off = d1 * WQ + d2
        part = lax.slice_in_dim(padded, pad + off, pad + off + cells, axis=1)
        valid = (col + d2 >= 0) & (col + d2 < WQ)
        outs.append(jnp.where(valid[None, :, None], part, jnp.zeros((), x.dtype)))
    return outs


def band_weights(weight_first, weight_second):
    onehot = tap_onehot()
    hid = weight_first.shape[0]
    cells = HQ * WQ
    w1 = weight_first.reshape(hid, TAPS, TAPS)
    w2 = weight_second.reshape(hid, TAPS, TAPS)
    k1 = jnp.einsum("cde,exy->dxcy", w1, onehot, preferred_element_type=jnp.float32)
    k1 = k1.astype(jnp.bfloat16).reshape(TAPS * cells, hid * cells)
    k2 = jnp.einsum("cde,exy->cxdy", w2, onehot, preferred_element_type=jnp.float32)
    k2 = k2.astype(jnp.bfloat16).reshape(hid * cells, TAPS * cells)
    return k1, k2


def consensus_stack(volumes, k1, k2, bias_first, bias_second):
    cells = volumes.shape[1]
    hid = bias_first.shape[0]
    stacked = jnp.concatenate(row_shifts(volumes), axis=-1)
    pre = jnp.einsum("vak,kn->van", stacked, k1, preferred_element_type=jnp.float32)
    pre = pre + jnp.repeat(bias_first, cells)[None, None, :]
    hidden = jax.nn.relu(pre).astype(jnp.bfloat16)
    part = jnp.einsum("vak,kn->van", hidden, k2, preferred_element_type=jnp.float32)
    pieces = [part[:, :, d * cells:(d + 1) * cells] for d in range(TAPS)]
    shifted = []
    for d in range(TAPS):
        shifted.append(row_shifts(pieces[d])[d])
    total = shifted[0]
    for d in range(1, TAPS):
        total = total + shifted[d]
    return jax.nn.relu(total + bias_second[0])


def scaled_corr(query, sources):
    query_f = query.astype(jnp.float32)
    sources_f = sources.astype(jnp.float32)
    query_rms = jnp.sqrt(jnp.mean(query_f * query_f, axis=-1) + 1e-06)
    source_rms = jnp.sqrt(jnp.mean(sources_f * sources_f, axis=-1) + 1e-06)
    inner = jnp.einsum("ac,jbc->jab", query, sources, preferred_element_type=jnp.float32)
    scale = jnp.sqrt(jnp.float32(query.shape[1]))
    return (inner / (scale * query_rms[None, :, None] * source_rms[:, None, :])).astype(
        jnp.bfloat16
    )


def per_device(
    query_maps, source_maps, hubs, pick, weight_first, bias_first, weight_second, bias_second
):
    owners = pick[0]
    cells, channels = source_maps.shape
    chosen = jnp.zeros((2, cells, channels), jnp.bfloat16)
    for index in range(hubs.shape[0]):
        arrived = spread(source_maps, "wide", hubs[index])
        chosen = jnp.where((owners == index)[:, None, None], arrived[None], chosen)
    correlation = scaled_corr(query_maps, chosen)
    volumes = jnp.concatenate([correlation, jnp.swapaxes(correlation, 1, 2)], axis=0)
    k1, k2 = band_weights(weight_first, weight_second)
    filtered = consensus_stack(volumes, k1, k2, bias_first, bias_second)
    return (filtered[:2] + jnp.swapaxes(filtered[2:], 1, 2))[None]


def solution(mesh):
    return jax.shard_map(
        per_device,
        mesh=mesh,
        in_specs=(
            P(("grp", "wide"), None),
            P(("grp", "wide"), None),
            P("grp"),
            P(("grp", "wide"), None),
            P(),
            P(),
            P(),
            P(),
        ),
        out_specs=P(("grp", "wide"), None, None, None),
        check_vma=False,
    )
```

time: 572 us -> 133 us (0.23)
  matrix products: 207 us -> 16.1 us
  local copies, waits for them, and re-layouts: 196 us -> 30.8 us
  waiting for transfers between devices: 95.2 us -> 63.6 us
  other arithmetic: 35.3 us -> 4.95 us
  loops' own time: 19.4 us -> 0 us
    conv_general_dilated x24 -> x0, matrix products: 206 us -> none  [conv_volume(): lax.conv_general_dilated(padded[offset:offset + height], kernel[:, :, off...]
    conv_general_dilated x52 -> x0, local copies, waits for them, and re-layouts: 89.9 us -> none  [conv_volume(): lax.conv_general_dilated(padded[offset:offset + height], kernel[:, :, off...]
    convert_element_type x20 -> x2, local copies, waits for them, and re-layouts: 85.4 us -> 10.9 us  [the longest x1 7.71 us: band_weights(): k2 = k2.astype(jnp.bfloat16).reshape(hid * cells, TAPS * cells)]
    psum x1, waiting for transfers between devices: 95.2 us -> 63.6 us  [spread(): return lax.psum(kept, axis)]
    conv_general_dilated x20 -> x0, other arithmetic: 19.8 us -> none  [conv_volume(): lax.conv_general_dilated(padded[offset:offset + height], kernel[:, :, off...]
    another operation x1 -> x0, loops' own time: 19.4 us -> none  [per_device(): filtered = lax.map(filter_one, volumes)]
    reshape x8 -> x4, local copies, waits for them, and re-layouts: 0.78 us -> 16.5 us  [the longest x1 8.26 us: band_weights(): k2 = k2.astype(jnp.bfloat16).reshape(hid * cells, TAPS * cells)]
    dot_general x0 -> x3, matrix products: none -> 14.6 us  [the longest x1 9.55 us: consensus_stack(): jnp.einsum('vak,kn->van', hidden, k2, preferred_element_type=jnp.float32)]
  transfers between devices with their start and end apart: 1 -> 1, of which waited for: 1 -> 1; matrix products, arithmetic and copies ran while one was open for 0% -> 25% of each run, Pallas kernels for 0% -> 0%
where the time goes in v1:
time: 133 us; the launch traced here: 132 us
  waiting for transfers between devices  63.6 us (48%)
  local copies, waits for them, and re-layouts  30.8 us (23%)
  between operations  16.9 us (13%)
  matrix products  16.1 us (12%)
  other arithmetic  4.95 us (4%)
    psum x1, waiting for transfers between devices, spread(): return lax.psum(kept, axis)  63.6 us
    dot_general x1, matrix products, consensus_stack(): jnp.einsum('vak,kn->van', hidden, k2, preferred_element_type=jnp.float32)  9.55 us
    reshape x1, local copies, waits for them, and re-layouts, band_weights(): k2 = k2.astype(jnp.bfloat16).reshape(hid * cells, TAPS * cells)  8.26 us
    reshape x1, local copies, waits for them, and re-layouts, band_weights(): k1 = k1.astype(jnp.bfloat16).reshape(TAPS * cells, hid * cells)  8.2 us
    convert_element_type x1, local copies, waits for them, and re-layouts, band_weights(): k2 = k2.astype(jnp.bfloat16).reshape(hid * cells, TAPS * cells)  7.71 us
    dot_general x1, matrix products, band_weights(): jnp.einsum('cde,exy->cxdy', w2, onehot, preferred_element_type=jnp.float32)  3.61 us
    convert_element_type x1, local copies, waits for them, and re-layouts, band_weights(): k1 = k1.astype(jnp.bfloat16).reshape(TAPS * cells, hid * cells)  3.17 us
  transfers between devices with their start and end apart: 1, of which 1 were waited for; matrix products, arithmetic and copies ran while one was open for 25% of the time, Pallas kernels for 0%

profile of v1, /device:TPU:0, one launch (start us, length us, event | category | flops | bytes accessed | tf_op | source)
XLA Modules:
  0.0 132.4 jit_solution(6491326838082933903)
XLA Ops:
  6.5 0.0 copy-start
  6.5 0.0 all-reduce.12.cloned.1.call-start
  6.5 1.5 %fusion.50 = (s32[1]{0:T(128)}, s32[1]{0:T(128)}, s32[1]{0:T(128)}, s32[1]{0:T(128)}) fusion(s32[4]{0:T(128)} %param.29), kind=kLoop, calls=%fused_computation.88 | loop fusion | bytes 32 | tf_op jit(solution)/shard_map/slice | solution.py:95
  10.5 0.0 copy-start.2
  10.5 0.0 copy-start.3
  10.6 0.0 copy-start.4
  10.6 0.0 copy-start.1
  10.6 2.0 %broadcast_select_fusion.3 = (bf16[128,1024]{1,0:T(8,128)(2,1)}, bf16[128,1024]{1,0:T(8,128)(2,1)}, bf16[128,1024]{1,0:T(8,128)(2,1)}, bf16[128,1024]{1,0:T(8,128)(2,1)}) fusion(bf16[128,1024]{1,0:T(8,128)(2,1)} %param.28, pred[]{:T(512)S(6)} %eq.54, pred[]{:T(512)S(6)} %eq.57, pred[]{:T(512)S(6)} %eq.63, pred[]{:T(512)S(6)} %eq.60), kind=kLoop, calls=%fused_computation.53 | loop fusion | flops 524288 | bytes 1310724 | tf_op jit(solution)/shard_map/jit(_where)/select_n | solution.py:13
  12.6 0.0 all-reduce.12.cloned.1.call-update
  12.6 0.0 copy-done.2
  12.7 0.1 multiply_reduce_fusion.1
  12.8 0.0 copy-done.3
  12.8 0.0 copy-done.4
  12.9 0.0 copy-done.1
  12.9 1.4 %convert_bitcast_fusion.1 = bf16[9,128,16,128]{3,2,0,1:T(8,128)(2,1)S(1)} fusion(bf16[9,128,128,1]{2,0,3,1:T(8,128)(2,1)S(1)} %copy-done.1, bf16[16,9,9]{0,2,1:T(8,128)(2,1)S(1)} %reshape.57), kind=kOutput, calls=%fused_computation.1 | convolution fusion | flops 44826624 | bytes 5016096 | tf_op jit(solution)/shard_map/cde,exy->dxcy/dot_general | solution.py:51
  14.3 3.6 %convert_bitcast_fusion = bf16[16,128,9,128]{3,0,2,1:T(8,128)(2,1)} fusion(bf16[9,128,128,1]{2,0,3,1:T(8,128)(2,1)S(1)} %copy-done.1, bf16[16,9,9]{0,2,1:T(8,128)(2,1)S(1)} %reshape.59), kind=kOutput, calls=%fused_computation | convolution fusion | flops 44826624 | bytes 5016096 | tf_op jit(solution)/shard_map/cde,exy->cxdy/dot_general | solution.py:53
  17.9 3.2 %copy.35 = bf16[9,128,16,128]{3,2,1,0:T(8,128)(2,1)} copy(bf16[9,128,16,128]{3,2,0,1:T(8,128)(2,1)S(1)} %convert_bitcast_fusion.1) | data formatting | bytes 9437184 | tf_op jit(solution)/shard_map/convert_element_type | solution.py:52
  21.1 8.2 %reshape.64 = bf16[1152,2048,1]{1,0,2:T(8,128)(2,1)} reshape(bf16[9,128,16,128]{3,2,1,0:T(8,128)(2,1)} %copy.35) | data formatting | bytes 9437184 | tf_op jit(solution)/shard_map/reshape | solution.py:52
  29.3 7.7 %copy.37 = bf16[16,128,9,128]{1,0,3,2:T(8,128)(2,1)} copy(bf16[16,128,9,128]{3,0,2,1:T(8,128)(2,1)} %convert_bitcast_fusion) | data formatting | bytes 9437184 | tf_op jit(solution)/shard_map/convert_element_type | solution.py:54
  37.0 0.0 copy-start.8
  37.0 8.3 %reshape.70 = bf16[2048,1152,1]{0,1,2:T(8,128)(2,1)} reshape(bf16[16,128,9,128]{1,0,3,2:T(8,128)(2,1)} %copy.37) | data formatting | bytes 9437184 | tf_op jit(solution)/shard_map/reshape | solution.py:54
  45.9 0.0 copy-done.8
  45.9 0.0 copy-done
  45.9 0.1 broadcast_bitcast_fusion
  46.0 63.6 %all-reduce.12.cloned.1.call-done = (bf16[128,1024]{1,0:T(8,128)(2,1)}, bf16[128,1024]{1,0:T(8,128)(2,1)}, bf16[128,1024]{1,0:T(8,128)(2,1)}, bf16[128,1024]{1,0:T(8,128)(2,1)}) async-done(((bf16[128,1024]{1,0:T(8,128)(2,1)}, bf16[128,1024]{1,0:T(8,128)(2,1)}, bf16[128,1024]{1,0:T(8,128)(2,1)}, bf16[128,1024]{1,0:T(8,128)(2,1)}), (bf16[128,1024]{1,0:T(8,128)(2,1)}, bf16[128,1024]{1,0:T(8,128)(2,1)}, ...) | async-done | bytes 1048592 | tf_op jit(solution)/shard_map/psum | solution.py:14
  109.6 1.6 %multiply_reduce_fusion = f32[2,128]{1,0:T(2,128)S(1)} fusion(pred[2]{0:T(512)(128)(4,1)S(1)} %get-tuple-element.29, pred[2]{0:T(512)(128)(4,1)S(1)} %get-tuple-element.30, pred[2]{0:T(512)(128)(4,1)S(1)} %get-tuple-element.28, pred[2]{0:T(512)(128)(4,1)S(1)} %get-tuple-element.27, bf16[128,1024]{1,0:T(8,128)(2,1)} %get-tuple-element.5, ...), kind=kLoop, calls=%fused_computation.3 | loop fusion | flops 1834752 | bytes 1049608 | tf_op jit(solution)/shard_map/reduce_sum | solution.py:80
  111.3 0.0 copy-start.5
  111.3 1.6 %fusion.1 = f32[2,128,128]{2,1,0:T(8,128)S(1)} fusion(pred[2]{0:T(512)(128)(4,1)S(1)} %get-tuple-element.29, pred[2]{0:T(512)(128)(4,1)S(1)} %get-tuple-element.30, pred[2]{0:T(512)(128)(4,1)S(1)} %get-tuple-element.28, pred[2]{0:T(512)(128)(4,1)S(1)} %get-tuple-element.27, bf16[128,1024]{1,0:T(8,128)(2,1)S(1)} %copy-done.2, ...), kind=kOutput, calls=%fused_computation.7 | convolution fusion | flops 68157440 | bytes 1441800 | tf_op jit(solution)/shard_map/ac,jbc->jab/dot_general | solution.py:81
  112.8 0.0 copy-start.6
  112.9 0.1 copy.33
  113.0 0.1 fusion.44
  113.1 0.0 copy-done.5
  113.1 0.1 fusion.29
  113.3 0.2 copy-done.6
  113.5 0.1 fusion.32
  113.6 0.1 fusion.34
  113.8 0.1 fusion.36
  113.9 0.1 fusion.38
  114.1 0.1 fusion.41
  114.2 9.5 %fusion = f32[4,128,1152]{2,1,0:T(8,128)S(1)} fusion(bf16[2048,1152,1]{0,1,2:T(8,128)(2,1)} %reshape.70, bf16[4,128,1152]{2,1,0:T(8,128)(2,1)S(1)} %fusion.41, bf16[1152,2048,1]{1,0,2:T(8,128)(2,1)} %reshape.64, f32[2048]{0:T(1024)S(1)} %broadcast_bitcast_fusion), kind=kOutput, calls=%fused_computation.4 | convolution fusion | flops 4834983936 | bytes 12984320 | tf_op jit(solution)/shard_map/vak,kn->van/dot_general | solution.py:65
  123.7 0.0 copy-start.7
  123.7 0.2 fusion.49
  124.0 0.4 copy-done.7
  124.4 0.3 fusion.16
  124.7 0.1 copy.48
  124.8 0.8 copy.40
  (11 shorter events, 0.2 us)
Async XLA Ops:
  6.5 39.4 %copy-start = (f32[16]{0:T(128)S(1)}, f32[16]{0:T(128)}, u32[]{:S(2)}) copy-start(f32[16]{0:T(128)} %param.32) | copy-start | bytes 196
  6.5 103.1 %all-reduce.12.cloned.1.call-start = ((), (), s32[]{:S(2)}) async-start(), calls=%async_computation | async-start | bytes 2097152 | tf_op jit(solution)/shard_map/psum | solution.py:14
  10.5 2.1 %copy-start.2 = (bf16[128,1024]{1,0:T(8,128)(2,1)S(1)}, bf16[128,1024]{1,0:T(8,128)(2,1)}, u32[]{:S(2)}) copy-start(bf16[128,1024]{1,0:T(8,128)(2,1)} %param.27) | copy-start | bytes 786436
  10.5 2.2 %copy-start.3 = (bf16[16,1,3,3,3,3]{0,5,4,3,2,1:T(4,128)(2,1)S(1)}, bf16[16,1,3,3,3,3]{0,5,4,3,2,1:T(4,128)(2,1)}, u32[]{:S(2)}) copy-start(bf16[16,1,3,3,3,3]{0,5,4,3,2,1:T(4,128)(2,1)} %param.31) | copy-start | bytes 7780
  10.6 2.3 %copy-start.4 = (bf16[1,16,3,3,3,3]{1,5,4,3,2,0:T(4,128)(2,1)S(1)}, bf16[1,16,3,3,3,3]{1,5,4,3,2,0:T(4,128)(2,1)}, u32[]{:S(2)}) copy-start(bf16[1,16,3,3,3,3]{1,5,4,3,2,0:T(4,128)(2,1)} %param.33) | copy-start | bytes 7780
  10.6 2.3 %copy-start.1 = (bf16[9,128,128,1]{2,0,3,1:T(8,128)(2,1)S(1)}, bf16[9,128,128,1]{2,0,3,1:T(8,128)(2,1)}, u32[]{:S(2)}) copy-start(bf16[9,128,128,1]{2,0,3,1:T(8,128)(2,1)} %constant.67) | copy-start | bytes 884740
  37.0 8.9 %copy-start.8 = (s32[1,2]{1,0:T(1,128)S(1)}, s32[1,2]{1,0:T(1,128)}, u32[]{:S(2)}) copy-start(s32[1,2]{1,0:T(1,128)} %param.30) | copy-start | bytes 28
  111.3 1.9 %copy-start.5 = (pred[128]{0:T(512)(128)(4,1)S(1)}, pred[128]{0:T(512)(128)(4,1)}, u32[]{:S(2)}) copy-start(pred[128]{0:T(512)(128)(4,1)} %constant.65) | copy-start | bytes 388
  112.8 0.7 copy-start.6
  123.7 0.7 copy-start.7
Sparse Core Ops, SparseCore 0:
  12.8 96.8 all-reduce.11

commit v2 on v1

--- a/solution.py
+++ b/solution.py
@@ -9,22 +9,34 @@
 TAPS = 9
 
 
-def spread(value, axis, source):
-    kept = jnp.where(lax.axis_index(axis) == source, value, 0).astype(value.dtype)
-    return lax.psum(kept, axis)
+def tap_table(cells, cols):
+    row = lax.broadcasted_iota(jnp.int32, (cells, cols), 0)
+    col = lax.broadcasted_iota(jnp.int32, (cells, cols), 1) % cells
+    e1 = row // WQ - col // WQ + 1
+    e2 = row % WQ - col % WQ + 1
+    inside = (e1 >= 0) & (e1 < 3) & (e2 >= 0) & (e2 < 3)
+    return jnp.where(inside, e1 * 3 + e2, -1)
 
 
-def tap_onehot():
+def banded(weights, table, cells):
+    rows, _, groups = weights.shape
+    spread_w = jnp.repeat(weights, cells, axis=2)
+    band = jnp.zeros((rows, cells, groups * cells), weights.dtype)
+    for e in range(TAPS):
+        band = jnp.where(table[None] == e, spread_w[:, e, None, :], band)
+    return band
+
+
+def band_weights(weight_first, weight_second):
+    hid = weight_first.shape[0]
     cells = HQ * WQ
-    table = np.zeros((TAPS, cells, cells), np.float32)
-    for b1 in range(HQ):
-        for b2 in range(WQ):
-            for e1 in range(3):
-                for e2 in range(3):
-                    p1, p2 = b1 + e1 - 1, b2 + e2 - 1
-                    if 0 <= p1 < HQ and 0 <= p2 < WQ:
-                        table[e1 * 3 + e2, p1 * WQ + p2, b1 * WQ + b2] = 1.0
-    return jnp.asarray(table, jnp.bfloat16)
+    w1 = weight_first.reshape(hid, TAPS, TAPS)
+    w2 = weight_second.reshape(hid, TAPS, TAPS)
+    k1 = banded(jnp.transpose(w1, (1, 2, 0)), tap_table(cells, hid * cells), cells)
+    k1 = k1.reshape(TAPS * cells, hid * cells)
+    k2 = banded(jnp.transpose(w2, (0, 2, 1)), tap_table(cells, TAPS * cells), cells)
+    k2 = k2.reshape(hid * cells, TAPS * cells)
+    return k1, k2
 
 
 def row_shifts(x):
@@ -40,19 +52,6 @@
         valid = (col + d2 >= 0) & (col + d2 < WQ)
         outs.append(jnp.where(valid[None, :, None], part, jnp.zeros((), x.dtype)))
     return outs
-
-
-def band_weights(weight_first, weight_second):
-    onehot = tap_onehot()
-    hid = weight_first.shape[0]
-    cells = HQ * WQ
-    w1 = weight_first.reshape(hid, TAPS, TAPS)
-    w2 = weight_second.reshape(hid, TAPS, TAPS)
-    k1 = jnp.einsum("cde,exy->dxcy", w1, onehot, preferred_element_type=jnp.float32)
-    k1 = k1.astype(jnp.bfloat16).reshape(TAPS * cells, hid * cells)
-    k2 = jnp.einsum("cde,exy->cxdy", w2, onehot, preferred_element_type=jnp.float32)
-    k2 = k2.astype(jnp.bfloat16).reshape(hid * cells, TAPS * cells)
-    return k1, k2
 
 
 def consensus_stack(volumes, k1, k2, bias_first, bias_second):
@@ -85,15 +84,22 @@
     )
 
 
+def gather_sources(source_maps, hubs, pick, wide):
+    cells, channels = source_maps.shape
+    rows = cells // wide
+    chunks = lax.all_to_all(source_maps.reshape(wide, rows, channels), "wide", 0, 0)
+    picks = lax.all_to_all(jnp.broadcast_to(pick[0][None], (wide, 2)), "wide", 0, 0)
+    owners = hubs[picks]
+    parcel = chunks[owners]
+    got = lax.all_to_all(parcel, "wide", 0, 0)
+    return jnp.swapaxes(got, 0, 1).reshape(2, cells, channels)
+
+
 def per_device(
-    query_maps, source_maps, hubs, pick, weight_first, bias_first, weight_second, bias_second
+    query_maps, source_maps, hubs, pick, weight_first, bias_first, weight_second, bias_second,
+    wide,
 ):
-    owners = pick[0]
-    cells, channels = source_maps.shape
-    chosen = jnp.zeros((2, cells, channels), jnp.bfloat16)
-    for index in range(hubs.shape[0]):
-        arrived = spread(source_maps, "wide", hubs[index])
-        chosen = jnp.where((owners == index)[:, None, None], arrived[None], chosen)
+    chosen = gather_sources(source_maps, hubs, pick, wide)
     correlation = scaled_corr(query_maps, chosen)
     volumes = jnp.concatenate([correlation, jnp.swapaxes(correlation, 1, 2)], axis=0)
     k1, k2 = band_weights(weight_first, weight_second)
@@ -102,8 +108,13 @@
 
 
 def solution(mesh):
+    wide = mesh.shape["wide"]
+
+    def body(*args):
+        return per_device(*args, wide)
+
     return jax.shard_map(
-        per_device,
+        body,
         mesh=mesh,
         in_specs=(
             P(("grp", "wide"), None),

time: 133 us -> 74 us (0.56)
  waiting for transfers between devices: 63.6 us -> 15.5 us
  local copies, waits for them, and re-layouts: 30.8 us -> 8.59 us
  starting transfers between devices: 0.01 us -> 17.2 us
  between operations: 16.9 us -> 1.03 us
  other arithmetic: 4.95 us -> 20.1 us
  matrix products: 16.1 us -> 11.1 us
    psum x1 -> x0, waiting for transfers between devices: 63.6 us -> none  [spread(): return lax.psum(kept, axis)]
    all_to_all x0 -> x3, starting transfers between devices: none -> 17.2 us  [the longest x1 7.42 us: gather_sources(): lax.all_to_all(jnp.broadcast_to(pick[0][None], (wide, 2)), 'wide', 0, 0)]
    reshape x2, local copies, waits for them, and re-layouts: 16.5 us -> 0.36 us  [banded(): spread_w = jnp.repeat(weights, cells, axis=2)]
    all_to_all x0 -> x3, waiting for transfers between devices: none -> 15.5 us  [the longest x1 8.64 us: gather_sources(): lax.all_to_all(source_maps.reshape(wide, rows, channels), 'wide', 0, 0)]
    select_n x1 -> x4, other arithmetic: 2.03 us -> 14.5 us  [the longest x2 14.5 us: banded(): band = jnp.where(table[None] == e, spread_w[:, e, None, :], band)]
    convert_element_type x2 -> x0, local copies, waits for them, and re-layouts: 10.9 us -> none  [the longest x1 7.71 us: band_weights(): k2 = k2.astype(jnp.bfloat16).reshape(hid * cells, TAPS * cells)]
    dot_general x2 -> x0, matrix products: 5.02 us -> none  [the longest x1 3.61 us: band_weights(): jnp.einsum('cde,exy->cxdy', w2, onehot, preferred_element_type=jnp.float32)]
    eq x1 -> x2, other arithmetic: 0.01 us -> 4.03 us  [banded(): band = jnp.where(table[None] == e, spread_w[:, e, None, :], band)]
  transfers between devices with their start and end apart: 1 -> 3, of which waited for: 1 -> 2; matrix products, arithmetic and copies ran while one was open for 25% -> 30% of each run, Pallas kernels for 0% -> 0%
where the time goes in v2:
time: 74 us; the launch traced here: 73.5 us
  other arithmetic  20.1 us (27%)
  starting transfers between devices  17.2 us (23%)
  waiting for transfers between devices  15.5 us (21%)
  matrix products  11.1 us (15%)
  local copies, waits for them, and re-layouts  8.59 us (12%)
  between operations  1.03 us (1%)
    select_n x2, other arithmetic, banded(): band = jnp.where(table[None] == e, spread_w[:, e, None, :], band)  14.5 us
    dot_general x1, matrix products, consensus_stack(): jnp.einsum('vak,kn->van', hidden, k2, preferred_element_type=jnp.float32)  9.82 us
    all_to_all x1, waiting for transfers between devices, gather_sources(): lax.all_to_all(source_maps.reshape(wide, rows, channels), 'wide', 0, 0)  8.64 us
    all_to_all x1, starting transfers between devices, gather_sources(): lax.all_to_all(jnp.broadcast_to(pick[0][None], (wide, 2)), 'wide', 0, 0)  7.42 us
    all_to_all x1, waiting for transfers between devices, gather_sources(): got = lax.all_to_all(parcel, 'wide', 0, 0)  6.89 us
    all_to_all x1, starting transfers between devices, gather_sources(): lax.all_to_all(source_maps.reshape(wide, rows, channels), 'wide', 0, 0)  6.02 us
    eq x2, other arithmetic, banded(): band = jnp.where(table[None] == e, spread_w[:, e, None, :], band)  4.03 us
    all_to_all x1, starting transfers between devices, gather_sources(): got = lax.all_to_all(parcel, 'wide', 0, 0)  3.75 us
  transfers between devices with their start and end apart: 3, of which 2 were waited for; matrix products, arithmetic and copies ran while one was open for 30% of the time, Pallas kernels for 0%

profile of v2, /device:TPU:0, one launch (start us, length us, event | category | flops | bytes accessed | tf_op | source)
XLA Modules:
  0.0 73.5 jit_solution(1627659417812735402)
XLA Ops:
  0.0 1.3 %broadcast_in_dim.477 = s32[16,1,2]{2,1,0:T(1,128)} broadcast(s32[2]{0:T(128)} %bitcast.97), dimensions={2} | broadcast | bytes 136 | tf_op jit(solution)/shard_map/broadcast_in_dim | solution.py:91
  1.3 7.4 %all-to-all-start.1 = ((s32[16,1,2]{2,1,0:T(1,128)}), s32[16,1,2]{2,1,0:T(1,128)S(1)}, u32[]{:S(2)}, u32[]{:S(2)}) async-start(s32[16,1,2]{2,1,0:T(1,128)} %broadcast_in_dim.477), calls=%async_computation.1 | async-start | bytes 16384 | tf_op jit(solution)/shard_map/all_to_all | solution.py:91
  8.8 0.8 %reshape.2167 = bf16[16,9,9]{0,2,1:T(8,128)(2,1)S(1)} reshape(bf16[16,1,3,3,3,3]{0,5,4,3,2,1:T(4,128)(2,1)} %param.30) | data formatting | bytes 5184 | tf_op jit(solution)/shard_map/reshape | solution.py:33
  9.6 0.2 broadcast_in_dim.497
  9.8 0.2 reshape.2168
  10.1 0.1 multiply_reduce_fusion.1
  10.3 0.1 copy.72
  10.4 0.4 broadcast_in_dim.537
  10.8 0.2 reshape.2170
  11.0 0.1 broadcast_bitcast_fusion
  11.1 2.3 %broadcast_compare_fusion.4 = (pred[128,2048]{1,0:T(8,128)(4,1)S(1)}, pred[128,2048]{1,0:T(8,128)(4,1)S(1)}, pred[128,2048]{1,0:T(8,128)(4,1)S(1)}, pred[128,204...) fusion(s32[128]{0:T(128)S(1)} %get-tuple-element.56, ...), kind=kLoop, calls=%fused_computation.48 | loop fusion | flops 11796480 | bytes 2380032 | tf_op jit(solution)/shard_map/eq | solution.py:26
  13.4 1.7 %broadcast_compare_fusion.13 = (pred[128,1152]{1,0:T(8,128)(4,1)S(1)}, pred[128,1152]{1,0:T(8,128)(4,1)S(1)}, pred[128,1152]{1,0:T(8,128)(4,1)S(1)}, pred[128,11...) fusion(s32[128]{0:T(128)S(1)} %get-tuple-element.56, ...), kind=kLoop, calls=%fused_computation.66 | loop fusion | flops 6635520 | bytes 1339776 | tf_op jit(solution)/shard_map/eq | solution.py:26
  15.1 0.0 copy-start.1
  15.1 7.3 %select_select_fusion = bf16[16,128,1152]{2,1,0:T(8,128)(2,1)} fusion(pred[128,1152]{1,0:T(8,128)(4,1)S(1)} %get-tuple-element.45, pred[128,1152]{1,0:T(8,128)(4,1)S(1)} %get-tuple-element.44, pred[128,1152]{1,0:T(8,128)(4,1)S(1)} %get-tuple-element.43, pred[128,1152]{1,0:T(8,128)(4,1)S(1)} %get-tuple-element.42, pred[128,1152]{1,0:T(8,128)(4,1)S(1)} %get-tuple-element.41, ...), kind=kLoop, calls=%fused_computation.2 | loop fusion | flops 21233664 | bytes 6377472 | tf_op jit(solution)/shard_map/jit(_where)/select_n | solution.py:26
  23.2 0.0 all-to-all-done.1
  23.2 6.0 %all-to-all-start = ((bf16[16,8,1024]{2,1,0:T(8,128)(2,1)}), bf16[16,8,1024]{2,1,0:T(8,128)(2,1)S(1)}, u32[]{:S(2)}, u32[]{:S(2)}) async-start(bf16[16,8,1024]{2,1,0:T(8,128)(2,1)} %bitcast), calls=%async_computation | async-start | bytes 524288 | tf_op jit(solution)/shard_map/all_to_all | solution.py:90
  29.2 0.1 copy.61
  29.3 0.1 copy.62
  29.4 0.1 reshape.2181
  29.5 0.7 gather_fusion
  30.2 0.1 gather.9
  30.3 0.1 copy.63
  30.4 0.1 copy.66
  30.4 0.1 reshape.2189
  30.6 8.6 %all-to-all-done = bf16[16,8,1024]{2,1,0:T(8,128)(2,1)S(1)} async-done(((bf16[16,8,1024]{2,1,0:T(8,128)(2,1)}), bf16[16,8,1024]{2,1,0:T(8,128)(2,1)S(1)}, u32[]{:S(2)}, u32[]{:S(2)}) %all-to-all-start) | async-done | bytes 262176 | tf_op jit(solution)/shard_map/all_to_all | solution.py:90
  39.2 1.4 %gather_fusion.1 = bf16[32,8,1024]{2,1,0:T(8,128)(2,1)} fusion(bf16[16,8,1024]{2,1,0:T(8,128)(2,1)S(1)} %all-to-all-done, s32[1024]{0:T(1024)S(1)} %pad_clamp_fusion), kind=kCustom, calls=%fused_computation.1 | custom fusion | bytes 1048704 | tf_op jit(solution)/shard_map/gather | solution.py:93
  40.6 3.8 %all-to-all-start.2 = ((bf16[16,2,8,1024]{3,2,1,0:T(8,128)(2,1)}), bf16[16,2,8,1024]{3,2,1,0:T(8,128)(2,1)S(1)}, u32[]{:S(2)}, u32[]{:S(2)}) async-start(bf16[16,2,8,1024]{3,2,1,0:T(8,128)(2,1)} %bitcast.3), calls=%async_computation.2 | async-start | bytes 1048576 | tf_op jit(solution)/shard_map/all_to_all | solution.py:94
  44.3 7.2 %select_select_fusion.1 = bf16[9,128,2048]{2,1,0:T(8,128)(2,1)} fusion(pred[128,2048]{1,0:T(8,128)(4,1)S(1)} %get-tuple-element.39, pred[128,2048]{1,0:T(8,128)(4,1)S(1)} %get-tuple-element.38, pred[128,2048]{1,0:T(8,128)(4,1)S(1)} %get-tuple-element.37, pred[128,2048]{1,0:T(8,128)(4,1)S(1)} %get-tuple-element.36, ...), kind=kLoop, calls=%fused_computation.3 | loop fusion | flops 21233664 | bytes 7409664 | tf_op jit(solution)/shard_map/jit(_where)/select_n | solution.py:26
  51.5 6.9 %all-to-all-done.2 = bf16[16,2,8,1024]{3,2,1,0:T(8,128)(2,1)S(1)} async-done(((bf16[16,2,8,1024]{3,2,1,0:T(8,128)(2,1)}), bf16[16,2,8,1024]{3,2,1,0:T(8,128)(2,1)S(1)}, u32[]{:S(2)}, u32[]{:S(2)}) %all-to-all-start.2) | async-done | bytes 524320 | tf_op jit(solution)/shard_map/all_to_all | solution.py:94
  58.4 1.3 %fusion.17 = f32[2,128,128]{2,1,0:T(8,128)S(1)} fusion(bf16[128,1024]{1,0:T(8,128)(2,1)} %param.26, bf16[16,2,8,1024]{3,2,1,0:T(8,128)(2,1)S(1)} %all-to-all-done.2), kind=kOutput, calls=%fused_computation.41 | convolution fusion | flops 67108864 | bytes 917504 | tf_op jit(solution)/shard_map/ac,jbc->jab/dot_general | solution.py:80
  59.7 0.1 copy.68
  59.8 0.2 multiply_reduce_fusion
  60.0 0.1 copy.69
  60.1 0.1 copy.70
  60.1 0.1 sqrt.19
  60.2 0.1 fusion.53
  60.4 0.1 fusion.38
  60.6 0.1 fusion.41
  60.7 0.1 fusion.43
  60.8 0.1 fusion.45
  61.0 0.1 fusion.47
  61.1 0.1 fusion.50
  61.2 1.0 %copy-done.4 = bf16[4,128,1152]{2,1,0:T(8,128)(2,1)} copy-done((bf16[4,128,1152]{2,1,0:T(8,128)(2,1)}, bf16[4,128,1152]{2,1,0:T(8,128)(2,1)S(1)}, u32[]{:S(2)}) %copy-start.4) | copy-done | bytes 1179672
  62.3 9.8 %fusion.8 = f32[4,128,1152]{2,1,0:T(8,128)S(1)} fusion(bf16[2048,1152,1]{1,0,2:T(8,128)(2,1)} %bitcast.93, bf16[4,128,1152]{2,1,0:T(8,128)(2,1)} %copy-done.4, bf16[1152,2048,1]{1,0,2:T(8,128)(2,1)} %bitcast.94, f32[2048]{0:T(1024)S(1)} %broadcast_bitcast_fusion), kind=kOutput, calls=%fused_computation.31 | convolution fusion | flops 4834983936 | bytes 12984320 | tf_op jit(solution)/shard_map/vak,kn->van/dot_general | solution.py:64
  72.1 0.2 fusion.63
  72.3 0.3 fusion.30
  72.6 0.1 copy.75
  72.8 0.8 %copy.74 = f32[1,2,128,128]{3,2,1,0:T(8,128)} copy(f32[1,2,128,128]{2,3,1,0:T(8,128)S(1)} %fusion.52) | data formatting | bytes 262144 | tf_op jit(solution)/shard_map/broadcast_in_dim | solution.py:107
  (35 shorter events, 0.4 us)
Async XLA Ops:
  0.0 11.0 %copy-start = (f32[16]{0:T(128)S(1)}, f32[16]{0:T(128)}, u32[]{:S(2)}) copy-start(f32[16]{0:T(128)} %param.31) | copy-start | bytes 196
  0.0 10.1 %copy-start.2 = (bf16[128,1024]{1,0:T(8,128)(2,1)S(1)}, bf16[128,1024]{1,0:T(8,128)(2,1)}, u32[]{:S(2)}) copy-start(bf16[128,1024]{1,0:T(8,128)(2,1)} %param.26) | copy-start | bytes 786436
  0.0 10.2 %copy-start.3 = (bf16[1,16,3,3,3,3]{1,5,4,3,2,0:T(4,128)(2,1)S(1)}, bf16[1,16,3,3,3,3]{1,5,4,3,2,0:T(4,128)(2,1)}, u32[]{:S(2)}) copy-start(bf16[1,16,3,3,3,3]{1,5,4,3,2,0:T(4,128)(2,1)} %param.32) | copy-start | bytes 7780
  1.3 21.8 %all-to-all-start.1 = ((s32[16,1,2]{2,1,0:T(1,128)}), s32[16,1,2]{2,1,0:T(1,128)S(1)}, u32[]{:S(2)}, u32[]{:S(2)}) async-start(s32[16,1,2]{2,1,0:T(1,128)} %broadcast_in_dim.477), calls=%async_computation.1 | async-start | bytes 16384 | tf_op jit(solution)/shard_map/all_to_all | solution.py:91
  15.1 14.3 %copy-start.1 = (s32[4]{0:T(128)S(1)}, s32[4]{0:T(128)}, u32[]{:S(2)}) copy-start(s32[4]{0:T(128)} %param.28) | copy-start | bytes 52
  23.2 16.0 %all-to-all-start = ((bf16[16,8,1024]{2,1,0:T(8,128)(2,1)}), bf16[16,8,1024]{2,1,0:T(8,128)(2,1)S(1)}, u32[]{:S(2)}, u32[]{:S(2)}) async-start(bf16[16,8,1024]{2,1,0:T(8,128)(2,1)} %bitcast), calls=%async_computation | async-start | bytes 524288 | tf_op jit(solution)/shard_map/all_to_all | solution.py:90
  40.6 17.8 %all-to-all-start.2 = ((bf16[16,2,8,1024]{3,2,1,0:T(8,128)(2,1)}), bf16[16,2,8,1024]{3,2,1,0:T(8,128)(2,1)S(1)}, u32[]{:S(2)}, u32[]{:S(2)}) async-start(bf16[16,2,8,1024]{3,2,1,0:T(8,128)(2,1)} %bitcast.3), calls=%async_computation.2 | async-start | bytes 1048576 | tf_op jit(solution)/shard_map/all_to_all | solution.py:94
  51.5 8.9 %copy-start.5 = (pred[128]{0:T(512)(128)(4,1)S(1)}, pred[128]{0:T(512)(128)(4,1)}, u32[]{:S(2)}) copy-start(pred[128]{0:T(512)(128)(4,1)} %constant.180) | copy-start | bytes 388
  51.5 9.0 %copy-start.6 = (pred[128]{0:T(512)(128)(4,1)S(1)}, pred[128]{0:T(512)(128)(4,1)}, u32[]{:S(2)}) copy-start(pred[128]{0:T(512)(128)(4,1)} %constant.181) | copy-start | bytes 388
  61.2 1.0 %copy-start.4 = (bf16[4,128,1152]{2,1,0:T(8,128)(2,1)}, bf16[4,128,1152]{2,1,0:T(8,128)(2,1)S(1)}, u32[]{:S(2)}) copy-start(bf16[4,128,1152]{2,1,0:T(8,128)(2,1)S(1)} %fusion.50) | copy-start | bytes 3538948

commit v3 on v2

--- a/solution.py
+++ b/solution.py
@@ -87,8 +87,13 @@
 def gather_sources(source_maps, hubs, pick, wide):
     cells, channels = source_maps.shape
     rows = cells // wide
-    chunks = lax.all_to_all(source_maps.reshape(wide, rows, channels), "wide", 0, 0)
-    picks = lax.all_to_all(jnp.broadcast_to(pick[0][None], (wide, 2)), "wide", 0, 0)
+    lanes = 128
+    tag = jnp.zeros((wide, rows, lanes), source_maps.dtype)
+    tag = tag.at[:, 0, :2].set(pick[0][None, :].astype(source_maps.dtype))
+    payload = jnp.concatenate([source_maps.reshape(wide, rows, channels), tag], axis=2)
+    arrived = lax.all_to_all(payload, "wide", 0, 0)
+    chunks = arrived[:, :, :channels]
+    picks = arrived[:, 0, channels:channels + 2].astype(jnp.int32)
     owners = hubs[picks]
     parcel = chunks[owners]
     got = lax.all_to_all(parcel, "wide", 0, 0)

time: 74 us -> 63.3 us (0.86)
  waiting for transfers between devices: 15.5 us -> 6.19 us
  other arithmetic: 20.1 us -> 24.9 us
  starting transfers between devices: 17.2 us -> 13.4 us
  matrix products: 11.1 us -> 9.86 us
  local copies, waits for them, and re-layouts: 8.59 us -> 7.43 us
    all_to_all x2 -> x1, waiting for transfers between devices: 8.65 us -> 0.01 us  [gather_sources(): arrived = lax.all_to_all(payload, 'wide', 0, 0)]
    all_to_all x2 -> x1, starting transfers between devices: 13.4 us -> 7.41 us  [gather_sources(): arrived = lax.all_to_all(payload, 'wide', 0, 0)]
    all_to_all x1, starting transfers between devices: 3.75 us -> 6.01 us  [gather_sources(): got = lax.all_to_all(parcel, 'wide', 0, 0)]
    concatenate x0 -> x1, other arithmetic: none -> 1.69 us  [gather_sources(): jnp.concatenate([source_maps.reshape(wide, rows, channels), tag], axis=2)]
    broadcast_in_dim x1 -> x0, local copies, waits for them, and re-layouts: 1.3 us -> none  [gather_sources(): jnp.broadcast_to(pick[0][None], (wide, 2))]
    dot_general x1, matrix products: 1.25 us -> 0.3 us  [scaled_corr(): jnp.einsum('ac,jbc->jab', query, sources, preferred_element_type=jnp.floa...]
    reduce_sum x1, other arithmetic: 0.13 us -> 1.08 us  [scaled_corr(): query_rms = jnp.sqrt(jnp.mean(query_f * query_f, axis=-1) + 1e-06)]
    select_n x2, other arithmetic: 14.5 us -> 15.4 us  [banded(): band = jnp.where(table[None] == e, spread_w[:, e, None, :], band)]
  transfers between devices with their start and end apart: 3 -> 2, of which waited for: 2 -> 1; matrix products, arithmetic and copies ran while one was open for 30% -> 38% of each run, Pallas kernels for 0% -> 0%
where the time goes in v3:
time: 63.3 us; the launch traced here: 62.8 us
  other arithmetic  24.9 us (39%)
  starting transfers between devices  13.4 us (21%)
  matrix products  9.86 us (16%)
  local copies, waits for them, and re-layouts  7.43 us (12%)
  waiting for transfers between devices  6.19 us (10%)
  between operations  1.02 us (2%)
    select_n x2, other arithmetic, banded(): band = jnp.where(table[None] == e, spread_w[:, e, None, :], band)  15.4 us
    dot_general x1, matrix products, consensus_stack(): jnp.einsum('vak,kn->van', hidden, k2, preferred_element_type=jnp.float32)  9.56 us
    all_to_all x1, starting transfers between devices, gather_sources(): arrived = lax.all_to_all(payload, 'wide', 0, 0)  7.41 us
    all_to_all x1, waiting for transfers between devices, gather_sources(): got = lax.all_to_all(parcel, 'wide', 0, 0)  6.19 us
    all_to_all x1, starting transfers between devices, gather_sources(): got = lax.all_to_all(parcel, 'wide', 0, 0)  6.01 us
    eq x2, other arithmetic, banded(): band = jnp.where(table[None] == e, spread_w[:, e, None, :], band)  4.6 us
    concatenate x1, other arithmetic, gather_sources(): jnp.concatenate([source_maps.reshape(wide, rows, channels), tag], axis=2)  1.69 us
    gather x1, local copies, waits for them, and re-layouts, gather_sources(): parcel = chunks[owners]  1.39 us
  transfers between devices with their start and end apart: 2, of which 1 were waited for; matrix products, arithmetic and copies ran while one was open for 38% of the time, Pallas kernels for 0%

profile of v3, /device:TPU:0, one launch (start us, length us, event | category | flops | bytes accessed | tf_op | source)
XLA Modules:
  0.0 62.8 jit_solution(12164486023879773031)
XLA Ops:
  0.0 0.7 %convert_element_type.44 = bf16[1,2]{1,0:T(2,128)(2,1)S(1)} convert(s32[1,2]{1,0:T(1,128)} %param.31) | non-fusion elementwise | flops 2 | bytes 12 | tf_op jit(solution)/shard_map/convert_element_type | solution.py:92
  0.7 1.7 %pad_maximum_fusion = bf16[16,8,1152]{2,1,0:T(8,128)(2,1)} fusion(bf16[16,8,128]{2,1,0:T(8,128)(2,1)S(1)} %scatter.8, bf16[16,8,1024]{2,1,0:T(8,128)(2,1)} %bitcast.95), kind=kLoop, calls=%fused_computation.62 | loop fusion | flops 589824 | bytes 589824 | tf_op jit(solution)/shard_map/concatenate | solution.py:93
  2.4 7.4 %all-to-all-start = ((bf16[16,8,1152]{2,1,0:T(8,128)(2,1)}), bf16[16,8,1152]{2,1,0:T(8,128)(2,1)S(1)}, u32[]{:S(2)}, u32[]{:S(2)}) async-start(bf16[16,8,1152]{2,1,0:T(8,128)(2,1)} %pad_maximum_fusion), calls=%async_computation | async-start | bytes 589824 | tf_op jit(solution)/shard_map/all_to_all | solution.py:94
  9.9 1.1 %multiply_reduce_fusion.1 = f32[128]{0:T(128)S(1)} fusion(bf16[128,1024]{1,0:T(8,128)(2,1)} %param.28), kind=kLoop, calls=%fused_computation.53 | loop fusion | flops 393088 | bytes 262656 | tf_op jit(solution)/shard_map/reduce_sum | solution.py:78
  11.0 0.8 %reshape.2198 = bf16[16,9,9]{0,2,1:T(8,128)(2,1)S(1)} reshape(bf16[1,16,3,3,3,3]{1,5,4,3,2,0:T(4,128)(2,1)} %param.34) | data formatting | bytes 5184 | tf_op jit(solution)/shard_map/reshape | solution.py:34
  11.7 0.1 copy.104
  11.9 0.4 broadcast_in_dim.535
  12.3 0.2 reshape.2199
  12.5 0.1 broadcast_bitcast_fusion
  12.6 2.9 %broadcast_compare_fusion.4 = (pred[128,2048]{1,0:T(8,128)(4,1)S(1)}, pred[128,2048]{1,0:T(8,128)(4,1)S(1)}, pred[128,2048]{1,0:T(8,128)(4,1)S(1)}, pred[128,204...) fusion(s32[128]{0:T(128)S(1)} %get-tuple-element.68, ...), kind=kLoop, calls=%fused_computation.48 | loop fusion | flops 11796480 | bytes 2380032 | tf_op jit(solution)/shard_map/eq | solution.py:26
  15.5 1.7 %broadcast_compare_fusion.13 = (pred[128,1152]{1,0:T(8,128)(4,1)S(1)}, pred[128,1152]{1,0:T(8,128)(4,1)S(1)}, pred[128,1152]{1,0:T(8,128)(4,1)S(1)}, pred[128,11...) fusion(s32[128]{0:T(128)S(1)} %get-tuple-element.68, ...), kind=kLoop, calls=%fused_computation.67 | loop fusion | flops 6635520 | bytes 1339776 | tf_op jit(solution)/shard_map/eq | solution.py:26
  17.2 7.3 %select_select_fusion = bf16[16,128,1152]{2,1,0:T(8,128)(2,1)} fusion(pred[128,1152]{1,0:T(8,128)(4,1)S(1)} %get-tuple-element.57, pred[128,1152]{1,0:T(8,128)(4,1)S(1)} %get-tuple-element.56, pred[128,1152]{1,0:T(8,128)(4,1)S(1)} %get-tuple-element.55, pred[128,1152]{1,0:T(8,128)(4,1)S(1)} %get-tuple-element.54, pred[128,1152]{1,0:T(8,128)(4,1)S(1)} %get-tuple-element.53, ...), kind=kLoop, calls=%fused_computation.2 | loop fusion | flops 21233664 | bytes 6377472 | tf_op jit(solution)/shard_map/jit(_where)/select_n | solution.py:26
  24.6 0.2 broadcast_in_dim.495
  24.8 0.2 reshape.2197
  25.7 0.7 %slice_bitcast_fusion.9 = (bf16[9,2048]{1,0:T(8,128)(2,1)S(1)}, bf16[9,2048]{1,0:T(8,128)(2,1)S(1)}, bf16[9,2048]{1,0:T(8,128)(2,1)S(1)}, bf16[9,2048]{1,0:T(8,1...) fusion(bf16[9,9,2048]{2,0,1:T(8,128)(2,1)S(1)} %reshape.2197), kind=kLoop, calls=%fused_computation.126 | loop fusion | bytes 663552 | tf_op jit(solution)/shard_map/jit(_where)/broadcast_in_dim | solution.py:26
  26.4 0.1 copy.107
  26.5 0.1 copy.94
  26.6 0.1 reshape.2211
  26.7 0.7 %gather_fusion = s32[32]{0:T(128)S(1)} fusion(s32[4]{0:T(128)S(1)} %copy-done.1, s32[1024]{0:T(1024)S(1)} %pad_clamp_fusion.1), kind=kCustom, calls=%fused_computation | custom fusion | bytes 384 | tf_op jit(solution)/shard_map/gather | solution.py:97
  27.4 0.1 gather.9
  27.5 0.1 copy.95
  27.6 0.1 copy.98
  27.7 0.1 reshape.2219
  27.8 1.4 %gather_fusion.1 = bf16[32,8,1024]{2,1,0:T(8,128)(2,1)} fusion(bf16[16,8,1024]{2,1,0:T(8,128)(2,1)S(1)} %slice.217, s32[1024]{0:T(1024)S(1)} %pad_clamp_fusion), kind=kCustom, calls=%fused_computation.1 | custom fusion | bytes 1048704 | tf_op jit(solution)/shard_map/gather | solution.py:98
  29.2 6.0 %all-to-all-start.1 = ((bf16[16,2,8,1024]{3,2,1,0:T(8,128)(2,1)}), bf16[16,2,8,1024]{3,2,1,0:T(8,128)(2,1)S(1)}, u32[]{:S(2)}, u32[]{:S(2)}) async-start(bf16[16,2,8,1024]{3,2,1,0:T(8,128)(2,1)} %bitcast.3), calls=%async_computation.1 | async-start | bytes 1048576 | tf_op jit(solution)/shard_map/all_to_all | solution.py:99
  35.2 0.0 copy-start.3
  35.2 8.1 %select_select_fusion.1 = bf16[9,128,2048]{2,1,0:T(8,128)(2,1)} fusion(pred[128,2048]{1,0:T(8,128)(4,1)S(1)} %copy-done.2, pred[128,2048]{1,0:T(8,128)(4,1)S(1)} %get-tuple-element.50, pred[128,2048]{1,0:T(8,128)(4,1)S(1)} %get-tuple-element.49, pred[128,2048]{1,0:T(8,128)(4,1)S(1)} %get-tuple-element.48, pred[128,2048]{1,0:T(8,128)(4,1)S(1)} %get-tuple-element.47, ...), kind=kLoop, calls=%fused_computation.3 | loop fusion | flops 21233664 | bytes 7409664 | tf_op jit(solution)/shard_map/jit(_where)/select_n | solution.py:26
  43.3 6.2 %all-to-all-done.1 = bf16[16,2,8,1024]{3,2,1,0:T(8,128)(2,1)S(1)} async-done(((bf16[16,2,8,1024]{3,2,1,0:T(8,128)(2,1)}), bf16[16,2,8,1024]{3,2,1,0:T(8,128)(2,1)S(1)}, u32[]{:S(2)}, u32[]{:S(2)}) %all-to-all-start.1) | async-done | bytes 524320 | tf_op jit(solution)/shard_map/all_to_all | solution.py:99
  49.5 0.3 fusion.17
  49.8 0.1 copy.100
  49.9 0.2 multiply_reduce_fusion
  50.1 0.1 copy.101
  50.2 0.1 copy.102
  50.3 0.1 sqrt.19
  50.4 0.1 fusion.53
  50.5 0.1 fusion.38
  50.7 0.1 fusion.41
  50.8 0.1 fusion.43
  51.0 0.1 fusion.45
  51.1 0.1 fusion.47
  51.3 0.1 fusion.50
  51.4 9.6 %fusion.8 = f32[4,128,1152]{2,1,0:T(8,128)S(1)} fusion(bf16[2048,1152,1]{1,0,2:T(8,128)(2,1)} %bitcast.93, bf16[4,128,1152]{2,1,0:T(8,128)(2,1)S(1)} %fusion.50, bf16[1152,2048,1]{1,0,2:T(8,128)(2,1)} %bitcast.94, f32[2048]{0:T(1024)S(1)} %broadcast_bitcast_fusion), kind=kOutput, calls=%fused_computation.31 | convolution fusion | flops 4834983936 | bytes 12984320 | tf_op jit(solution)/shard_map/vak,kn->van/dot_general | solution.py:64
  60.9 0.0 copy-start.7
  61.0 0.2 fusion.63
  61.2 0.4 copy-done.7
  61.6 0.3 fusion.30
  61.9 0.1 copy.108
  62.0 0.8 %copy.106 = f32[1,2,128,128]{3,2,1,0:T(8,128)} copy(f32[1,2,128,128]{2,3,1,0:T(8,128)S(1)} %fusion.52) | data formatting | bytes 262144 | tf_op jit(solution)/shard_map/broadcast_in_dim | solution.py:112
  (40 shorter events, 0.4 us)
Async XLA Ops:
  0.0 12.5 %copy-start = (f32[16]{0:T(128)S(1)}, f32[16]{0:T(128)}, u32[]{:S(2)}) copy-start(f32[16]{0:T(128)} %param.33) | copy-start | bytes 196
  2.4 24.0 %all-to-all-start = ((bf16[16,8,1152]{2,1,0:T(8,128)(2,1)}), bf16[16,8,1152]{2,1,0:T(8,128)(2,1)S(1)}, u32[]{:S(2)}, u32[]{:S(2)}) async-start(bf16[16,8,1152]{2,1,0:T(8,128)(2,1)} %pad_maximum_fusion), calls=%async_computation | async-start | bytes 589824 | tf_op jit(solution)/shard_map/all_to_all | solution.py:94
  17.2 7.4 %copy-start.4 = (bf16[16,1,3,3,3,3]{0,5,4,3,2,1:T(4,128)(2,1)S(1)}, bf16[16,1,3,3,3,3]{0,5,4,3,2,1:T(4,128)(2,1)}, u32[]{:S(2)}) copy-start(bf16[16,1,3,3,3,3]{0,5,4,3,2,1:T(4,128)(2,1)} %param.32) | copy-start | bytes 7780
  24.5 2.2 %copy-start.1 = (s32[4]{0:T(128)S(1)}, s32[4]{0:T(128)}, u32[]{:S(2)}) copy-start(s32[4]{0:T(128)} %param.30) | copy-start | bytes 52
  27.4 7.8 %copy-start.2 = (pred[128,2048]{1,0:T(8,128)(4,1)S(1)}, pred[128,2048]{1,0:T(8,128)(4,1)}, u32[]{:S(2)}) copy-start(pred[128,2048]{1,0:T(8,128)(4,1)} %get-tuple-element.51) | copy-start | bytes 786436
  29.2 20.3 %all-to-all-start.1 = ((bf16[16,2,8,1024]{3,2,1,0:T(8,128)(2,1)}), bf16[16,2,8,1024]{3,2,1,0:T(8,128)(2,1)S(1)}, u32[]{:S(2)}, u32[]{:S(2)}) async-start(bf16[16,2,8,1024]{3,2,1,0:T(8,128)(2,1)} %bitcast.3), calls=%async_computation.1 | async-start | bytes 1048576 | tf_op jit(solution)/shard_map/all_to_all | solution.py:99
  35.2 14.3 %copy-start.3 = (bf16[128,1024]{1,0:T(8,128)(2,1)S(1)}, bf16[128,1024]{1,0:T(8,128)(2,1)}, u32[]{:S(2)}) copy-start(bf16[128,1024]{1,0:T(8,128)(2,1)} %param.28) | copy-start | bytes 786436
  43.3 7.2 %copy-start.5 = (pred[128]{0:T(512)(128)(4,1)S(1)}, pred[128]{0:T(512)(128)(4,1)}, u32[]{:S(2)}) copy-start(pred[128]{0:T(512)(128)(4,1)} %constant.211) | copy-start | bytes 388
  43.3 7.4 %copy-start.6 = (pred[128]{0:T(512)(128)(4,1)S(1)}, pred[128]{0:T(512)(128)(4,1)}, u32[]{:S(2)}) copy-start(pred[128]{0:T(512)(128)(4,1)} %constant.212) | copy-start | bytes 388
  60.9 0.7 %copy-start.7 = (pred[128]{0:T(512)(128)(4,1)S(1)}, pred[128]{0:T(512)(128)(4,1)}, u32[]{:S(2)}) copy-start(pred[128]{0:T(512)(128)(4,1)} %constant.212) | copy-start | bytes 388

commit v4 on v3

--- a/solution.py
+++ b/solution.py
@@ -97,16 +97,19 @@
     owners = hubs[picks]
     parcel = chunks[owners]
     got = lax.all_to_all(parcel, "wide", 0, 0)
-    return jnp.swapaxes(got, 0, 1).reshape(2, cells, channels)
+    return jnp.swapaxes(got, 0, 1).reshape(2, cells, channels), parcel
 
 
 def per_device(
     query_maps, source_maps, hubs, pick, weight_first, bias_first, weight_second, bias_second,
     wide,
 ):
-    chosen = gather_sources(source_maps, hubs, pick, wide)
+    chosen, parcel = gather_sources(source_maps, hubs, pick, wide)
     correlation = scaled_corr(query_maps, chosen)
     volumes = jnp.concatenate([correlation, jnp.swapaxes(correlation, 1, 2)], axis=0)
+    weight_first, weight_second, _ = lax.optimization_barrier(
+        (weight_first, weight_second, parcel)
+    )
     k1, k2 = band_weights(weight_first, weight_second)
     filtered = consensus_stack(volumes, k1, k2, bias_first, bias_second)
     return (filtered[:2] + jnp.swapaxes(filtered[2:], 1, 2))[None]

time: 63.3 us -> 60 us (0.948)
  waiting for transfers between devices: 6.19 us -> 2.94 us
  starting transfers between devices: 13.4 us -> 11.1 us
  other arithmetic: 24.9 us -> 26 us
  local copies, waits for them, and re-layouts: 7.43 us -> 8.18 us
    all_to_all x1, waiting for transfers between devices: 6.19 us -> 0.01 us  [gather_sources(): got = lax.all_to_all(parcel, 'wide', 0, 0)]
    all_to_all x1, waiting for transfers between devices: 0.01 us -> 2.93 us  [gather_sources(): arrived = lax.all_to_all(payload, 'wide', 0, 0)]
    all_to_all x1, starting transfers between devices: 6.01 us -> 3.57 us  [gather_sources(): got = lax.all_to_all(parcel, 'wide', 0, 0)]
    unnamed x20 -> x40, local copies, waits for them, and re-layouts: 0.69 us -> 1.38 us
  transfers between devices with their start and end apart: 2 -> 2, of which waited for: 1 -> 1; matrix products, arithmetic and copies ran while one was open for 38% -> 42% of each run, Pallas kernels for 0% -> 0%
where the time goes in v4:
time: 60 us; the launch traced here: 59.5 us
  other arithmetic  26 us (43%)
  starting transfers between devices  11.1 us (18%)
  matrix products  10.1 us (17%)
  local copies, waits for them, and re-layouts  8.18 us (14%)
  waiting for transfers between devices  2.94 us (5%)
  between operations  1.18 us (2%)
    select_n x2, other arithmetic, banded(): band = jnp.where(table[None] == e, spread_w[:, e, None, :], band)  15.4 us
    dot_general x1, matrix products, consensus_stack(): jnp.einsum('vak,kn->van', hidden, k2, preferred_element_type=jnp.float32)  9.81 us
    all_to_all x1, starting transfers between devices, gather_sources(): arrived = lax.all_to_all(payload, 'wide', 0, 0)  7.55 us
    eq x2, other arithmetic, banded(): band = jnp.where(table[None] == e, spread_w[:, e, None, :], band)  5.19 us
    all_to_all x1, starting transfers between devices, gather_sources(): got = lax.all_to_all(parcel, 'wide', 0, 0)  3.57 us
    all_to_all x1, waiting for transfers between devices, gather_sources(): arrived = lax.all_to_all(payload, 'wide', 0, 0)  2.93 us
    concatenate x1, other arithmetic, gather_sources(): jnp.concatenate([source_maps.reshape(wide, rows, channels), tag], axis=2)  1.68 us
    gather x1, local copies, waits for them, and re-layouts, gather_sources(): parcel = chunks[owners]  1.38 us
  transfers between devices with their start and end apart: 2, of which 1 were waited for; matrix products, arithmetic and copies ran while one was open for 42% of the time, Pallas kernels for 0%

profile of v4, /device:TPU:0, one launch (start us, length us, event | category | flops | bytes accessed | tf_op | source)
XLA Modules:
  0.0 59.5 jit_solution(16473998827614956202)
XLA Ops:
  0.0 0.7 %convert_element_type.44 = bf16[1,2]{1,0:T(2,128)(2,1)S(1)} convert(s32[1,2]{1,0:T(1,128)} %param.31) | non-fusion elementwise | flops 2 | bytes 12 | tf_op jit(solution)/shard_map/convert_element_type | solution.py:92
  0.7 1.7 %pad_maximum_fusion = bf16[16,8,1152]{2,1,0:T(8,128)(2,1)} fusion(bf16[16,8,128]{2,1,0:T(8,128)(2,1)S(1)} %scatter.8, bf16[16,8,1024]{2,1,0:T(8,128)(2,1)} %bitcast.95), kind=kLoop, calls=%fused_computation.62 | loop fusion | flops 589824 | bytes 589824 | tf_op jit(solution)/shard_map/concatenate | solution.py:93
  2.4 7.5 %all-to-all-start = ((bf16[16,8,1152]{2,1,0:T(8,128)(2,1)}), bf16[16,8,1152]{2,1,0:T(8,128)(2,1)S(1)}, u32[]{:S(2)}, u32[]{:S(2)}) async-start(bf16[16,8,1152]{2,1,0:T(8,128)(2,1)} %pad_maximum_fusion), calls=%async_computation | async-start | bytes 589824 | tf_op jit(solution)/shard_map/all_to_all | solution.py:94
  10.0 1.1 %multiply_reduce_fusion.1 = f32[128]{0:T(128)S(1)} fusion(bf16[128,1024]{1,0:T(8,128)(2,1)} %param.28), kind=kLoop, calls=%fused_computation.53 | loop fusion | flops 393088 | bytes 262656 | tf_op jit(solution)/shard_map/reduce_sum | solution.py:78
  11.1 0.5 sqrt_multiply_fusion
  11.6 0.1 broadcast_bitcast_fusion
  12.3 3.0 %broadcast_compare_fusion.4 = (pred[128,2048]{1,0:T(8,128)(4,1)S(1)}, pred[128,2048]{1,0:T(8,128)(4,1)S(1)}, pred[128,2048]{1,0:T(8,128)(4,1)S(1)}, pred[128,204...) fusion(s32[128]{0:T(128)S(1)} %get-tuple-element.72, ...), kind=kLoop, calls=%fused_computation.48 | loop fusion | flops 11796480 | bytes 2380032 | tf_op jit(solution)/shard_map/eq | solution.py:26
  15.4 2.2 %broadcast_compare_fusion.13 = (pred[128,1152]{1,0:T(8,128)(4,1)}, pred[128,1152]{1,0:T(8,128)(4,1)}, pred[128,1152]{1,0:T(8,128)(4,1)}, pred[128,1152]{1,0:T(8,...) fusion(s32[128]{0:T(128)S(1)} %get-tuple-element.72, ...), kind=kLoop, calls=%fused_computation.67 | loop fusion | flops 6635520 | bytes 1339776 | tf_op jit(solution)/shard_map/eq | solution.py:26
  17.5 2.9 %all-to-all-done = bf16[16,8,1152]{2,1,0:T(8,128)(2,1)S(1)} async-done(((bf16[16,8,1152]{2,1,0:T(8,128)(2,1)}), bf16[16,8,1152]{2,1,0:T(8,128)(2,1)S(1)}, u32[]{:S(2)}, u32[]{:S(2)}) %all-to-all-start) | async-done | bytes 294944 | tf_op jit(solution)/shard_map/all_to_all | solution.py:94
  20.5 0.1 copy.107
  20.6 0.1 copy.94
  20.7 0.1 reshape.2211
  20.8 0.7 %gather_fusion = s32[32]{0:T(128)S(1)} fusion(s32[4]{0:T(128)S(1)} %copy-done.1, s32[1024]{0:T(1024)S(1)} %pad_clamp_fusion.1), kind=kCustom, calls=%fused_computation | custom fusion | bytes 384 | tf_op jit(solution)/shard_map/gather | solution.py:97
  21.5 0.1 gather.9
  21.6 0.1 copy.95
  21.7 0.1 copy.98
  21.8 0.1 reshape.2219
  21.9 1.4 %gather_fusion.1 = bf16[32,8,1024]{2,1,0:T(8,128)(2,1)} fusion(bf16[16,8,1024]{2,1,0:T(8,128)(2,1)S(1)} %slice.217, s32[1024]{0:T(1024)S(1)} %pad_clamp_fusion), kind=kCustom, calls=%fused_computation.1 | custom fusion | bytes 1048704 | tf_op jit(solution)/shard_map/gather | solution.py:98
  23.3 3.6 %all-to-all-start.1 = ((bf16[16,2,8,1024]{3,2,1,0:T(8,128)(2,1)}), bf16[16,2,8,1024]{3,2,1,0:T(8,128)(2,1)S(1)}, u32[]{:S(2)}, u32[]{:S(2)}) async-start(bf16[16,2,8,1024]{3,2,1,0:T(8,128)(2,1)} %bitcast.3), calls=%async_computation.1 | async-start | bytes 1048576 | tf_op jit(solution)/shard_map/all_to_all | solution.py:99
  26.9 0.2 broadcast_in_dim.495
  27.2 0.2 reshape.2197
  27.3 0.8 %slice_bitcast_fusion.9 = (bf16[9,2048]{1,0:T(8,128)(2,1)}, bf16[9,2048]{1,0:T(8,128)(2,1)}, bf16[9,2048]{1,0:T(8,128)(2,1)}, bf16[9,2048]{1,0:T(8,128)(2,1)}, b...) fusion(bf16[9,9,2048]{2,0,1:T(8,128)(2,1)S(1)} %reshape.2197), kind=kLoop, calls=%fused_computation.126 | loop fusion | bytes 663552 | tf_op jit(solution)/shard_map/jit(_where)/broadcast_in_dim | solution.py:26
  28.1 0.8 %reshape.2198 = bf16[16,9,9]{0,2,1:T(8,128)(2,1)S(1)} reshape(bf16[1,16,3,3,3,3]{1,5,4,3,2,0:T(4,128)(2,1)} %param.34) | data formatting | bytes 5184 | tf_op jit(solution)/shard_map/reshape | solution.py:34
  28.9 0.1 copy.104
  29.1 0.4 broadcast_in_dim.535
  29.4 0.2 reshape.2199
  29.7 0.0 copy-start.3
  29.8 8.3 %select_select_fusion = bf16[16,128,1152]{2,1,0:T(8,128)(2,1)} fusion(pred[128,1152]{1,0:T(8,128)(4,1)} %get-tuple-element.61, pred[128,1152]{1,0:T(8,128)(4,1)} %get-tuple-element.60, pred[128,1152]{1,0:T(8,128)(4,1)} %get-tuple-element.59, pred[128,1152]{1,0:T(8,128)(4,1)} %get-tuple-element.58, pred[128,1152]{1,0:T(8,128)(4,1)} %get-tuple-element.57, ...), kind=kLoop, calls=%fused_computation.2 | loop fusion | flops 21233664 | bytes 6377472 | tf_op jit(solution)/shard_map/jit(_where)/select_n | solution.py:26
  38.2 7.2 %select_select_fusion.1 = bf16[9,128,2048]{2,1,0:T(8,128)(2,1)} fusion(pred[128,2048]{1,0:T(8,128)(4,1)S(1)} %copy-done.2, pred[128,2048]{1,0:T(8,128)(4,1)S(1)} %get-tuple-element.54, pred[128,2048]{1,0:T(8,128)(4,1)S(1)} %get-tuple-element.53, pred[128,2048]{1,0:T(8,128)(4,1)S(1)} %get-tuple-element.52, pred[128,2048]{1,0:T(8,128)(4,1)S(1)} %get-tuple-element.51, ...), kind=kLoop, calls=%fused_computation.3 | loop fusion | flops 21233664 | bytes 7409664 | tf_op jit(solution)/shard_map/jit(_where)/select_n | solution.py:26
  45.3 0.3 fusion.17
  45.6 0.1 copy.100
  45.8 0.2 multiply_reduce_fusion
  46.0 0.1 copy.101
  46.0 0.1 copy.102
  46.1 0.1 sqrt.19
  46.2 0.1 fusion.53
  46.4 0.1 fusion.38
  46.5 0.1 fusion.41
  46.7 0.1 fusion.43
  46.8 0.1 fusion.45
  47.0 0.1 fusion.47
  47.1 0.1 fusion.50
  47.2 1.0 %copy-done.14 = bf16[4,128,1152]{2,1,0:T(8,128)(2,1)} copy-done((bf16[4,128,1152]{2,1,0:T(8,128)(2,1)}, bf16[4,128,1152]{2,1,0:T(8,128)(2,1)S(1)}, u32[]{:S(2)}) %copy-start.14) | copy-done | bytes 1179672
  48.3 9.8 %fusion.8 = f32[4,128,1152]{2,1,0:T(8,128)S(1)} fusion(bf16[2048,1152,1]{1,0,2:T(8,128)(2,1)} %bitcast.93, bf16[4,128,1152]{2,1,0:T(8,128)(2,1)} %copy-done.14, bf16[1152,2048,1]{1,0,2:T(8,128)(2,1)} %bitcast.94, f32[2048]{0:T(1024)S(1)} %broadcast_bitcast_fusion), kind=kOutput, calls=%fused_computation.31 | convolution fusion | flops 4834983936 | bytes 12984320 | tf_op jit(solution)/shard_map/vak,kn->van/dot_general | solution.py:64
  58.1 0.2 fusion.63
  58.3 0.3 fusion.30
  58.6 0.1 copy.108
  58.8 0.8 %copy.106 = f32[1,2,128,128]{3,2,1,0:T(8,128)} copy(f32[1,2,128,128]{2,3,1,0:T(8,128)S(1)} %fusion.52) | data formatting | bytes 262144 | tf_op jit(solution)/shard_map/broadcast_in_dim | solution.py:115
  (60 shorter events, 0.4 us)
Async XLA Ops:
  0.0 11.6 %copy-start = (f32[16]{0:T(128)S(1)}, f32[16]{0:T(128)}, u32[]{:S(2)}) copy-start(f32[16]{0:T(128)} %param.33) | copy-start | bytes 196
  2.4 18.4 %copy-start.1 = (s32[4]{0:T(128)S(1)}, s32[4]{0:T(128)}, u32[]{:S(2)}) copy-start(s32[4]{0:T(128)} %param.30) | copy-start | bytes 52
  2.4 18.1 %all-to-all-start = ((bf16[16,8,1152]{2,1,0:T(8,128)(2,1)}), bf16[16,8,1152]{2,1,0:T(8,128)(2,1)S(1)}, u32[]{:S(2)}, u32[]{:S(2)}) async-start(bf16[16,8,1152]{2,1,0:T(8,128)(2,1)} %pad_maximum_fusion), calls=%async_computation | async-start | bytes 589824 | tf_op jit(solution)/shard_map/all_to_all | solution.py:94
  21.5 5.4 %copy-start.13 = (bf16[16,1,3,3,3,3]{0,5,4,3,2,1:T(4,128)(2,1)S(1)}, bf16[16,1,3,3,3,3]{0,5,4,3,2,1:T(4,128)(2,1)}, u32[]{:S(2)}) copy-start(bf16[16,1,3,3,3,3]{0,5,4,3,2,1:T(4,128)(2,1)} %param.32) | copy-start | bytes 7780
  23.3 22.1 %all-to-all-start.1 = ((bf16[16,2,8,1024]{3,2,1,0:T(8,128)(2,1)}), bf16[16,2,8,1024]{3,2,1,0:T(8,128)(2,1)S(1)}, u32[]{:S(2)}, u32[]{:S(2)}) async-start(bf16[16,2,8,1024]{3,2,1,0:T(8,128)(2,1)} %bitcast.3), calls=%async_computation.1 | async-start | bytes 1048576 | tf_op jit(solution)/shard_map/all_to_all | solution.py:99
  29.7 8.4 %copy-start.2 = (pred[128,2048]{1,0:T(8,128)(4,1)S(1)}, pred[128,2048]{1,0:T(8,128)(4,1)}, u32[]{:S(2)}) copy-start(pred[128,2048]{1,0:T(8,128)(4,1)} %get-tuple-element.55) | copy-start | bytes 786436
  29.7 8.4 %copy-start.3 = (bf16[9,2048]{1,0:T(8,128)(2,1)S(1)}, bf16[9,2048]{1,0:T(8,128)(2,1)}, u32[]{:S(2)}) copy-start(bf16[9,2048]{1,0:T(8,128)(2,1)} %get-tuple-element.29) | copy-start | bytes 110596
  29.7 8.4 %copy-start.4 = (bf16[9,2048]{1,0:T(8,128)(2,1)S(1)}, bf16[9,2048]{1,0:T(8,128)(2,1)}, u32[]{:S(2)}) copy-start(bf16[9,2048]{1,0:T(8,128)(2,1)} %get-tuple-element.30) | copy-start | bytes 110596
  29.7 8.4 %copy-start.5 = (bf16[9,2048]{1,0:T(8,128)(2,1)S(1)}, bf16[9,2048]{1,0:T(8,128)(2,1)}, u32[]{:S(2)}) copy-start(bf16[9,2048]{1,0:T(8,128)(2,1)} %get-tuple-element.31) | copy-start | bytes 110596
  29.7 8.4 %copy-start.6 = (bf16[9,2048]{1,0:T(8,128)(2,1)S(1)}, bf16[9,2048]{1,0:T(8,128)(2,1)}, u32[]{:S(2)}) copy-start(bf16[9,2048]{1,0:T(8,128)(2,1)} %get-tuple-element.32) | copy-start | bytes 110596
  29.7 8.4 %copy-start.7 = (bf16[9,2048]{1,0:T(8,128)(2,1)S(1)}, bf16[9,2048]{1,0:T(8,128)(2,1)}, u32[]{:S(2)}) copy-start(bf16[9,2048]{1,0:T(8,128)(2,1)} %get-tuple-element.33) | copy-start | bytes 110596
  29.7 8.4 %copy-start.8 = (bf16[9,2048]{1,0:T(8,128)(2,1)S(1)}, bf16[9,2048]{1,0:T(8,128)(2,1)}, u32[]{:S(2)}) copy-start(bf16[9,2048]{1,0:T(8,128)(2,1)} %get-tuple-element.34) | copy-start | bytes 110596
  29.7 8.4 %copy-start.9 = (bf16[9,2048]{1,0:T(8,128)(2,1)S(1)}, bf16[9,2048]{1,0:T(8,128)(2,1)}, u32[]{:S(2)}) copy-start(bf16[9,2048]{1,0:T(8,128)(2,1)} %get-tuple-element.35) | copy-start | bytes 110596
  29.7 8.4 %copy-start.10 = (bf16[9,2048]{1,0:T(8,128)(2,1)S(1)}, bf16[9,2048]{1,0:T(8,128)(2,1)}, u32[]{:S(2)}) copy-start(bf16[9,2048]{1,0:T(8,128)(2,1)} %get-tuple-element.36) | copy-start | bytes 110596
  29.8 8.4 %copy-start.11 = (bf16[9,2048]{1,0:T(8,128)(2,1)S(1)}, bf16[9,2048]{1,0:T(8,128)(2,1)}, u32[]{:S(2)}) copy-start(bf16[9,2048]{1,0:T(8,128)(2,1)} %get-tuple-element.37) | copy-start | bytes 110596
  38.1 7.2 %copy-start.12 = (bf16[128,1024]{1,0:T(8,128)(2,1)S(1)}, bf16[128,1024]{1,0:T(8,128)(2,1)}, u32[]{:S(2)}) copy-start(bf16[128,1024]{1,0:T(8,128)(2,1)} %param.28) | copy-start | bytes 786436
  38.2 8.1 %copy-start.17 = (f32[128]{0:T(128)S(1)}, f32[128]{0:T(128)}, u32[]{:S(2)}) copy-start(f32[128]{0:T(128)} %sqrt_multiply_fusion) | copy-start | bytes 1540
  45.3 1.1 %copy-start.15 = (pred[128]{0:T(512)(128)(4,1)S(1)}, pred[128]{0:T(512)(128)(4,1)}, u32[]{:S(2)}) copy-start(pred[128]{0:T(512)(128)(4,1)} %constant.211) | copy-start | bytes 388
  45.3 1.2 %copy-start.16 = (pred[128]{0:T(512)(128)(4,1)S(1)}, pred[128]{0:T(512)(128)(4,1)}, u32[]{:S(2)}) copy-start(pred[128]{0:T(512)(128)(4,1)} %constant.212) | copy-start | bytes 388
  47.2 1.1 %copy-start.14 = (bf16[4,128,1152]{2,1,0:T(8,128)(2,1)}, bf16[4,128,1152]{2,1,0:T(8,128)(2,1)S(1)}, u32[]{:S(2)}) copy-start(bf16[4,128,1152]{2,1,0:T(8,128)(2,1)S(1)} %fusion.50) | copy-start | bytes 3538948

commit v5 on v4

--- a/solution.py
+++ b/solution.py
@@ -27,14 +27,17 @@
     return band
 
 
-def band_weights(weight_first, weight_second):
+def band_weights(weight_first, weight_second, tie):
     hid = weight_first.shape[0]
     cells = HQ * WQ
     w1 = weight_first.reshape(hid, TAPS, TAPS)
-    w2 = weight_second.reshape(hid, TAPS, TAPS)
     k1 = banded(jnp.transpose(w1, (1, 2, 0)), tap_table(cells, hid * cells), cells)
     k1 = k1.reshape(TAPS * cells, hid * cells)
-    k2 = banded(jnp.transpose(w2, (0, 2, 1)), tap_table(cells, TAPS * cells), cells)
+    table, weight_second, _ = lax.optimization_barrier(
+        (tap_table(cells, TAPS * cells), weight_second, tie)
+    )
+    w2 = weight_second.reshape(hid, TAPS, TAPS)
+    k2 = banded(jnp.transpose(w2, (0, 2, 1)), table, cells)
     k2 = k2.reshape(hid * cells, TAPS * cells)
     return k1, k2
 
@@ -107,10 +110,7 @@
     chosen, parcel = gather_sources(source_maps, hubs, pick, wide)
     correlation = scaled_corr(query_maps, chosen)
     volumes = jnp.concatenate([correlation, jnp.swapaxes(correlation, 1, 2)], axis=0)
-    weight_first, weight_second, _ = lax.optimization_barrier(
-        (weight_first, weight_second, parcel)
-    )
-    k1, k2 = band_weights(weight_first, weight_second)
+    k1, k2 = band_weights(weight_first, weight_second, parcel)
     filtered = consensus_stack(volumes, k1, k2, bias_first, bias_second)
     return (filtered[:2] + jnp.swapaxes(filtered[2:], 1, 2))[None]
 

time: 60 us -> 58.7 us (0.978)
  other arithmetic: 26 us -> 21.8 us
  waiting for transfers between devices: 2.94 us -> 5.39 us
  starting transfers between devices: 11.1 us -> 13.4 us
  local copies, waits for them, and re-layouts: 8.18 us -> 6.76 us
    all_to_all x1, waiting for transfers between devices: 0.01 us -> 5.39 us  [gather_sources(): got = lax.all_to_all(parcel, 'wide', 0, 0)]
    all_to_all x1, waiting for transfers between devices: 2.93 us -> 0.01 us  [gather_sources(): arrived = lax.all_to_all(payload, 'wide', 0, 0)]
    all_to_all x1, starting transfers between devices: 3.57 us -> 6.01 us  [gather_sources(): got = lax.all_to_all(parcel, 'wide', 0, 0)]
    eq x2, other arithmetic: 5.19 us -> 2.97 us  [banded(): band = jnp.where(table[None] == e, spread_w[:, e, None, :], band)]
    select_n x2, other arithmetic: 15.4 us -> 14.4 us  [banded(): band = jnp.where(table[None] == e, spread_w[:, e, None, :], band)]
    reduce_sum x1, other arithmetic: 1.08 us -> 0.13 us  [scaled_corr(): query_rms = jnp.sqrt(jnp.mean(query_f * query_f, axis=-1) + 1e-06)]
    broadcast_in_dim x2, local copies, waits for them, and re-layouts: 0.83 us -> 0.07 us  [banded(): band = jnp.where(table[None] == e, spread_w[:, e, None, :], band)]
    reshape x1, local copies, waits for them, and re-layouts: 0.03 us -> 0.77 us  [band_weights(): w1 = weight_first.reshape(hid, TAPS, TAPS)]
  transfers between devices with their start and end apart: 2 -> 2, of which waited for: 1 -> 1; matrix products, arithmetic and copies ran while one was open for 42% -> 34% of each run, Pallas kernels for 0% -> 0%
where the time goes in v5:
time: 58.7 us; the launch traced here: 58.2 us
  other arithmetic  21.8 us (37%)
  starting transfers between devices  13.4 us (23%)
  matrix products  9.87 us (17%)
  local copies, waits for them, and re-layouts  6.76 us (12%)
  waiting for transfers between devices  5.39 us (9%)
  between operations  1.05 us (2%)
    select_n x2, other arithmetic, banded(): band = jnp.where(table[None] == e, spread_w[:, e, None, :], band)  14.4 us
    dot_general x1, matrix products, consensus_stack(): jnp.einsum('vak,kn->van', hidden, k2, preferred_element_type=jnp.float32)  9.56 us
    all_to_all x1, starting transfers between devices, gather_sources(): arrived = lax.all_to_all(payload, 'wide', 0, 0)  7.41 us
    all_to_all x1, starting transfers between devices, gather_sources(): got = lax.all_to_all(parcel, 'wide', 0, 0)  6.01 us
    all_to_all x1, waiting for transfers between devices, gather_sources(): got = lax.all_to_all(parcel, 'wide', 0, 0)  5.39 us
    eq x2, other arithmetic, banded(): band = jnp.where(table[None] == e, spread_w[:, e, None, :], band)  2.97 us
    concatenate x1, other arithmetic, gather_sources(): jnp.concatenate([source_maps.reshape(wide, rows, channels), tag], axis=2)  1.69 us
    gather x1, local copies, waits for them, and re-layouts, gather_sources(): parcel = chunks[owners]  1.39 us
  transfers between devices with their start and end apart: 2, of which 1 were waited for; matrix products, arithmetic and copies ran while one was open for 34% of the time, Pallas kernels for 0%

profile of v5, /device:TPU:0, one launch (start us, length us, event | category | flops | bytes accessed | tf_op | source)
XLA Modules:
  0.0 58.2 jit_solution(7168357771029874023)
XLA Ops:
  0.0 0.7 %convert_element_type.44 = bf16[1,2]{1,0:T(2,128)(2,1)S(1)} convert(s32[1,2]{1,0:T(1,128)} %param.31) | non-fusion elementwise | flops 2 | bytes 12 | tf_op jit(solution)/shard_map/convert_element_type | solution.py:95
  0.7 1.7 %pad_maximum_fusion = bf16[16,8,1152]{2,1,0:T(8,128)(2,1)} fusion(bf16[16,8,128]{2,1,0:T(8,128)(2,1)S(1)} %scatter.8, bf16[16,8,1024]{2,1,0:T(8,128)(2,1)} %bitcast.95), kind=kLoop, calls=%fused_computation.62 | loop fusion | flops 589824 | bytes 589824 | tf_op jit(solution)/shard_map/concatenate | solution.py:96
  2.4 7.4 %all-to-all-start = ((bf16[16,8,1152]{2,1,0:T(8,128)(2,1)}), bf16[16,8,1152]{2,1,0:T(8,128)(2,1)S(1)}, u32[]{:S(2)}, u32[]{:S(2)}) async-start(bf16[16,8,1152]{2,1,0:T(8,128)(2,1)} %pad_maximum_fusion), calls=%async_computation | async-start | bytes 589824 | tf_op jit(solution)/shard_map/all_to_all | solution.py:97
  9.9 0.8 %reshape.1199 = bf16[16,9,9]{0,2,1:T(8,128)(2,1)S(1)} reshape(bf16[16,1,3,3,3,3]{0,5,4,3,2,1:T(4,128)(2,1)} %param.32) | data formatting | bytes 5184 | tf_op jit(solution)/shard_map/reshape | solution.py:33
  10.7 0.2 broadcast_in_dim.495
  10.9 0.2 reshape.1200
  11.2 0.1 multiply_reduce_fusion.1
  11.3 0.1 broadcast_bitcast_fusion
  12.1 2.2 %broadcast_compare_fusion.4 = (pred[128,2048]{1,0:T(8,128)(4,1)S(1)}, pred[128,2048]{1,0:T(8,128)(4,1)S(1)}, pred[128,2048]{1,0:T(8,128)(4,1)S(1)}, pred[128,204...) fusion(s32[128]{0:T(128)S(1)} %get-tuple-element.72, ...), kind=kLoop, calls=%fused_computation.48 | loop fusion | flops 11796480 | bytes 2380032 | tf_op jit(solution)/shard_map/eq | solution.py:26
  14.2 0.0 copy-start.1
  14.3 7.2 %select_select_fusion.1 = bf16[9,128,2048]{2,1,0:T(8,128)(2,1)} fusion(pred[128,2048]{1,0:T(8,128)(4,1)S(1)} %get-tuple-element.61, pred[128,2048]{1,0:T(8,128)(4,1)S(1)} %get-tuple-element.60, pred[128,2048]{1,0:T(8,128)(4,1)S(1)} %get-tuple-element.59, pred[128,2048]{1,0:T(8,128)(4,1)S(1)} %get-tuple-element.58, ...), kind=kLoop, calls=%fused_computation.3 | loop fusion | flops 21233664 | bytes 7409664 | tf_op jit(solution)/shard_map/jit(_where)/select_n | solution.py:26
  21.4 0.4 add_select_fusion.5
  21.9 0.1 copy.107
  22.0 0.1 copy.94
  22.1 0.1 reshape.1214
  22.2 0.7 %gather_fusion = s32[32]{0:T(128)S(1)} fusion(s32[4]{0:T(128)S(1)} %copy-done.1, s32[1024]{0:T(1024)S(1)} %pad_clamp_fusion.1), kind=kCustom, calls=%fused_computation | custom fusion | bytes 384 | tf_op jit(solution)/shard_map/gather | solution.py:100
  22.9 0.1 gather.9
  23.0 0.1 copy.95
  23.0 0.1 copy.98
  23.1 0.1 reshape.1222
  23.3 1.4 %gather_fusion.1 = bf16[32,8,1024]{2,1,0:T(8,128)(2,1)} fusion(bf16[16,8,1024]{2,1,0:T(8,128)(2,1)S(1)} %slice.217, s32[1024]{0:T(1024)S(1)} %pad_clamp_fusion), kind=kCustom, calls=%fused_computation.1 | custom fusion | bytes 1048704 | tf_op jit(solution)/shard_map/gather | solution.py:101
  24.7 6.0 %all-to-all-start.1 = ((bf16[16,2,8,1024]{3,2,1,0:T(8,128)(2,1)}), bf16[16,2,8,1024]{3,2,1,0:T(8,128)(2,1)S(1)}, u32[]{:S(2)}, u32[]{:S(2)}) async-start(bf16[16,2,8,1024]{3,2,1,0:T(8,128)(2,1)} %bitcast.3), calls=%async_computation.1 | async-start | bytes 1048576 | tf_op jit(solution)/shard_map/all_to_all | solution.py:102
  30.7 0.8 %broadcast_compare_fusion.13 = (pred[128,1152]{1,0:T(8,128)(4,1)S(1)}, pred[128,1152]{1,0:T(8,128)(4,1)S(1)}, pred[128,1152]{1,0:T(8,128)(4,1)S(1)}, pred[128,11...) fusion(s32[128,1152]{1,0:T(8,128)S(1)} %add_select_fusion.5), kind=kLoop, calls=%fused_computation.67 | loop fusion | flops 1327104 | bytes 1916928 | tf_op jit(solution)/shard_map/eq | solution.py:26
  31.5 0.1 copy.104
  31.7 0.4 broadcast_in_dim.535
  32.1 0.2 reshape.1202
  32.3 7.3 %select_select_fusion = bf16[16,128,1152]{2,1,0:T(8,128)(2,1)} fusion(pred[128,1152]{1,0:T(8,128)(4,1)S(1)} %get-tuple-element.39, pred[128,1152]{1,0:T(8,128)(4,1)S(1)} %get-tuple-element.40, pred[128,1152]{1,0:T(8,128)(4,1)S(1)} %get-tuple-element.41, pred[128,1152]{1,0:T(8,128)(4,1)S(1)} %get-tuple-element.42, pred[128,1152]{1,0:T(8,128)(4,1)S(1)} %get-tuple-element.43, ...), kind=kLoop, calls=%fused_computation.2 | loop fusion | flops 21233664 | bytes 6377472 | tf_op jit(solution)/shard_map/jit(_where)/select_n | solution.py:26
  39.6 5.4 %all-to-all-done.1 = bf16[16,2,8,1024]{3,2,1,0:T(8,128)(2,1)S(1)} async-done(((bf16[16,2,8,1024]{3,2,1,0:T(8,128)(2,1)}), bf16[16,2,8,1024]{3,2,1,0:T(8,128)(2,1)S(1)}, u32[]{:S(2)}, u32[]{:S(2)}) %all-to-all-start.1) | async-done | bytes 524320 | tf_op jit(solution)/shard_map/all_to_all | solution.py:102
  45.0 0.3 fusion.17
  45.3 0.1 copy.100
  45.4 0.2 multiply_reduce_fusion
  45.6 0.1 copy.101
  45.7 0.1 copy.102
  45.7 0.1 sqrt.19
  45.8 0.1 fusion.53
  46.0 0.1 fusion.38
  46.2 0.1 fusion.41
  46.3 0.1 fusion.43
  46.4 0.1 fusion.45
  46.6 0.1 fusion.47
  46.7 0.1 fusion.50
  46.8 9.6 %fusion.8 = f32[4,128,1152]{2,1,0:T(8,128)S(1)} fusion(bf16[2048,1152,1]{1,0,2:T(8,128)(2,1)} %bitcast.93, bf16[4,128,1152]{2,1,0:T(8,128)(2,1)S(1)} %fusion.50, bf16[1152,2048,1]{1,0,2:T(8,128)(2,1)} %bitcast.94, f32[2048]{0:T(1024)S(1)} %broadcast_bitcast_fusion), kind=kOutput, calls=%fused_computation.31 | convolution fusion | flops 4834983936 | bytes 12984320 | tf_op jit(solution)/shard_map/vak,kn->van/dot_general | solution.py:67
  56.4 0.0 copy-start.6
  56.4 0.2 fusion.63
  56.7 0.4 copy-done.6
  57.1 0.3 fusion.30
  57.4 0.1 copy.108
  57.5 0.8 %copy.106 = f32[1,2,128,128]{3,2,1,0:T(8,128)} copy(f32[1,2,128,128]{2,3,1,0:T(8,128)S(1)} %fusion.52) | data formatting | bytes 262144 | tf_op jit(solution)/shard_map/broadcast_in_dim | solution.py:115
  (39 shorter events, 0.4 us)
Async XLA Ops:
  0.0 11.3 %copy-start = (f32[16]{0:T(128)S(1)}, f32[16]{0:T(128)}, u32[]{:S(2)}) copy-start(f32[16]{0:T(128)} %param.33) | copy-start | bytes 196
  0.0 11.2 %copy-start.2 = (bf16[128,1024]{1,0:T(8,128)(2,1)S(1)}, bf16[128,1024]{1,0:T(8,128)(2,1)}, u32[]{:S(2)}) copy-start(bf16[128,1024]{1,0:T(8,128)(2,1)} %param.28) | copy-start | bytes 786436
  2.4 19.4 %all-to-all-start = ((bf16[16,8,1152]{2,1,0:T(8,128)(2,1)}), bf16[16,8,1152]{2,1,0:T(8,128)(2,1)S(1)}, u32[]{:S(2)}, u32[]{:S(2)}) async-start(bf16[16,8,1152]{2,1,0:T(8,128)(2,1)} %pad_maximum_fusion), calls=%async_computation | async-start | bytes 589824 | tf_op jit(solution)/shard_map/all_to_all | solution.py:97
  14.2 7.9 %copy-start.1 = (s32[4]{0:T(128)S(1)}, s32[4]{0:T(128)}, u32[]{:S(2)}) copy-start(s32[4]{0:T(128)} %param.30) | copy-start | bytes 52
  22.9 8.6 %copy-start.3 = (bf16[1,16,3,3,3,3]{1,5,4,3,2,0:T(4,128)(2,1)S(1)}, bf16[1,16,3,3,3,3]{1,5,4,3,2,0:T(4,128)(2,1)}, u32[]{:S(2)}) copy-start(bf16[1,16,3,3,3,3]{1,5,4,3,2,0:T(4,128)(2,1)} %param.34) | copy-start | bytes 7780
  24.7 20.3 %all-to-all-start.1 = ((bf16[16,2,8,1024]{3,2,1,0:T(8,128)(2,1)}), bf16[16,2,8,1024]{3,2,1,0:T(8,128)(2,1)S(1)}, u32[]{:S(2)}, u32[]{:S(2)}) async-start(bf16[16,2,8,1024]{3,2,1,0:T(8,128)(2,1)} %bitcast.3), calls=%async_computation.1 | async-start | bytes 1048576 | tf_op jit(solution)/shard_map/all_to_all | solution.py:102
  39.6 6.5 %copy-start.4 = (pred[128]{0:T(512)(128)(4,1)S(1)}, pred[128]{0:T(512)(128)(4,1)}, u32[]{:S(2)}) copy-start(pred[128]{0:T(512)(128)(4,1)} %constant.211) | copy-start | bytes 388
  39.6 6.6 %copy-start.5 = (pred[128]{0:T(512)(128)(4,1)S(1)}, pred[128]{0:T(512)(128)(4,1)}, u32[]{:S(2)}) copy-start(pred[128]{0:T(512)(128)(4,1)} %constant.212) | copy-start | bytes 388
  56.4 0.7 %copy-start.6 = (pred[128]{0:T(512)(128)(4,1)S(1)}, pred[128]{0:T(512)(128)(4,1)}, u32[]{:S(2)}) copy-start(pred[128]{0:T(512)(128)(4,1)} %constant.212) | copy-start | bytes 388

commit v6 on v5

--- a/solution.py
+++ b/solution.py
@@ -87,27 +87,31 @@
     )
 
 
-def gather_sources(source_maps, hubs, pick, wide):
+def gather_sources(source_maps, hubs, pick, sub):
     cells, channels = source_maps.shape
-    rows = cells // wide
+    rows = cells // sub
     lanes = 128
-    tag = jnp.zeros((wide, rows, lanes), source_maps.dtype)
+    tag = jnp.zeros((sub, rows, lanes), source_maps.dtype)
     tag = tag.at[:, 0, :2].set(pick[0][None, :].astype(source_maps.dtype))
-    payload = jnp.concatenate([source_maps.reshape(wide, rows, channels), tag], axis=2)
-    arrived = lax.all_to_all(payload, "wide", 0, 0)
+    payload = jnp.concatenate([source_maps.reshape(sub, rows, channels), tag], axis=2)
+    arrived = lax.all_to_all(payload, "sub", 0, 0)
     chunks = arrived[:, :, :channels]
     picks = arrived[:, 0, channels:channels + 2].astype(jnp.int32)
-    owners = hubs[picks]
-    parcel = chunks[owners]
-    got = lax.all_to_all(parcel, "wide", 0, 0)
+    mine = lax.axis_index("half")
+    local = chunks[hubs % sub]
+    mirror = lax.ppermute(local, "half", [(0, 1), (1, 0)])
+    here = (hubs // sub == mine)[:, None, None]
+    named = jnp.where(here, local, mirror)
+    parcel = named[picks]
+    got = lax.all_to_all(parcel, "sub", 0, 0)
     return jnp.swapaxes(got, 0, 1).reshape(2, cells, channels), parcel
 
 
 def per_device(
     query_maps, source_maps, hubs, pick, weight_first, bias_first, weight_second, bias_second,
-    wide,
+    sub,
 ):
-    chosen, parcel = gather_sources(source_maps, hubs, pick, wide)
+    chosen, parcel = gather_sources(source_maps, hubs, pick, sub)
     correlation = scaled_corr(query_maps, chosen)
     volumes = jnp.concatenate([correlation, jnp.swapaxes(correlation, 1, 2)], axis=0)
     k1, k2 = band_weights(weight_first, weight_second, parcel)
@@ -116,24 +120,27 @@
 
 
 def solution(mesh):
-    wide = mesh.shape["wide"]
+    groups, wide = mesh.shape["grp"], mesh.shape["wide"]
+    sub = wide // 2
+    split = jax.sharding.Mesh(mesh.devices.reshape(groups, 2, sub), ("grp", "half", "sub"))
+    spread = ("grp", "half", "sub")
 
     def body(*args):
-        return per_device(*args, wide)
+        return per_device(*args, sub)
 
     return jax.shard_map(
         body,
-        mesh=mesh,
+        mesh=split,
         in_specs=(
-            P(("grp", "wide"), None),
-            P(("grp", "wide"), None),
+            P(spread, None),
+            P(spread, None),
             P("grp"),
-            P(("grp", "wide"), None),
+            P(spread, None),
             P(),
             P(),
             P(),
             P(),
         ),
-        out_specs=P(("grp", "wide"), None, None, None),
+        out_specs=P(spread, None, None, None),
         check_vma=False,
     )

time: 58.7 us -> 57.8 us (0.985)
  starting transfers between devices: 13.4 us -> 11.6 us
  waiting for transfers between devices: 5.39 us -> 6.74 us
  local copies, waits for them, and re-layouts: 6.76 us -> 6.14 us
    ppermute x0 -> x1, waiting for transfers between devices: none -> 6.73 us  [gather_sources(): mirror = lax.ppermute(local, 'half', [(0, 1), (1, 0)])]
    all_to_all x2, waiting for transfers between devices: 5.39 us -> 0.01 us  [the longest x1 0.01 us: gather_sources(): arrived = lax.all_to_all(payload, 'sub', 0, 0)]
    all_to_all x2, starting transfers between devices: 13.4 us -> 8.96 us  [the longest x1 5.29 us: gather_sources(): arrived = lax.all_to_all(payload, 'sub', 0, 0)]
    ppermute x0 -> x1, starting transfers between devices: none -> 2.65 us  [gather_sources(): mirror = lax.ppermute(local, 'half', [(0, 1), (1, 0)])]
    gather x4 -> x2, local copies, waits for them, and re-layouts: 2.25 us -> 1.95 us  [the longest x1 1.39 us: gather_sources(): parcel = named[picks]]
  transfers between devices with their start and end apart: 2 -> 3, of which waited for: 1 -> 1; matrix products, arithmetic and copies ran while one was open for 34% -> 36% of each run, Pallas kernels for 0% -> 0%
where the time goes in v6:
time: 57.8 us; the launch traced here: 57.4 us
  other arithmetic  22 us (38%)
  starting transfers between devices  11.6 us (20%)
  matrix products  9.85 us (17%)
  waiting for transfers between devices  6.74 us (12%)
  local copies, waits for them, and re-layouts  6.14 us (11%)
  between operations  1.04 us (2%)
    select_n x2, other arithmetic, banded(): band = jnp.where(table[None] == e, spread_w[:, e, None, :], band)  14.5 us
    dot_general x1, matrix products, consensus_stack(): jnp.einsum('vak,kn->van', hidden, k2, preferred_element_type=jnp.float32)  9.55 us
    ppermute x1, waiting for transfers between devices, gather_sources(): mirror = lax.ppermute(local, 'half', [(0, 1), (1, 0)])  6.73 us
    all_to_all x1, starting transfers between devices, gather_sources(): arrived = lax.all_to_all(payload, 'sub', 0, 0)  5.29 us
    all_to_all x1, starting transfers between devices, gather_sources(): got = lax.all_to_all(parcel, 'sub', 0, 0)  3.67 us
    eq x2, other arithmetic, banded(): band = jnp.where(table[None] == e, spread_w[:, e, None, :], band)  3.1 us
    ppermute x1, starting transfers between devices, gather_sources(): mirror = lax.ppermute(local, 'half', [(0, 1), (1, 0)])  2.65 us
    concatenate x1, other arithmetic, gather_sources(): jnp.concatenate([source_maps.reshape(sub, rows, channels), tag], axis=2)  1.69 us
  transfers between devices with their start and end apart: 3, of which 1 were waited for; matrix products, arithmetic and copies ran while one was open for 36% of the time, Pallas kernels for 0%

profile of v6, /device:TPU:0, one launch (start us, length us, event | category | flops | bytes accessed | tf_op | source)
XLA Modules:
  0.0 57.4 jit_solution(1221452276988236193)
XLA Ops:
  0.0 0.7 %convert_element_type.44 = bf16[1,2]{1,0:T(2,128)(2,1)S(1)} convert(s32[1,2]{1,0:T(1,128)} %param.31) | non-fusion elementwise | flops 2 | bytes 12 | tf_op jit(solution)/shard_map/convert_element_type | solution.py:95
  0.7 1.7 %pad_maximum_fusion = bf16[8,16,1152]{2,1,0:T(8,128)(2,1)} fusion(bf16[8,16,128]{2,1,0:T(8,128)(2,1)S(1)} %scatter.8, bf16[8,16,1024]{2,1,0:T(8,128)(2,1)} %bitcast.91), kind=kLoop, calls=%fused_computation.59 | loop fusion | flops 589824 | bytes 589824 | tf_op jit(solution)/shard_map/concatenate | solution.py:96
  2.4 5.3 %all-to-all-start = ((bf16[8,16,1152]{2,1,0:T(8,128)(2,1)}), bf16[8,16,1152]{2,1,0:T(8,128)(2,1)S(1)}, u32[]{:S(2)}, u32[]{:S(2)}) async-start(bf16[8,16,1152]{2,1,0:T(8,128)(2,1)} %pad_maximum_fusion), calls=%async_computation | async-start | bytes 589824 | tf_op jit(solution)/shard_map/all_to_all | solution.py:97
  7.8 0.8 %reshape.1187 = bf16[16,9,9]{0,2,1:T(8,128)(2,1)S(1)} reshape(bf16[16,1,3,3,3,3]{0,5,4,3,2,1:T(4,128)(2,1)} %param.32) | data formatting | bytes 5184 | tf_op jit(solution)/shard_map/reshape | solution.py:33
  8.6 0.2 broadcast_in_dim.508
  8.8 0.2 reshape.1188
  9.0 0.1 slice_bitcast_fusion.9
  9.1 0.1 multiply_reduce_fusion.1
  9.3 0.1 broadcast_bitcast_fusion
  9.3 2.3 %broadcast_compare_fusion.4 = (pred[128,2048]{1,0:T(8,128)(4,1)S(1)}, pred[128,2048]{1,0:T(8,128)(4,1)S(1)}, pred[128,2048]{1,0:T(8,128)(4,1)S(1)}, pred[128,204...) fusion(s32[128]{0:T(128)S(1)} %get-tuple-element.72, ...), kind=kLoop, calls=%fused_computation.45 | loop fusion | flops 11796480 | bytes 2380032 | tf_op jit(solution)/shard_map/eq | solution.py:26
  11.7 7.2 %select_select_fusion.1 = bf16[9,128,2048]{2,1,0:T(8,128)(2,1)} fusion(pred[128,2048]{1,0:T(8,128)(4,1)S(1)} %get-tuple-element.61, pred[128,2048]{1,0:T(8,128)(4,1)S(1)} %get-tuple-element.60, pred[128,2048]{1,0:T(8,128)(4,1)S(1)} %get-tuple-element.59, pred[128,2048]{1,0:T(8,128)(4,1)S(1)} %get-tuple-element.58, ...), kind=kLoop, calls=%fused_computation.3 | loop fusion | flops 21233664 | bytes 7409664 | tf_op jit(solution)/shard_map/jit(_where)/select_n | solution.py:26
  19.5 0.4 add_select_fusion.5
  19.9 0.0 all-to-all-done
  19.9 0.0 copy-start.2
  20.0 0.6 gather_fusion
  20.5 2.7 %collective-permute-start = (bf16[4,16,1024]{2,1,0:T(8,128)(2,1)S(1)}, bf16[4,16,1024]{2,1,0:T(8,128)(2,1)S(1)}, u32[]{:S(2)}, u32[]{:S(2)}) collective-permute-start(bf16[4,16,1024]{2,1,0:T(8,128)(2,1)S(1)} %gather_fusion), channel_id=1, source_target_pairs={{0,8},{8,0},{1,9},{9,1},{2,10},{10,2},{3,11},{11,3},{4,12},{12,4},... | collective-permute-start | bytes 393224 | tf_op jit(solution)/shard_map/ppermute | solution.py:102
  23.2 0.1 copy.88
  23.3 0.1 copy.80
  23.4 0.1 reshape.1210
  23.5 6.7 %collective-permute-done = bf16[4,16,1024]{2,1,0:T(8,128)(2,1)S(1)} collective-permute-done((bf16[4,16,1024]{2,1,0:T(8,128)(2,1)S(1)}, bf16[4,16,1024]{2,1,0:T(8,128)(2,1)S(1)}, u32[]{:S(2)}, u32[]{:S(2)}) %collective-permute-start) | collective-permute-done | bytes 131104 | tf_op jit(solution)/shard_map/ppermute | solution.py:102
  30.2 0.1 broadcast_select_fusion
  30.3 1.4 %gather_fusion.1 = bf16[16,16,1024]{2,1,0:T(8,128)(2,1)} fusion(bf16[4,16,1024]{2,1,0:T(8,128)(2,1)S(1)} %broadcast_select_fusion, s32[1024]{0:T(1024)S(1)} %pad_clamp_fusion), kind=kCustom, calls=%fused_computation.1 | custom fusion | bytes 1048640 | tf_op jit(solution)/shard_map/gather | solution.py:105
  31.7 3.7 %all-to-all-start.1 = ((bf16[8,2,16,1024]{3,2,1,0:T(8,128)(2,1)}), bf16[8,2,16,1024]{3,2,1,0:T(8,128)(2,1)S(1)}, u32[]{:S(2)}, u32[]{:S(2)}) async-start(bf16[8,2,16,1024]{3,2,1,0:T(8,128)(2,1)} %bitcast.3), calls=%async_computation.1 | async-start | bytes 1048576 | tf_op jit(solution)/shard_map/all_to_all | solution.py:106
  35.4 0.8 %broadcast_compare_fusion.13 = (pred[128,1152]{1,0:T(8,128)(4,1)S(1)}, pred[128,1152]{1,0:T(8,128)(4,1)S(1)}, pred[128,1152]{1,0:T(8,128)(4,1)S(1)}, pred[128,11...) fusion(s32[128,1152]{1,0:T(8,128)S(1)} %add_select_fusion.5), kind=kLoop, calls=%fused_computation.64 | loop fusion | flops 1327104 | bytes 1916928 | tf_op jit(solution)/shard_map/eq | solution.py:26
  36.2 0.1 copy.85
  36.3 0.4 broadcast_in_dim.548
  36.7 0.2 reshape.1190
  37.0 7.3 %select_select_fusion = bf16[16,128,1152]{2,1,0:T(8,128)(2,1)} fusion(pred[128,1152]{1,0:T(8,128)(4,1)S(1)} %get-tuple-element.39, pred[128,1152]{1,0:T(8,128)(4,1)S(1)} %get-tuple-element.40, pred[128,1152]{1,0:T(8,128)(4,1)S(1)} %get-tuple-element.41, pred[128,1152]{1,0:T(8,128)(4,1)S(1)} %get-tuple-element.42, pred[128,1152]{1,0:T(8,128)(4,1)S(1)} %get-tuple-element.43, ...), kind=kLoop, calls=%fused_computation.2 | loop fusion | flops 21233664 | bytes 6377472 | tf_op jit(solution)/shard_map/jit(_where)/select_n | solution.py:26
  44.2 0.0 all-to-all-done.1
  44.3 0.3 fusion.33
  44.6 0.1 copy.82
  44.7 0.2 multiply_reduce_fusion
  44.9 0.1 sqrt.19
  45.0 0.1 fusion.51
  45.1 0.0 copy-done.3
  45.2 0.1 fusion.36
  45.3 0.1 fusion.39
  45.4 0.1 fusion.41
  45.6 0.1 fusion.43
  45.7 0.1 fusion.45
  45.9 0.1 fusion.48
  46.0 9.6 %fusion.8 = f32[4,128,1152]{2,1,0:T(8,128)S(1)} fusion(bf16[2048,1152,1]{1,0,2:T(8,128)(2,1)} %bitcast.87, bf16[4,128,1152]{2,1,0:T(8,128)(2,1)S(1)} %fusion.48, bf16[1152,2048,1]{1,0,2:T(8,128)(2,1)} %bitcast.89, f32[2048]{0:T(1024)S(1)} %broadcast_bitcast_fusion), kind=kOutput, calls=%fused_computation.31 | convolution fusion | flops 4834983936 | bytes 12984320 | tf_op jit(solution)/shard_map/vak,kn->van/dot_general | solution.py:67
  55.5 0.0 copy-start.5
  55.6 0.2 fusion.64
  55.8 0.4 copy-done.5
  56.2 0.3 fusion.27
  56.5 0.1 copy.89
  56.6 0.8 %copy.87 = f32[1,2,128,128]{3,2,1,0:T(8,128)} copy(f32[1,2,128,128]{2,3,1,0:T(8,128)S(1)} %fusion.50) | data formatting | bytes 262144 | tf_op jit(solution)/shard_map/broadcast_in_dim | solution.py:119
  (38 shorter events, 0.4 us)
Async XLA Ops:
  0.0 9.3 %copy-start = (f32[16]{0:T(128)S(1)}, f32[16]{0:T(128)}, u32[]{:S(2)}) copy-start(f32[16]{0:T(128)} %param.33) | copy-start | bytes 196
  0.0 9.1 %copy-start.6 = (s32[4]{0:T(128)S(1)}, s32[4]{0:T(128)}, u32[]{:S(2)}) copy-start(s32[4]{0:T(128)} %param.30) | copy-start | bytes 52
  0.0 9.1 %copy-start.1 = (bf16[128,1024]{1,0:T(8,128)(2,1)S(1)}, bf16[128,1024]{1,0:T(8,128)(2,1)}, u32[]{:S(2)}) copy-start(bf16[128,1024]{1,0:T(8,128)(2,1)} %param.28) | copy-start | bytes 786436
  2.4 17.5 %all-to-all-start = ((bf16[8,16,1152]{2,1,0:T(8,128)(2,1)}), bf16[8,16,1152]{2,1,0:T(8,128)(2,1)S(1)}, u32[]{:S(2)}, u32[]{:S(2)}) async-start(bf16[8,16,1152]{2,1,0:T(8,128)(2,1)} %pad_maximum_fusion), calls=%async_computation | async-start | bytes 589824 | tf_op jit(solution)/shard_map/all_to_all | solution.py:97
  19.9 16.2 %copy-start.2 = (bf16[1,16,3,3,3,3]{1,5,4,3,2,0:T(4,128)(2,1)S(1)}, bf16[1,16,3,3,3,3]{1,5,4,3,2,0:T(4,128)(2,1)}, u32[]{:S(2)}) copy-start(bf16[1,16,3,3,3,3]{1,5,4,3,2,0:T(4,128)(2,1)} %param.34) | copy-start | bytes 7780
  20.5 9.7 %collective-permute-start = (bf16[4,16,1024]{2,1,0:T(8,128)(2,1)S(1)}, bf16[4,16,1024]{2,1,0:T(8,128)(2,1)S(1)}, u32[]{:S(2)}, u32[]{:S(2)}) collective-permute-start(bf16[4,16,1024]{2,1,0:T(8,128)(2,1)S(1)} %gather_fusion), channel_id=1, source_target_pairs={{0,8},{8,0},{1,9},{9,1},{2,10},{10,2},{3,11},{11,3},{4,12},{12,4},... | collective-permute-start | bytes 393224 | tf_op jit(solution)/shard_map/ppermute | solution.py:102
  31.7 12.6 %all-to-all-start.1 = ((bf16[8,2,16,1024]{3,2,1,0:T(8,128)(2,1)}), bf16[8,2,16,1024]{3,2,1,0:T(8,128)(2,1)S(1)}, u32[]{:S(2)}, u32[]{:S(2)}) async-start(bf16[8,2,16,1024]{3,2,1,0:T(8,128)(2,1)} %bitcast.3), calls=%async_computation.1 | async-start | bytes 1048576 | tf_op jit(solution)/shard_map/all_to_all | solution.py:106
  44.2 0.9 %copy-start.3 = (pred[128]{0:T(512)(128)(4,1)S(1)}, pred[128]{0:T(512)(128)(4,1)}, u32[]{:S(2)}) copy-start(pred[128]{0:T(512)(128)(4,1)} %constant.239) | copy-start | bytes 388
  44.2 1.1 %copy-start.4 = (pred[128]{0:T(512)(128)(4,1)S(1)}, pred[128]{0:T(512)(128)(4,1)}, u32[]{:S(2)}) copy-start(pred[128]{0:T(512)(128)(4,1)} %constant.240) | copy-start | bytes 388
  55.5 0.7 %copy-start.5 = (pred[128]{0:T(512)(128)(4,1)S(1)}, pred[128]{0:T(512)(128)(4,1)}, u32[]{:S(2)}) copy-start(pred[128]{0:T(512)(128)(4,1)} %constant.240) | copy-start | bytes 388

commit v7 on v6

--- a/solution.py
+++ b/solution.py
@@ -87,7 +87,7 @@
     )
 
 
-def gather_sources(source_maps, hubs, pick, sub):
+def gather_sources(source_maps, hubs, pick, sub, build):
     cells, channels = source_maps.shape
     rows = cells // sub
     lanes = 128
@@ -100,21 +100,25 @@
     mine = lax.axis_index("half")
     local = chunks[hubs % sub]
     mirror = lax.ppermute(local, "half", [(0, 1), (1, 0)])
+    bands = build(local)
+    mirror, bands = lax.optimization_barrier((mirror, bands))
     here = (hubs // sub == mine)[:, None, None]
     named = jnp.where(here, local, mirror)
     parcel = named[picks]
     got = lax.all_to_all(parcel, "sub", 0, 0)
-    return jnp.swapaxes(got, 0, 1).reshape(2, cells, channels), parcel
+    return jnp.swapaxes(got, 0, 1).reshape(2, cells, channels), bands
 
 
 def per_device(
     query_maps, source_maps, hubs, pick, weight_first, bias_first, weight_second, bias_second,
     sub,
 ):
-    chosen, parcel = gather_sources(source_maps, hubs, pick, sub)
+    chosen, (k1, k2) = gather_sources(
+        source_maps, hubs, pick, sub,
+        lambda tie: band_weights(weight_first, weight_second, tie),
+    )
     correlation = scaled_corr(query_maps, chosen)
     volumes = jnp.concatenate([correlation, jnp.swapaxes(correlation, 1, 2)], axis=0)
-    k1, k2 = band_weights(weight_first, weight_second, parcel)
     filtered = consensus_stack(volumes, k1, k2, bias_first, bias_second)
     return (filtered[:2] + jnp.swapaxes(filtered[2:], 1, 2))[None]
 

time: 57.8 us -> 60.3 us (1.043)
  waiting for transfers between devices: 6.74 us -> 7.96 us
  starting transfers between devices: 11.6 us -> 12.3 us
    all_to_all x1, waiting for transfers between devices: 0.01 us -> 7.95 us  [gather_sources(): got = lax.all_to_all(parcel, 'sub', 0, 0)]
    ppermute x1, waiting for transfers between devices: 6.73 us -> 0.01 us  [gather_sources(): mirror = lax.ppermute(local, 'half', [(0, 1), (1, 0)])]
    all_to_all x1, starting transfers between devices: 3.67 us -> 4.33 us  [gather_sources(): got = lax.all_to_all(parcel, 'sub', 0, 0)]
    select_n x1, other arithmetic: 0.01 us -> 0.67 us  [gather_sources(): local = chunks[hubs % sub]]
  transfers between devices with their start and end apart: 3 -> 3, of which waited for: 1 -> 1; matrix products, arithmetic and copies ran while one was open for 36% -> 35% of each run, Pallas kernels for 0% -> 0%
where the time goes in v7:
time: 60.3 us; the launch traced here: 59.9 us
  other arithmetic  22.6 us (37%)
  starting transfers between devices  12.3 us (20%)
  matrix products  9.86 us (16%)
  waiting for transfers between devices  7.96 us (13%)
  local copies, waits for them, and re-layouts  6.13 us (10%)
  between operations  1.04 us (2%)
    select_n x2, other arithmetic, banded(): band = jnp.where(table[None] == e, spread_w[:, e, None, :], band)  14.4 us
    dot_general x1, matrix products, consensus_stack(): jnp.einsum('vak,kn->van', hidden, k2, preferred_element_type=jnp.float32)  9.55 us
    all_to_all x1, waiting for transfers between devices, gather_sources(): got = lax.all_to_all(parcel, 'sub', 0, 0)  7.95 us
    all_to_all x1, starting transfers between devices, gather_sources(): arrived = lax.all_to_all(payload, 'sub', 0, 0)  5.28 us
    all_to_all x1, starting transfers between devices, gather_sources(): got = lax.all_to_all(parcel, 'sub', 0, 0)  4.33 us
    eq x2, other arithmetic, banded(): band = jnp.where(table[None] == e, spread_w[:, e, None, :], band)  3.13 us
    ppermute x1, starting transfers between devices, gather_sources(): mirror = lax.ppermute(local, 'half', [(0, 1), (1, 0)])  2.65 us
    concatenate x1, other arithmetic, gather_sources(): jnp.concatenate([source_maps.reshape(sub, rows, channels), tag], axis=2)  1.69 us
  transfers between devices with their start and end apart: 3, of which 1 were waited for; matrix products, arithmetic and copies ran while one was open for 35% of the time, Pallas kernels for 0%

profile of v7, /device:TPU:0, one launch (start us, length us, event | category | flops | bytes accessed | tf_op | source)
XLA Modules:
  0.0 59.9 jit_solution(8806952332437811672)
XLA Ops:
  0.0 0.7 %convert_element_type.44 = bf16[1,2]{1,0:T(2,128)(2,1)S(1)} convert(s32[1,2]{1,0:T(1,128)} %param.31) | non-fusion elementwise | flops 2 | bytes 12 | tf_op jit(solution)/shard_map/convert_element_type | solution.py:95
  0.7 1.7 %pad_maximum_fusion = bf16[8,16,1152]{2,1,0:T(8,128)(2,1)} fusion(bf16[8,16,128]{2,1,0:T(8,128)(2,1)S(1)} %scatter.8, bf16[8,16,1024]{2,1,0:T(8,128)(2,1)} %bitcast.95), kind=kLoop, calls=%fused_computation.62 | loop fusion | flops 589824 | bytes 589824 | tf_op jit(solution)/shard_map/concatenate | solution.py:96
  2.4 5.3 %all-to-all-start = ((bf16[8,16,1152]{2,1,0:T(8,128)(2,1)}), bf16[8,16,1152]{2,1,0:T(8,128)(2,1)S(1)}, u32[]{:S(2)}, u32[]{:S(2)}) async-start(bf16[8,16,1152]{2,1,0:T(8,128)(2,1)} %pad_maximum_fusion), calls=%async_computation | async-start | bytes 589824 | tf_op jit(solution)/shard_map/all_to_all | solution.py:97
  7.8 0.7 %compare_select_fusion.1 = s32[4]{0:T(128)S(1)} fusion(s32[4]{0:T(128)} %param.30), kind=kLoop, calls=%fused_computation.156 | loop fusion | flops 56 | bytes 32 | tf_op jit(solution)/shard_map/select_n | solution.py:101
  8.4 0.8 %reshape.1186 = bf16[16,9,9]{0,2,1:T(8,128)(2,1)S(1)} reshape(bf16[16,1,3,3,3,3]{0,5,4,3,2,1:T(4,128)(2,1)} %param.32) | data formatting | bytes 5184 | tf_op jit(solution)/shard_map/reshape | solution.py:33
  9.2 0.2 broadcast_in_dim.491
  9.5 0.2 reshape.1187
  9.7 0.0 copy-done.6
  9.7 2.3 %broadcast_compare_fusion.4 = (pred[128,2048]{1,0:T(8,128)(4,1)S(1)}, pred[128,2048]{1,0:T(8,128)(4,1)S(1)}, pred[128,2048]{1,0:T(8,128)(4,1)S(1)}, pred[128,204...) fusion(s32[128]{0:T(128)S(1)} %get-tuple-element.78, ...), kind=kLoop, calls=%fused_computation.49 | loop fusion | flops 11796480 | bytes 2380032 | tf_op jit(solution)/shard_map/eq | solution.py:26
  12.1 7.2 %select_select_fusion.1 = bf16[9,128,2048]{2,1,0:T(8,128)(2,1)} fusion(pred[128,2048]{1,0:T(8,128)(4,1)S(1)} %get-tuple-element.67, pred[128,2048]{1,0:T(8,128)(4,1)S(1)} %get-tuple-element.66, pred[128,2048]{1,0:T(8,128)(4,1)S(1)} %get-tuple-element.65, pred[128,2048]{1,0:T(8,128)(4,1)S(1)} %get-tuple-element.64, ...), kind=kLoop, calls=%fused_computation.7 | loop fusion | flops 21233664 | bytes 7409664 | tf_op jit(solution)/shard_map/jit(_where)/select_n | solution.py:26
  19.3 0.4 add_select_fusion.5
  19.7 0.0 all-to-all-done
  19.7 0.6 gather_fusion
  20.3 2.7 %collective-permute-start = (bf16[4,16,1024]{2,1,0:T(8,128)(2,1)S(1)}, bf16[4,16,1024]{2,1,0:T(8,128)(2,1)S(1)}, u32[]{:S(2)}, u32[]{:S(2)}) collective-permute-start(bf16[4,16,1024]{2,1,0:T(8,128)(2,1)S(1)} %gather_fusion), channel_id=1, source_target_pairs={{0,8},{8,0},{1,9},{9,1},{2,10},{10,2},{3,11},{11,3},{4,12},{12,4},... | collective-permute-start | bytes 393224 | tf_op jit(solution)/shard_map/ppermute | solution.py:102
  22.9 0.8 %broadcast_compare_fusion.13 = (pred[128,1152]{1,0:T(8,128)(4,1)S(1)}, pred[128,1152]{1,0:T(8,128)(4,1)S(1)}, pred[128,1152]{1,0:T(8,128)(4,1)S(1)}, pred[128,11...) fusion(s32[128,1152]{1,0:T(8,128)S(1)} %add_select_fusion.5), kind=kLoop, calls=%fused_computation.67 | loop fusion | flops 1327104 | bytes 1916928 | tf_op jit(solution)/shard_map/eq | solution.py:26
  23.8 0.1 copy.80
  23.9 0.4 broadcast_in_dim.530
  24.3 0.2 reshape.1189
  24.5 0.1 copy.88
  24.6 7.2 %select_select_fusion = bf16[16,128,1152]{2,1,0:T(8,128)(2,1)} fusion(pred[128,1152]{1,0:T(8,128)(4,1)S(1)} %get-tuple-element.36, pred[128,1152]{1,0:T(8,128)(4,1)S(1)} %get-tuple-element.37, pred[128,1152]{1,0:T(8,128)(4,1)S(1)} %get-tuple-element.38, pred[128,1152]{1,0:T(8,128)(4,1)S(1)} %get-tuple-element.39, pred[128,1152]{1,0:T(8,128)(4,1)S(1)} %get-tuple-element.40, ...), kind=kLoop, calls=%fused_computation.6 | loop fusion | flops 21233664 | bytes 6377472 | tf_op jit(solution)/shard_map/jit(_where)/select_n | solution.py:26
  31.9 0.1 copy.82
  32.0 0.1 reshape.1210
  32.1 0.0 collective-permute-done
  32.1 0.1 broadcast_select_fusion
  32.2 1.4 %gather_fusion.1 = bf16[16,16,1024]{2,1,0:T(8,128)(2,1)} fusion(bf16[4,16,1024]{2,1,0:T(8,128)(2,1)S(1)} %broadcast_select_fusion, s32[1024]{0:T(1024)S(1)} %pad_clamp_fusion), kind=kCustom, calls=%fused_computation.1 | custom fusion | bytes 1048640 | tf_op jit(solution)/shard_map/gather | solution.py:107
  33.6 4.3 %all-to-all-start.1 = ((bf16[8,2,16,1024]{3,2,1,0:T(8,128)(2,1)}), bf16[8,2,16,1024]{3,2,1,0:T(8,128)(2,1)S(1)}, u32[]{:S(2)}, u32[]{:S(2)}) async-start(bf16[8,2,16,1024]{3,2,1,0:T(8,128)(2,1)} %bitcast.25), calls=%async_computation.1 | async-start | bytes 1048576 | tf_op jit(solution)/shard_map/all_to_all | solution.py:108
  38.6 0.0 copy-done.1
  38.6 0.1 multiply_reduce_fusion.1
  38.7 0.1 broadcast_bitcast_fusion
  38.8 8.0 %all-to-all-done.1 = bf16[8,2,16,1024]{3,2,1,0:T(8,128)(2,1)S(1)} async-done(((bf16[8,2,16,1024]{3,2,1,0:T(8,128)(2,1)}), bf16[8,2,16,1024]{3,2,1,0:T(8,128)(2,1)S(1)}, u32[]{:S(2)}, u32[]{:S(2)}) %all-to-all-start.1) | async-done | bytes 524320 | tf_op jit(solution)/shard_map/all_to_all | solution.py:108
  46.8 0.3 fusion.40
  47.1 0.1 copy.84
  47.2 0.2 multiply_reduce_fusion
  47.4 0.1 sqrt.19
  47.5 0.1 fusion.58
  47.7 0.1 fusion.43
  47.8 0.1 fusion.46
  47.9 0.1 fusion.48
  48.1 0.1 fusion.50
  48.2 0.1 fusion.52
  48.4 0.1 fusion.55
  48.5 9.6 %fusion = f32[4,128,1152]{2,1,0:T(8,128)S(1)} fusion(bf16[2048,1152]{1,0:T(8,128)(2,1)} %bitcast.91, bf16[4,128,1152]{2,1,0:T(8,128)(2,1)S(1)} %fusion.55, bf16[1152,2048]{1,0:T(8,128)(2,1)} %bitcast.93, f32[2048]{0:T(1024)S(1)} %broadcast_bitcast_fusion), kind=kOutput, calls=%fused_computation.2 | convolution fusion | flops 4834983936 | bytes 12984320 | tf_op jit(solution)/shard_map/vak,kn->van/dot_general | solution.py:67
  58.0 0.0 copy-start.5
  58.1 0.2 fusion.71
  58.3 0.4 copy-done.5
  58.7 0.3 fusion.34
  59.0 0.1 copy.89
  59.1 0.8 %copy.87 = f32[1,2,128,128]{3,2,1,0:T(8,128)} copy(f32[1,2,128,128]{2,3,1,0:T(8,128)S(1)} %fusion.57) | data formatting | bytes 262144 | tf_op jit(solution)/shard_map/broadcast_in_dim | solution.py:123
  (38 shorter events, 0.5 us)
Async XLA Ops:
  0.0 38.7 %copy-start = (f32[16]{0:T(128)S(1)}, f32[16]{0:T(128)}, u32[]{:S(2)}) copy-start(f32[16]{0:T(128)} %param.33) | copy-start | bytes 196
  0.0 9.7 %copy-start.6 = (s32[4]{0:T(128)S(1)}, s32[4]{0:T(128)}, u32[]{:S(2)}) copy-start(s32[4]{0:T(128)} %param.30) | copy-start | bytes 52
  2.4 17.3 %all-to-all-start = ((bf16[8,16,1152]{2,1,0:T(8,128)(2,1)}), bf16[8,16,1152]{2,1,0:T(8,128)(2,1)S(1)}, u32[]{:S(2)}, u32[]{:S(2)}) async-start(bf16[8,16,1152]{2,1,0:T(8,128)(2,1)} %pad_maximum_fusion), calls=%async_computation | async-start | bytes 589824 | tf_op jit(solution)/shard_map/all_to_all | solution.py:97
  19.3 4.5 %copy-start.2 = (bf16[1,16,3,3,3,3]{1,5,4,3,2,0:T(4,128)(2,1)S(1)}, bf16[1,16,3,3,3,3]{1,5,4,3,2,0:T(4,128)(2,1)}, u32[]{:S(2)}) copy-start(bf16[1,16,3,3,3,3]{1,5,4,3,2,0:T(4,128)(2,1)} %param.34) | copy-start | bytes 7780
  20.3 11.8 %collective-permute-start = (bf16[4,16,1024]{2,1,0:T(8,128)(2,1)S(1)}, bf16[4,16,1024]{2,1,0:T(8,128)(2,1)S(1)}, u32[]{:S(2)}, u32[]{:S(2)}) collective-permute-start(bf16[4,16,1024]{2,1,0:T(8,128)(2,1)S(1)} %gather_fusion), channel_id=1, source_target_pairs={{0,8},{8,0},{1,9},{9,1},{2,10},{10,2},{3,11},{11,3},{4,12},{12,4},... | collective-permute-start | bytes 393224 | tf_op jit(solution)/shard_map/ppermute | solution.py:102
  31.9 6.7 %copy-start.1 = (bf16[128,1024]{1,0:T(8,128)(2,1)S(1)}, bf16[128,1024]{1,0:T(8,128)(2,1)}, u32[]{:S(2)}) copy-start(bf16[128,1024]{1,0:T(8,128)(2,1)} %param.28) | copy-start | bytes 786436
  33.6 14.1 %copy-start.3 = (pred[128]{0:T(512)(128)(4,1)S(1)}, pred[128]{0:T(512)(128)(4,1)}, u32[]{:S(2)}) copy-start(pred[128]{0:T(512)(128)(4,1)} %constant.239) | copy-start | bytes 388
  33.6 13.2 %all-to-all-start.1 = ((bf16[8,2,16,1024]{3,2,1,0:T(8,128)(2,1)}), bf16[8,2,16,1024]{3,2,1,0:T(8,128)(2,1)S(1)}, u32[]{:S(2)}, u32[]{:S(2)}) async-start(bf16[8,2,16,1024]{3,2,1,0:T(8,128)(2,1)} %bitcast.25), calls=%async_computation.1 | async-start | bytes 1048576 | tf_op jit(solution)/shard_map/all_to_all | solution.py:108
  37.9 9.9 %copy-start.4 = (pred[128]{0:T(512)(128)(4,1)S(1)}, pred[128]{0:T(512)(128)(4,1)}, u32[]{:S(2)}) copy-start(pred[128]{0:T(512)(128)(4,1)} %constant.240) | copy-start | bytes 388
  58.0 0.7 %copy-start.5 = (pred[128]{0:T(512)(128)(4,1)S(1)}, pred[128]{0:T(512)(128)(4,1)}, u32[]{:S(2)}) copy-start(pred[128]{0:T(512)(128)(4,1)} %constant.240) | copy-start | bytes 388

commit v8 on v6

--- a/solution.py
+++ b/solution.py
@@ -27,19 +27,26 @@
     return band
 
 
-def band_weights(weight_first, weight_second, tie):
+def band_first(weight_first, tie):
     hid = weight_first.shape[0]
     cells = HQ * WQ
+    table, weight_first, _ = lax.optimization_barrier(
+        (tap_table(cells, hid * cells), weight_first, tie)
+    )
     w1 = weight_first.reshape(hid, TAPS, TAPS)
-    k1 = banded(jnp.transpose(w1, (1, 2, 0)), tap_table(cells, hid * cells), cells)
-    k1 = k1.reshape(TAPS * cells, hid * cells)
+    k1 = banded(jnp.transpose(w1, (1, 2, 0)), table, cells)
+    return k1.reshape(TAPS * cells, hid * cells)
+
+
+def band_second(weight_second, tie):
+    hid = weight_second.shape[1]
+    cells = HQ * WQ
     table, weight_second, _ = lax.optimization_barrier(
         (tap_table(cells, TAPS * cells), weight_second, tie)
     )
     w2 = weight_second.reshape(hid, TAPS, TAPS)
     k2 = banded(jnp.transpose(w2, (0, 2, 1)), table, cells)
-    k2 = k2.reshape(hid * cells, TAPS * cells)
-    return k1, k2
+    return k2.reshape(hid * cells, TAPS * cells)
 
 
 def row_shifts(x):
@@ -87,7 +94,7 @@
     )
 
 
-def gather_sources(source_maps, hubs, pick, sub):
+def gather_sources(source_maps, hubs, pick, sub, weight_first):
     cells, channels = source_maps.shape
     rows = cells // sub
     lanes = 128
@@ -100,21 +107,23 @@
     mine = lax.axis_index("half")
     local = chunks[hubs % sub]
     mirror = lax.ppermute(local, "half", [(0, 1), (1, 0)])
+    k1 = band_first(weight_first, local)
+    mirror, k1 = lax.optimization_barrier((mirror, k1))
     here = (hubs // sub == mine)[:, None, None]
     named = jnp.where(here, local, mirror)
     parcel = named[picks]
     got = lax.all_to_all(parcel, "sub", 0, 0)
-    return jnp.swapaxes(got, 0, 1).reshape(2, cells, channels), parcel
+    return jnp.swapaxes(got, 0, 1).reshape(2, cells, channels), parcel, k1
 
 
 def per_device(
     query_maps, source_maps, hubs, pick, weight_first, bias_first, weight_second, bias_second,
     sub,
 ):
-    chosen, parcel = gather_sources(source_maps, hubs, pick, sub)
+    chosen, parcel, k1 = gather_sources(source_maps, hubs, pick, sub, weight_first)
     correlation = scaled_corr(query_maps, chosen)
     volumes = jnp.concatenate([correlation, jnp.swapaxes(correlation, 1, 2)], axis=0)
-    k1, k2 = band_weights(weight_first, weight_second, parcel)
+    k2 = band_second(weight_second, parcel)
     filtered = consensus_stack(volumes, k1, k2, bias_first, bias_second)
     return (filtered[:2] + jnp.swapaxes(filtered[2:], 1, 2))[None]
 

time: 57.8 us -> 59.5 us (1.029)
  other arithmetic: 22 us -> 27 us
  waiting for transfers between devices: 6.74 us -> 2.11 us
  local copies, waits for them, and re-layouts: 6.14 us -> 7.26 us
    ppermute x1, waiting for transfers between devices: 6.73 us -> 0.01 us  [gather_sources(): mirror = lax.ppermute(local, 'half', [(0, 1), (1, 0)])]
    all_to_all x1, waiting for transfers between devices: 0.01 us -> 2.1 us  [gather_sources(): arrived = lax.all_to_all(payload, 'sub', 0, 0)]
    select_n x2, other arithmetic: 14.5 us -> 15.6 us  [banded(): band = jnp.where(table[None] == e, spread_w[:, e, None, :], band)]
    select_n x1, other arithmetic: 0.08 us -> 1.05 us  [gather_sources(): named = jnp.where(here, local, mirror)]
    reduce_sum x1, other arithmetic: 0.13 us -> 1.08 us  [scaled_corr(): query_rms = jnp.sqrt(jnp.mean(query_f * query_f, axis=-1) + 1e-06)]
    reshape x2, local copies, waits for them, and re-layouts: 0.8 us -> 0.05 us  [the longest x1 0.03 us: band_second(): w2 = weight_second.reshape(hid, TAPS, TAPS)]
    eq x1, other arithmetic: 0.01 us -> 0.67 us  [gather_sources(): here = (hubs // sub == mine)[:, None, None]]
    select_n x1, other arithmetic: 0.01 us -> 0.67 us  [gather_sources(): local = chunks[hubs % sub]]
  transfers between devices with their start and end apart: 3 -> 3, of which waited for: 1 -> 1; matrix products, arithmetic and copies ran while one was open for 36% -> 41% of each run, Pallas kernels for 0% -> 0%
where the time goes in v8:
time: 59.5 us; the launch traced here: 59 us
  other arithmetic  27 us (45%)
  starting transfers between devices  11.5 us (19%)
  matrix products  10.1 us (17%)
  local copies, waits for them, and re-layouts  7.26 us (12%)
  waiting for transfers between devices  2.11 us (4%)
  between operations  1.01 us (2%)
    select_n x2, other arithmetic, banded(): band = jnp.where(table[None] == e, spread_w[:, e, None, :], band)  15.6 us
    dot_general x1, matrix products, consensus_stack(): jnp.einsum('vak,kn->van', hidden, k2, preferred_element_type=jnp.float32)  9.81 us
    all_to_all x1, starting transfers between devices, gather_sources(): arrived = lax.all_to_all(payload, 'sub', 0, 0)  5.28 us
    all_to_all x1, starting transfers between devices, gather_sources(): got = lax.all_to_all(parcel, 'sub', 0, 0)  3.67 us
    eq x2, other arithmetic, banded(): band = jnp.where(table[None] == e, spread_w[:, e, None, :], band)  3.13 us
    ppermute x1, starting transfers between devices, gather_sources(): mirror = lax.ppermute(local, 'half', [(0, 1), (1, 0)])  2.59 us
    all_to_all x1, waiting for transfers between devices, gather_sources(): arrived = lax.all_to_all(payload, 'sub', 0, 0)  2.1 us
    concatenate x1, other arithmetic, gather_sources(): jnp.concatenate([source_maps.reshape(sub, rows, channels), tag], axis=2)  1.68 us
  transfers between devices with their start and end apart: 3, of which 1 were waited for; matrix products, arithmetic and copies ran while one was open for 41% of the time, Pallas kernels for 0%

profile of v8, /device:TPU:0, one launch (start us, length us, event | category | flops | bytes accessed | tf_op | source)
XLA Modules:
  0.0 59.0 jit_solution(5176322056664019285)
XLA Ops:
  0.0 0.7 %convert_element_type.44 = bf16[1,2]{1,0:T(2,128)(2,1)S(1)} convert(s32[1,2]{1,0:T(1,128)} %param.31) | non-fusion elementwise | flops 2 | bytes 12 | tf_op jit(solution)/shard_map/convert_element_type | solution.py:102
  0.7 1.7 %pad_maximum_fusion = bf16[8,16,1152]{2,1,0:T(8,128)(2,1)} fusion(bf16[8,16,128]{2,1,0:T(8,128)(2,1)S(1)} %scatter.8, bf16[8,16,1024]{2,1,0:T(8,128)(2,1)} %bitcast.95), kind=kLoop, calls=%fused_computation.61 | loop fusion | flops 589824 | bytes 589824 | tf_op jit(solution)/shard_map/concatenate | solution.py:103
  2.4 5.3 %all-to-all-start = ((bf16[8,16,1152]{2,1,0:T(8,128)(2,1)}), bf16[8,16,1152]{2,1,0:T(8,128)(2,1)S(1)}, u32[]{:S(2)}, u32[]{:S(2)}) async-start(bf16[8,16,1152]{2,1,0:T(8,128)(2,1)} %pad_maximum_fusion), calls=%async_computation | async-start | bytes 589824 | tf_op jit(solution)/shard_map/all_to_all | solution.py:104
  7.7 0.7 %compare_select_fusion.1 = s32[4]{0:T(128)S(1)} fusion(s32[4]{0:T(128)} %param.30), kind=kLoop, calls=%fused_computation.155 | loop fusion | flops 56 | bytes 32 | tf_op jit(solution)/shard_map/select_n | solution.py:108
  8.4 0.7 %fusion.68 = pred[4]{0:T(512)(128)(4,1)S(1)} fusion(s32[4]{0:T(128)} %param.30, s32[]{:T(128)S(6)} %axis_index.15), kind=kLoop, calls=%fused_computation.167 | loop fusion | flops 64 | bytes 24 | tf_op jit(solution)/shard_map/eq | solution.py:112
  9.1 1.1 %multiply_reduce_fusion.1 = f32[128]{0:T(128)S(1)} fusion(bf16[128,1024]{1,0:T(8,128)(2,1)} %param.28), kind=kLoop, calls=%fused_computation.43 | loop fusion | flops 393088 | bytes 262656 | tf_op jit(solution)/shard_map/reduce_sum | solution.py:88
  10.2 0.1 broadcast_bitcast_fusion
  10.2 0.6 %add_select_fusion.2 = s32[128,2048]{1,0:T(8,128)S(1)} fusion(s32[128]{0:T(128)S(1)} %get-tuple-element.80, s32[128]{0:T(128)S(1)} %get-tuple-element.81, s32[2048]{0:T(1024)S(1)} %get-tuple-element.83, s32[2048]{0:T(1024)S(1)} %get-tuple-element.84, s32[128]{0:T(128)S(1)} %get-tuple-element.79, s32[128]{0:T(128)S(1)} %get-tuple-element.82, ...), kind=kLoop, calls=%fused_computation.27 | loop fusion | flops 9437184 | bytes 1069312 | tf_op jit(solution)/shard_map/jit(_where)/select_n | solution.py:18
  11.5 0.0 copy-start.2
  11.5 0.4 add_select_fusion.5
  12.0 2.1 %all-to-all-done = bf16[8,16,1152]{2,1,0:T(8,128)(2,1)S(1)} async-done(((bf16[8,16,1152]{2,1,0:T(8,128)(2,1)}), bf16[8,16,1152]{2,1,0:T(8,128)(2,1)S(1)}, u32[]{:S(2)}, u32[]{:S(2)}) %all-to-all-start) | async-done | bytes 294944 | tf_op jit(solution)/shard_map/all_to_all | solution.py:104
  14.1 1.2 %gather_fusion = bf16[4,16,1024]{2,1,0:T(8,128)(2,1)} fusion(bf16[8,16,1024]{2,1,0:T(8,128)(2,1)S(1)} %slice.217, s32[1024]{0:T(1024)S(1)} %pad_clamp_fusion.1), kind=kCustom, calls=%fused_computation | custom fusion | bytes 262160 | tf_op jit(solution)/shard_map/gather | solution.py:108
  15.3 2.6 %collective-permute-start = (bf16[4,16,1024]{2,1,0:T(8,128)(2,1)}, bf16[4,16,1024]{2,1,0:T(8,128)(2,1)}, u32[]{:S(2)}, u32[]{:S(2)}) collective-permute-start(bf16[4,16,1024]{2,1,0:T(8,128)(2,1)} %gather_fusion), channel_id=1, source_target_pairs={{0,8},{8,0},{1,9},{9,1},{2,10},{10,2},{3,11},{11,3},{4,12},{12,4},... | collective-permute-start | bytes 393224 | tf_op jit(solution)/shard_map/ppermute | solution.py:109
  17.9 2.4 %broadcast_compare_fusion.4 = (pred[128,2048]{1,0:T(8,128)(4,1)S(1)}, pred[128,2048]{1,0:T(8,128)(4,1)S(1)}, pred[128,2048]{1,0:T(8,128)(4,1)S(1)}, pred[128,204...) fusion(s32[128,2048]{1,0:T(8,128)S(1)} %add_select_fusion.2), kind=kLoop, calls=%fused_computation.48 | loop fusion | flops 2359296 | bytes 3407872 | tf_op jit(solution)/shard_map/eq | solution.py:26
  20.3 0.2 broadcast_in_dim.491
  20.6 0.2 reshape.190
  20.8 0.7 %slice_bitcast_fusion.9 = (bf16[9,2048]{1,0:T(8,128)(2,1)S(1)}, bf16[9,2048]{1,0:T(8,128)(2,1)S(1)}, bf16[9,2048]{1,0:T(8,128)(2,1)S(1)}, bf16[9,2048]{1,0:T(8,1...) fusion(bf16[9,9,2048]{2,0,1:T(8,128)(2,1)S(1)} %reshape.190), kind=kLoop, calls=%fused_computation.127 | loop fusion | bytes 663552 | tf_op jit(solution)/shard_map/jit(_where)/broadcast_in_dim | solution.py:26
  21.5 0.1 copy.88
  21.6 8.3 %select_select_fusion.1 = bf16[9,128,2048]{2,1,0:T(8,128)(2,1)} fusion(pred[128,2048]{1,0:T(8,128)(4,1)S(1)} %get-tuple-element.38, pred[128,2048]{1,0:T(8,128)(4,1)S(1)} %get-tuple-element.39, pred[128,2048]{1,0:T(8,128)(4,1)S(1)} %get-tuple-element.40, pred[128,2048]{1,0:T(8,128)(4,1)S(1)} %get-tuple-element.41, ...), kind=kLoop, calls=%fused_computation.5 | loop fusion | flops 21233664 | bytes 7409664 | tf_op jit(solution)/shard_map/jit(_where)/select_n | solution.py:26
  29.9 0.1 copy.81
  30.0 0.1 reshape.213
  30.1 0.0 collective-permute-done
  30.1 1.1 %broadcast_select_fusion = bf16[4,16,1024]{2,1,0:T(8,128)(2,1)S(1)} fusion(bf16[4,16,1024]{2,1,0:T(8,128)(2,1)} %gather_fusion, bf16[4,16,1024]{2,1,0:T(8,128)(2,1)} %collective-permute-done, pred[4]{0:T(512)(128)(4,1)S(1)} %fusion.68), kind=kLoop, calls=%fused_computation.118 | loop fusion | flops 65536 | bytes 393220 | tf_op jit(solution)/shard_map/jit(_where)/select_n | solution.py:113
  31.1 1.4 %gather_fusion.1 = bf16[16,16,1024]{2,1,0:T(8,128)(2,1)} fusion(bf16[4,16,1024]{2,1,0:T(8,128)(2,1)S(1)} %broadcast_select_fusion, s32[1024]{0:T(1024)S(1)} %pad_clamp_fusion), kind=kCustom, calls=%fused_computation.1 | custom fusion | bytes 1048640 | tf_op jit(solution)/shard_map/gather | solution.py:114
  32.5 3.7 %all-to-all-start.1 = ((bf16[8,2,16,1024]{3,2,1,0:T(8,128)(2,1)}), bf16[8,2,16,1024]{3,2,1,0:T(8,128)(2,1)S(1)}, u32[]{:S(2)}, u32[]{:S(2)}) async-start(bf16[8,2,16,1024]{3,2,1,0:T(8,128)(2,1)} %bitcast.14), calls=%async_computation.1 | async-start | bytes 1048576 | tf_op jit(solution)/shard_map/all_to_all | solution.py:115
  36.2 0.7 %broadcast_compare_fusion.13 = (pred[128,1152]{1,0:T(8,128)(4,1)S(1)}, pred[128,1152]{1,0:T(8,128)(4,1)S(1)}, pred[128,1152]{1,0:T(8,128)(4,1)S(1)}, pred[128,11...) fusion(s32[128,1152]{1,0:T(8,128)S(1)} %add_select_fusion.5), kind=kLoop, calls=%fused_computation.66 | loop fusion | flops 1327104 | bytes 1916928 | tf_op jit(solution)/shard_map/eq | solution.py:26
  37.0 0.1 copy.85
  37.1 0.4 broadcast_in_dim.548
  37.5 0.2 reshape.193
  37.7 0.0 copy-start.1
  37.7 7.3 %select_select_fusion = bf16[16,128,1152]{2,1,0:T(8,128)(2,1)} fusion(pred[128,1152]{1,0:T(8,128)(4,1)S(1)} %get-tuple-element.47, pred[128,1152]{1,0:T(8,128)(4,1)S(1)} %get-tuple-element.48, pred[128,1152]{1,0:T(8,128)(4,1)S(1)} %get-tuple-element.49, pred[128,1152]{1,0:T(8,128)(4,1)S(1)} %get-tuple-element.50, pred[128,1152]{1,0:T(8,128)(4,1)S(1)} %get-tuple-element.51, ...), kind=kLoop, calls=%fused_computation.4 | loop fusion | flops 21233664 | bytes 6377472 | tf_op jit(solution)/shard_map/jit(_where)/select_n | solution.py:26
  45.1 0.3 fusion.39
  45.4 0.1 copy.83
  45.5 0.2 multiply_reduce_fusion
  45.7 0.1 sqrt.19
  45.8 0.1 fusion.57
  46.0 0.1 fusion.42
  46.1 0.1 fusion.45
  46.2 0.1 fusion.47
  46.4 0.1 fusion.49
  46.5 0.1 fusion.51
  46.7 0.1 fusion.54
  46.8 1.0 %copy-done.4 = bf16[4,128,1152]{2,1,0:T(8,128)(2,1)} copy-done((bf16[4,128,1152]{2,1,0:T(8,128)(2,1)}, bf16[4,128,1152]{2,1,0:T(8,128)(2,1)S(1)}, u32[]{:S(2)}) %copy-start.4) | copy-done | bytes 1179672
  47.8 9.8 %fusion.13 = f32[4,128,1152]{2,1,0:T(8,128)S(1)} fusion(bf16[2048,1152,1]{1,0,2:T(8,128)(2,1)} %bitcast.91, bf16[4,128,1152]{2,1,0:T(8,128)(2,1)} %copy-done.4, bf16[1152,2048]{1,0:T(8,128)(2,1)} %bitcast.93, f32[2048]{0:T(1024)S(1)} %broadcast_bitcast_fusion), kind=kOutput, calls=%fused_computation.33 | convolution fusion | flops 4834983936 | bytes 12984320 | tf_op jit(solution)/shard_map/vak,kn->van/dot_general | solution.py:74
  57.6 0.2 fusion.70
  57.8 0.3 fusion.33
  58.2 0.1 copy.89
  58.3 0.8 %copy.87 = f32[1,2,128,128]{3,2,1,0:T(8,128)} copy(f32[1,2,128,128]{2,3,1,0:T(8,128)S(1)} %fusion.56) | data formatting | bytes 262144 | tf_op jit(solution)/shard_map/broadcast_in_dim | solution.py:128
  (39 shorter events, 0.4 us)
Async XLA Ops:
  0.0 10.2 %copy-start = (f32[16]{0:T(128)S(1)}, f32[16]{0:T(128)}, u32[]{:S(2)}) copy-start(f32[16]{0:T(128)} %param.33) | copy-start | bytes 196
  2.4 11.7 %all-to-all-start = ((bf16[8,16,1152]{2,1,0:T(8,128)(2,1)}), bf16[8,16,1152]{2,1,0:T(8,128)(2,1)S(1)}, u32[]{:S(2)}, u32[]{:S(2)}) async-start(bf16[8,16,1152]{2,1,0:T(8,128)(2,1)} %pad_maximum_fusion), calls=%async_computation | async-start | bytes 589824 | tf_op jit(solution)/shard_map/all_to_all | solution.py:104
  11.5 8.8 %copy-start.2 = (bf16[16,1,3,3,3,3]{0,5,4,3,2,1:T(4,128)(2,1)S(1)}, bf16[16,1,3,3,3,3]{0,5,4,3,2,1:T(4,128)(2,1)}, u32[]{:S(2)}) copy-start(bf16[16,1,3,3,3,3]{0,5,4,3,2,1:T(4,128)(2,1)} %param.32) | copy-start | bytes 7780
  15.3 14.8 %collective-permute-start = (bf16[4,16,1024]{2,1,0:T(8,128)(2,1)}, bf16[4,16,1024]{2,1,0:T(8,128)(2,1)}, u32[]{:S(2)}, u32[]{:S(2)}) collective-permute-start(bf16[4,16,1024]{2,1,0:T(8,128)(2,1)} %gather_fusion), channel_id=1, source_target_pairs={{0,8},{8,0},{1,9},{9,1},{2,10},{10,2},{3,11},{11,3},{4,12},{12,4},... | collective-permute-start | bytes 393224 | tf_op jit(solution)/shard_map/ppermute | solution.py:109
  29.9 7.1 %copy-start.3 = (bf16[1,16,3,3,3,3]{1,5,4,3,2,0:T(4,128)(2,1)S(1)}, bf16[1,16,3,3,3,3]{1,5,4,3,2,0:T(4,128)(2,1)}, u32[]{:S(2)}) copy-start(bf16[1,16,3,3,3,3]{1,5,4,3,2,0:T(4,128)(2,1)} %param.34) | copy-start | bytes 7780
  32.5 12.5 %all-to-all-start.1 = ((bf16[8,2,16,1024]{3,2,1,0:T(8,128)(2,1)}), bf16[8,2,16,1024]{3,2,1,0:T(8,128)(2,1)S(1)}, u32[]{:S(2)}, u32[]{:S(2)}) async-start(bf16[8,2,16,1024]{3,2,1,0:T(8,128)(2,1)} %bitcast.14), calls=%async_computation.1 | async-start | bytes 1048576 | tf_op jit(solution)/shard_map/all_to_all | solution.py:115
  37.7 7.4 %copy-start.1 = (bf16[128,1024]{1,0:T(8,128)(2,1)S(1)}, bf16[128,1024]{1,0:T(8,128)(2,1)}, u32[]{:S(2)}) copy-start(bf16[128,1024]{1,0:T(8,128)(2,1)} %param.28) | copy-start | bytes 786436
  45.0 0.9 %copy-start.5 = (pred[128]{0:T(512)(128)(4,1)S(1)}, pred[128]{0:T(512)(128)(4,1)}, u32[]{:S(2)}) copy-start(pred[128]{0:T(512)(128)(4,1)} %constant.239) | copy-start | bytes 388
  45.0 1.1 %copy-start.6 = (pred[128]{0:T(512)(128)(4,1)S(1)}, pred[128]{0:T(512)(128)(4,1)}, u32[]{:S(2)}) copy-start(pred[128]{0:T(512)(128)(4,1)} %constant.240) | copy-start | bytes 388
  46.8 1.0 %copy-start.4 = (bf16[4,128,1152]{2,1,0:T(8,128)(2,1)}, bf16[4,128,1152]{2,1,0:T(8,128)(2,1)S(1)}, u32[]{:S(2)}) copy-start(bf16[4,128,1152]{2,1,0:T(8,128)(2,1)S(1)} %fusion.54) | copy-start | bytes 3538948

commit v9 on v6

--- a/solution.py
+++ b/solution.py
@@ -1,7 +1,11 @@
+import functools
+
 import numpy as np
 import jax
 import jax.numpy as jnp
 from jax import lax
+from jax.experimental import pallas as pl
+from jax.experimental.pallas import tpu as pltpu
 from jax.sharding import PartitionSpec as P
 
 HQ = 4
@@ -9,36 +13,48 @@
 TAPS = 9
 
 
-def tap_table(cells, cols):
-    row = lax.broadcasted_iota(jnp.int32, (cells, cols), 0)
-    col = lax.broadcasted_iota(jnp.int32, (cells, cols), 1) % cells
-    e1 = row // WQ - col // WQ + 1
-    e2 = row % WQ - col % WQ + 1
-    inside = (e1 >= 0) & (e1 < 3) & (e2 >= 0) & (e2 < 3)
-    return jnp.where(inside, e1 * 3 + e2, -1)
+def band_kernel(w_ref, out_ref, *, groups):
+    r = pl.program_id(0)
+    cells = HQ * WQ
+    row = lax.broadcasted_iota(jnp.int32, (WQ, cells), 0)
+    lane = lax.broadcasted_iota(jnp.int32, (WQ, cells), 1)
+    diff = row - lane % WQ + 1
+    masks = [(diff == k).astype(jnp.float32) for k in range(3)]
+    block = lax.broadcasted_iota(jnp.int32, (1, cells), 1) // WQ
+    for g in range(groups):
+        for rb in range(HQ):
+            e1 = rb - block + 1
+            total = None
+            for k in range(3):
+                wv = jnp.zeros((1, cells), jnp.float32)
+                for j in range(3):
+                    wv = jnp.where(e1 == j, w_ref[r, (j * 3 + k) * groups + g], wv)
+                term = masks[k] * wv
+                total = term if total is None else total + term
+            out_ref[0, rb * WQ:(rb + 1) * WQ, g * cells:(g + 1) * cells] = total.astype(out_ref.dtype)
 
 
-def banded(weights, table, cells):
+def banded(weights):
     rows, _, groups = weights.shape
-    spread_w = jnp.repeat(weights, cells, axis=2)
-    band = jnp.zeros((rows, cells, groups * cells), weights.dtype)
-    for e in range(TAPS):
-        band = jnp.where(table[None] == e, spread_w[:, e, None, :], band)
-    return band
+    cells = HQ * WQ
+    flat = weights.astype(jnp.float32).reshape(rows, TAPS * groups)
+    return pl.pallas_call(
+        functools.partial(band_kernel, groups=groups),
+        out_shape=jax.ShapeDtypeStruct((rows, cells, groups * cells), weights.dtype),
+        grid=(rows,),
+        in_specs=[pl.BlockSpec(memory_space=pltpu.SMEM)],
+        out_specs=pl.BlockSpec((1, cells, groups * cells), lambda r: (r, 0, 0)),
+    )(flat)
 
 
 def band_weights(weight_first, weight_second, tie):
     hid = weight_first.shape[0]
     cells = HQ * WQ
     w1 = weight_first.reshape(hid, TAPS, TAPS)
-    k1 = banded(jnp.transpose(w1, (1, 2, 0)), tap_table(cells, hid * cells), cells)
-    k1 = k1.reshape(TAPS * cells, hid * cells)
-    table, weight_second, _ = lax.optimization_barrier(
-        (tap_table(cells, TAPS * cells), weight_second, tie)
-    )
+    k1 = banded(jnp.transpose(w1, (1, 2, 0))).reshape(TAPS * cells, hid * cells)
+    weight_second, _ = lax.optimization_barrier((weight_second, tie))
     w2 = weight_second.reshape(hid, TAPS, TAPS)
-    k2 = banded(jnp.transpose(w2, (0, 2, 1)), table, cells)
-    k2 = k2.reshape(hid * cells, TAPS * cells)
+    k2 = banded(jnp.transpose(w2, (0, 2, 1))).reshape(hid * cells, TAPS * cells)
     return k1, k2
 
 

time: 57.8 us -> 60 us (1.038)
  other arithmetic: 22 us -> 3.99 us
  Pallas kernels: 0 us -> 15.5 us
  waiting for transfers between devices: 6.74 us -> 12.3 us
    pallas_call x0 -> x2, Pallas kernels: none -> 15.5 us  [banded(): pl.pallas_call(functools.partial(band_kernel, groups=groups), out_shape=j...]
    select_n x3 -> x0, other arithmetic: 14.9 us -> none  [the longest x2 14.5 us: banded(): band = jnp.where(table[None] == e, spread_w[:, e, None, :], band)]
    all_to_all x1, waiting for transfers between devices: 0.01 us -> 6.34 us  [gather_sources(): arrived = lax.all_to_all(payload, 'sub', 0, 0)]
    eq x2 -> x0, other arithmetic: 3.1 us -> none  [banded(): band = jnp.where(table[None] == e, spread_w[:, e, None, :], band)]
    ppermute x1, waiting for transfers between devices: 6.73 us -> 5.94 us  [gather_sources(): mirror = lax.ppermute(local, 'half', [(0, 1), (1, 0)])]
    broadcast_in_dim x4 -> x0, local copies, waits for them, and re-layouts: 0.69 us -> none  [the longest x2 0.61 us: banded(): spread_w = jnp.repeat(weights, cells, axis=2)]
    reshape x4 -> x6, local copies, waits for them, and re-layouts: 1.16 us -> 1.42 us  [banded(): flat = weights.astype(jnp.float32).reshape(rows, TAPS * groups)]
  transfers between devices with their start and end apart: 3 -> 3, of which waited for: 1 -> 2; matrix products, arithmetic and copies ran while one was open for 36% -> 3% of each run, Pallas kernels for 0% -> 26%
where the time goes in v9:
time: 60 us; the launch traced here: 59.6 us
  Pallas kernels  15.5 us (26%)
  waiting for transfers between devices  12.3 us (20%)
  starting transfers between devices  11.4 us (19%)
  matrix products  9.86 us (16%)
  local copies, waits for them, and re-layouts  5.56 us (9%)
  other arithmetic  3.99 us (7%)
  between operations  0.95 us (2%)
    pallas_call x2, Pallas kernels, banded(): pl.pallas_call(functools.partial(band_kernel, groups=groups), out_shape=j...  15.5 us
    dot_general x1, matrix products, consensus_stack(): jnp.einsum('vak,kn->van', hidden, k2, preferred_element_type=jnp.float32)  9.55 us
    all_to_all x1, waiting for transfers between devices, gather_sources(): arrived = lax.all_to_all(payload, 'sub', 0, 0)  6.34 us
    ppermute x1, waiting for transfers between devices, gather_sources(): mirror = lax.ppermute(local, 'half', [(0, 1), (1, 0)])  5.94 us
    all_to_all x1, starting transfers between devices, gather_sources(): arrived = lax.all_to_all(payload, 'sub', 0, 0)  5.28 us
    all_to_all x1, starting transfers between devices, gather_sources(): got = lax.all_to_all(parcel, 'sub', 0, 0)  3.49 us
    ppermute x1, starting transfers between devices, gather_sources(): mirror = lax.ppermute(local, 'half', [(0, 1), (1, 0)])  2.65 us
    concatenate x1, other arithmetic, gather_sources(): jnp.concatenate([source_maps.reshape(sub, rows, channels), tag], axis=2)  1.69 us
  transfers between devices with their start and end apart: 3, of which 2 were waited for; matrix products, arithmetic and copies ran while one was open for 3% of the time, Pallas kernels for 26%

profile of v9, /device:TPU:0, one launch (start us, length us, event | category | flops | bytes accessed | tf_op | source)
XLA Modules:
  0.0 59.6 jit_solution(11940183718780819874)
XLA Ops:
  0.0 0.0 copy-start
  0.0 0.7 %convert_element_type.58 = bf16[1,2]{1,0:T(2,128)(2,1)S(1)} convert(s32[1,2]{1,0:T(1,128)} %param.31) | non-fusion elementwise | flops 2 | bytes 12 | tf_op jit(solution)/shard_map/convert_element_type | solution.py:111
  0.7 1.7 %pad_maximum_fusion = bf16[8,16,1152]{2,1,0:T(8,128)(2,1)} fusion(bf16[8,16,128]{2,1,0:T(8,128)(2,1)S(1)} %scatter.8, bf16[8,16,1024]{2,1,0:T(8,128)(2,1)} %bitcast.55), kind=kLoop, calls=%fused_computation.14 | loop fusion | flops 589824 | bytes 589824 | tf_op jit(solution)/shard_map/concatenate | solution.py:112
  2.4 5.3 %all-to-all-start = ((bf16[8,16,1152]{2,1,0:T(8,128)(2,1)}), bf16[8,16,1152]{2,1,0:T(8,128)(2,1)S(1)}, u32[]{:S(2)}, u32[]{:S(2)}) async-start(bf16[8,16,1152]{2,1,0:T(8,128)(2,1)} %pad_maximum_fusion), calls=%async_computation | async-start | bytes 589824 | tf_op jit(solution)/shard_map/all_to_all | solution.py:113
  7.7 0.0 copy-done.7
  7.7 6.3 %all-to-all-done = bf16[8,16,1152]{2,1,0:T(8,128)(2,1)S(1)} async-done(((bf16[8,16,1152]{2,1,0:T(8,128)(2,1)}), bf16[8,16,1152]{2,1,0:T(8,128)(2,1)S(1)}, u32[]{:S(2)}, u32[]{:S(2)}) %all-to-all-start) | async-done | bytes 294944 | tf_op jit(solution)/shard_map/all_to_all | solution.py:113
  14.1 0.6 gather_fusion
  14.7 2.7 %collective-permute-start = (bf16[4,16,1024]{2,1,0:T(8,128)(2,1)S(1)}, bf16[4,16,1024]{2,1,0:T(8,128)(2,1)S(1)}, u32[]{:S(2)}, u32[]{:S(2)}) collective-permute-start(bf16[4,16,1024]{2,1,0:T(8,128)(2,1)S(1)} %gather_fusion), channel_id=1, source_target_pairs={{0,8},{8,0},{1,9},{9,1},{2,10},{10,2},{3,11},{11,3},{4,12},{12,4},... | collective-permute-start | bytes 393224 | tf_op jit(solution)/shard_map/ppermute | solution.py:118
  17.3 0.1 copy.87
  17.4 0.1 copy.79
  17.5 0.1 reshape.143
  17.6 5.9 %collective-permute-done = bf16[4,16,1024]{2,1,0:T(8,128)(2,1)S(1)} collective-permute-done((bf16[4,16,1024]{2,1,0:T(8,128)(2,1)S(1)}, bf16[4,16,1024]{2,1,0:T(8,128)(2,1)S(1)}, u32[]{:S(2)}, u32[]{:S(2)}) %collective-permute-start) | collective-permute-done | bytes 131104 | tf_op jit(solution)/shard_map/ppermute | solution.py:118
  23.6 0.1 broadcast_select_fusion
  23.7 1.4 %gather_fusion.1 = bf16[16,16,1024]{2,1,0:T(8,128)(2,1)} fusion(bf16[4,16,1024]{2,1,0:T(8,128)(2,1)S(1)} %broadcast_select_fusion, s32[1024]{0:T(1024)S(1)} %pad_clamp_fusion), kind=kCustom, calls=%fused_computation.1 | custom fusion | bytes 1048640 | tf_op jit(solution)/shard_map/gather | solution.py:121
  25.0 3.5 %all-to-all-start.1 = ((bf16[8,2,16,1024]{3,2,1,0:T(8,128)(2,1)}), bf16[8,2,16,1024]{3,2,1,0:T(8,128)(2,1)S(1)}, u32[]{:S(2)}, u32[]{:S(2)}) async-start(bf16[8,2,16,1024]{3,2,1,0:T(8,128)(2,1)} %bitcast.3), calls=%async_computation.1 | async-start | bytes 1048576 | tf_op jit(solution)/shard_map/all_to_all | solution.py:122
  28.5 0.0 copy-done.2
  28.6 0.7 %reshape.124.w_ref = f32[9,144]{1,0:T(8,128)} reshape(f32[9,9,16]{2,1,0:T(8,128)S(1)} %bitcast.53) | data formatting | bytes 10368 | tf_op jit(solution)/shard_map/reshape | solution.py:40
  29.3 6.9 %shard_map.244 = bf16[9,128,2048]{2,1,0:T(8,128)(2,1)} custom-call(f32[9,144]{1,0:T(8,128)} %reshape.124.w_ref), custom_call_target="tpu_custom_call" | custom-call | tf_op jit(solution)/shard_map/pallas_call | solution.py:41
  36.9 0.0 copy-done.1
  36.9 0.1 multiply_reduce_fusion.1
  37.0 0.0 copy-done
  37.0 0.1 broadcast_bitcast_fusion
  37.1 0.0 copy-done.3
  37.2 0.7 %copy.84.w_ref = f32[16,81]{1,0:T(8,128)} copy(f32[16,81]{0,1:T(8,128)S(1)} %reshape.126) | data formatting | bytes 10368 | tf_op jit(solution)/shard_map/reshape | solution.py:40
  37.8 8.6 %shard_map.245 = bf16[16,128,1152]{2,1,0:T(8,128)(2,1)} custom-call(f32[16,81]{1,0:T(8,128)} %copy.84.w_ref), custom_call_target="tpu_custom_call" | custom-call | tf_op jit(solution)/shard_map/pallas_call | solution.py:41
  46.4 0.0 all-to-all-done.1
  46.5 0.0 copy-start.4
  46.5 0.3 fusion.17
  46.8 0.0 copy-start.5
  46.8 0.1 copy.81
  46.9 0.2 multiply_reduce_fusion
  47.1 0.1 sqrt.19
  47.2 0.1 fusion.35
  47.3 0.0 copy-done.4
  47.4 0.1 fusion.20
  47.5 0.0 copy-done.5
  47.5 0.1 fusion.23
  47.6 0.1 fusion.25
  47.8 0.1 fusion.27
  47.9 0.1 fusion.29
  48.1 0.1 fusion.32
  48.2 9.6 %fusion = f32[4,128,1152]{2,1,0:T(8,128)S(1)} fusion(bf16[2048,1152,1]{1,0,2:T(8,128)(2,1)} %bitcast.50, bf16[4,128,1152]{2,1,0:T(8,128)(2,1)S(1)} %fusion.32, bf16[1152,2048,1]{1,0,2:T(8,128)(2,1)} %bitcast.49, f32[2048]{0:T(1024)S(1)} %broadcast_bitcast_fusion), kind=kOutput, calls=%fused_computation.4 | convolution fusion | flops 4834983936 | bytes 12984320 | tf_op jit(solution)/shard_map/vak,kn->van/dot_general | solution.py:83
  57.7 0.0 copy-start.6
  57.8 0.2 fusion.40
  58.0 0.4 copy-done.6
  58.4 0.3 fusion.11
  58.7 0.1 copy.88
  58.8 0.8 %copy.86 = f32[1,2,128,128]{3,2,1,0:T(8,128)} copy(f32[1,2,128,128]{2,3,1,0:T(8,128)S(1)} %fusion.34) | data formatting | bytes 262144 | tf_op jit(solution)/shard_map/broadcast_in_dim | solution.py:135
  (26 shorter events, 0.4 us)
Async XLA Ops:
  0.0 37.0 %copy-start = (f32[16]{0:T(128)S(1)}, f32[16]{0:T(128)}, u32[]{:S(2)}) copy-start(f32[16]{0:T(128)} %param.33) | copy-start | bytes 196
  0.0 7.7 %copy-start.7 = (s32[4]{0:T(128)S(1)}, s32[4]{0:T(128)}, u32[]{:S(2)}) copy-start(s32[4]{0:T(128)} %param.30) | copy-start | bytes 52
  2.4 11.7 %all-to-all-start = ((bf16[8,16,1152]{2,1,0:T(8,128)(2,1)}), bf16[8,16,1152]{2,1,0:T(8,128)(2,1)S(1)}, u32[]{:S(2)}, u32[]{:S(2)}) async-start(bf16[8,16,1152]{2,1,0:T(8,128)(2,1)} %pad_maximum_fusion), calls=%async_computation | async-start | bytes 589824 | tf_op jit(solution)/shard_map/all_to_all | solution.py:113
  14.7 8.9 %collective-permute-start = (bf16[4,16,1024]{2,1,0:T(8,128)(2,1)S(1)}, bf16[4,16,1024]{2,1,0:T(8,128)(2,1)S(1)}, u32[]{:S(2)}, u32[]{:S(2)}) collective-permute-start(bf16[4,16,1024]{2,1,0:T(8,128)(2,1)S(1)} %gather_fusion), channel_id=1, source_target_pairs={{0,8},{8,0},{1,9},{9,1},{2,10},{10,2},{3,11},{11,3},{4,12},{12,4},... | collective-permute-start | bytes 393224 | tf_op jit(solution)/shard_map/ppermute | solution.py:118
  17.6 10.9 %copy-start.2 = (bf16[16,1,3,3,3,3]{0,5,4,3,2,1:T(4,128)(2,1)S(1)}, bf16[16,1,3,3,3,3]{0,5,4,3,2,1:T(4,128)(2,1)}, u32[]{:S(2)}) copy-start(bf16[16,1,3,3,3,3]{0,5,4,3,2,1:T(4,128)(2,1)} %param.32) | copy-start | bytes 7780
  25.0 21.4 %all-to-all-start.1 = ((bf16[8,2,16,1024]{3,2,1,0:T(8,128)(2,1)}), bf16[8,2,16,1024]{3,2,1,0:T(8,128)(2,1)S(1)}, u32[]{:S(2)}, u32[]{:S(2)}) async-start(bf16[8,2,16,1024]{3,2,1,0:T(8,128)(2,1)} %bitcast.3), calls=%async_computation.1 | async-start | bytes 1048576 | tf_op jit(solution)/shard_map/all_to_all | solution.py:122
  29.3 7.6 %copy-start.1 = (bf16[128,1024]{1,0:T(8,128)(2,1)S(1)}, bf16[128,1024]{1,0:T(8,128)(2,1)}, u32[]{:S(2)}) copy-start(bf16[128,1024]{1,0:T(8,128)(2,1)} %param.28) | copy-start | bytes 786436
  29.3 7.8 %copy-start.3 = (bf16[1,16,3,3,3,3]{1,5,4,3,2,0:T(4,128)(2,1)S(1)}, bf16[1,16,3,3,3,3]{1,5,4,3,2,0:T(4,128)(2,1)}, u32[]{:S(2)}) copy-start(bf16[1,16,3,3,3,3]{1,5,4,3,2,0:T(4,128)(2,1)} %param.34) | copy-start | bytes 7780
  46.5 0.9 %copy-start.4 = (pred[128]{0:T(512)(128)(4,1)S(1)}, pred[128]{0:T(512)(128)(4,1)}, u32[]{:S(2)}) copy-start(pred[128]{0:T(512)(128)(4,1)} %constant.119) | copy-start | bytes 388
  46.8 0.7 %copy-start.5 = (pred[128]{0:T(512)(128)(4,1)S(1)}, pred[128]{0:T(512)(128)(4,1)}, u32[]{:S(2)}) copy-start(pred[128]{0:T(512)(128)(4,1)} %constant.120) | copy-start | bytes 388
  57.7 0.7 %copy-start.6 = (pred[128]{0:T(512)(128)(4,1)S(1)}, pred[128]{0:T(512)(128)(4,1)}, u32[]{:S(2)}) copy-start(pred[128]{0:T(512)(128)(4,1)} %constant.120) | copy-start | bytes 388

commit v10 on v9

--- a/solution.py
+++ b/solution.py
@@ -13,23 +13,17 @@
 TAPS = 9
 
 
-def band_kernel(w_ref, out_ref, *, groups):
-    r = pl.program_id(0)
+def band_kernel(wv_ref, out_ref, *, groups):
     cells = HQ * WQ
     row = lax.broadcasted_iota(jnp.int32, (WQ, cells), 0)
     lane = lax.broadcasted_iota(jnp.int32, (WQ, cells), 1)
     diff = row - lane % WQ + 1
     masks = [(diff == k).astype(jnp.float32) for k in range(3)]
-    block = lax.broadcasted_iota(jnp.int32, (1, cells), 1) // WQ
     for g in range(groups):
         for rb in range(HQ):
-            e1 = rb - block + 1
             total = None
             for k in range(3):
-                wv = jnp.zeros((1, cells), jnp.float32)
-                for j in range(3):
-                    wv = jnp.where(e1 == j, w_ref[r, (j * 3 + k) * groups + g], wv)
-                term = masks[k] * wv
+                term = masks[k] * wv_ref[0, rb, k, pl.ds(g, 1), :]
                 total = term if total is None else total + term
             out_ref[0, rb * WQ:(rb + 1) * WQ, g * cells:(g + 1) * cells] = total.astype(out_ref.dtype)
 
@@ -37,14 +31,18 @@
 def banded(weights):
     rows, _, groups = weights.shape
     cells = HQ * WQ
-    flat = weights.astype(jnp.float32).reshape(rows, TAPS * groups)
+    w = weights.astype(jnp.float32).reshape(rows, 3, 3, groups)
+    e1 = (np.arange(HQ)[:, None] - np.arange(cells)[None, :] // WQ + 1)[None, :, None, None, :]
+    wv = jnp.zeros((rows, HQ, 3, groups, cells), jnp.float32)
+    for j in range(3):
+        wv = jnp.where(e1 == j, w[:, None, j, :, :, None], wv)
     return pl.pallas_call(
         functools.partial(band_kernel, groups=groups),
         out_shape=jax.ShapeDtypeStruct((rows, cells, groups * cells), weights.dtype),
         grid=(rows,),
-        in_specs=[pl.BlockSpec(memory_space=pltpu.SMEM)],
+        in_specs=[pl.BlockSpec((1, HQ, 3, groups, cells), lambda r: (r, 0, 0, 0, 0))],
         out_specs=pl.BlockSpec((1, cells, groups * cells), lambda r: (r, 0, 0)),
-    )(flat)
+    )(wv)
 
 
 def band_weights(weight_first, weight_second, tie):

time: 60 us -> 58.9 us (0.982); the launches traced: 59.6 us -> 57.9 us
  waiting for transfers between devices: 12.3 us -> 6.72 us
  other arithmetic: 3.99 us -> 6.69 us
  Pallas kernels: 15.5 us -> 17.6 us
  local copies, waits for them, and re-layouts: 5.56 us -> 4.56 us
    all_to_all x1, waiting for transfers between devices: 6.34 us -> 0.01 us  [gather_sources(): arrived = lax.all_to_all(payload, 'sub', 0, 0)]
    select_n x0 -> x2, other arithmetic: none -> 2.72 us  [banded(): wv = jnp.where(e1 == j, w[:, None, j, :, :, None], wv)]
    pallas_call x2, Pallas kernels: 15.5 us -> 17.6 us  [banded(): pl.pallas_call(functools.partial(band_kernel, groups=groups), out_shape=j...]
    reshape x6 -> x4, local copies, waits for them, and re-layouts: 1.42 us -> 0.08 us  [banded(): w = weights.astype(jnp.float32).reshape(rows, 3, 3, groups)]
    ppermute x1, waiting for transfers between devices: 5.94 us -> 6.72 us  [gather_sources(): mirror = lax.ppermute(local, 'half', [(0, 1), (1, 0)])]
  transfers between devices with their start and end apart: 3 -> 3, of which waited for: 2 -> 1; matrix products, arithmetic and copies ran while one was open for 3% -> 6% of each run, Pallas kernels for 26% -> 30%
where the time goes in v10:
time: 58.9 us; the launch traced here: 57.9 us
  Pallas kernels  17.6 us (30%)
  starting transfers between devices  11.4 us (19%)
  matrix products  9.86 us (17%)
  waiting for transfers between devices  6.72 us (11%)
  other arithmetic  6.69 us (11%)
  local copies, waits for them, and re-layouts  4.56 us (8%)
  between operations  1.02 us (2%)
    pallas_call x2, Pallas kernels, banded(): pl.pallas_call(functools.partial(band_kernel, groups=groups), out_shape=j...  17.6 us
    dot_general x1, matrix products, consensus_stack(): jnp.einsum('vak,kn->van', hidden, k2, preferred_element_type=jnp.float32)  9.55 us
    ppermute x1, waiting for transfers between devices, gather_sources(): mirror = lax.ppermute(local, 'half', [(0, 1), (1, 0)])  6.72 us
    all_to_all x1, starting transfers between devices, gather_sources(): arrived = lax.all_to_all(payload, 'sub', 0, 0)  5.29 us
    all_to_all x1, starting transfers between devices, gather_sources(): got = lax.all_to_all(parcel, 'sub', 0, 0)  3.49 us
    select_n x2, other arithmetic, banded(): wv = jnp.where(e1 == j, w[:, None, j, :, :, None], wv)  2.72 us
    ppermute x1, starting transfers between devices, gather_sources(): mirror = lax.ppermute(local, 'half', [(0, 1), (1, 0)])  2.65 us
    concatenate x1, other arithmetic, gather_sources(): jnp.concatenate([source_maps.reshape(sub, rows, channels), tag], axis=2)  1.69 us
  transfers between devices with their start and end apart: 3, of which 1 were waited for; matrix products, arithmetic and copies ran while one was open for 6% of the time, Pallas kernels for 30%

profile of v10, /device:TPU:0, one launch (start us, length us, event | category | flops | bytes accessed | tf_op | source)
XLA Modules:
  0.0 57.9 jit_solution(1363953625560569945)
XLA Ops:
  0.0 0.0 copy-start
  0.0 0.7 %convert_element_type.58 = bf16[1,2]{1,0:T(2,128)(2,1)S(1)} convert(s32[1,2]{1,0:T(1,128)} %param.37) | non-fusion elementwise | flops 2 | bytes 12 | tf_op jit(solution)/shard_map/convert_element_type | solution.py:109
  0.7 0.0 copy-start.10
  0.7 1.7 %pad_maximum_fusion = bf16[8,16,1152]{2,1,0:T(8,128)(2,1)} fusion(bf16[8,16,128]{2,1,0:T(8,128)(2,1)S(1)} %scatter.8, bf16[8,16,1024]{2,1,0:T(8,128)(2,1)} %bitcast.65), kind=kLoop, calls=%fused_computation.16 | loop fusion | flops 589824 | bytes 589824 | tf_op jit(solution)/shard_map/concatenate | solution.py:110
  2.4 5.3 %all-to-all-start = ((bf16[8,16,1152]{2,1,0:T(8,128)(2,1)}), bf16[8,16,1152]{2,1,0:T(8,128)(2,1)S(1)}, u32[]{:S(2)}, u32[]{:S(2)}) async-start(bf16[8,16,1152]{2,1,0:T(8,128)(2,1)} %pad_maximum_fusion), calls=%async_computation | async-start | bytes 589824 | tf_op jit(solution)/shard_map/all_to_all | solution.py:111
  7.7 0.0 copy-done.2
  7.8 0.0 copy-done.7
  7.8 1.2 %select_select_fusion.1.wv_ref = f32[9,4,3,16,128]{4,3,2,1,0:T(8,128)} fusion(f32[9,3,16]{2,1,0:T(4,128)S(1)} %get-tuple-element.28, f32[9,3,16]{2,1,0:T(4,128)S(1)} %get-tuple-element.29, f32[9,3,16]{2,1,0:T(4,128)S(1)} %get-tuple-element.27, pred[4,128]{1,0:T(4,128)(4,1)S(1)} %copy-done.9, pred[4,128]{1,0:T(4,128)(4,1)S(1)} %copy-done.8, ...), kind=kLoop, calls=%fused_computation.5 | loop fusion | flops 663552 | bytes 891456 | tf_op jit(solution)/shard_map/jit(_where)/select_n | solution.py:38
  9.0 0.0 copy-start.1
  9.1 7.1 %shard_map.298 = bf16[9,128,2048]{2,1,0:T(8,128)(2,1)} custom-call(f32[9,4,3,16,128]{4,3,2,1,0:T(8,128)} %select_select_fusion.1.wv_ref), custom_call_target="tpu_custom_call" | custom-call | tf_op jit(solution)/shard_map/pallas_call | solution.py:39
  16.8 0.1 multiply_reduce_fusion.1
  17.0 0.0 all-to-all-done
  17.0 0.6 gather_fusion
  17.6 2.7 %collective-permute-start = (bf16[4,16,1024]{2,1,0:T(8,128)(2,1)S(1)}, bf16[4,16,1024]{2,1,0:T(8,128)(2,1)S(1)}, u32[]{:S(2)}, u32[]{:S(2)}) collective-permute-start(bf16[4,16,1024]{2,1,0:T(8,128)(2,1)S(1)} %gather_fusion), channel_id=1, source_target_pairs={{0,8},{8,0},{1,9},{9,1},{2,10},{10,2},{3,11},{11,3},{4,12},{12,4},... | collective-permute-start | bytes 393224 | tf_op jit(solution)/shard_map/ppermute | solution.py:116
  20.2 0.1 copy.98
  20.3 0.1 copy.89
  20.4 0.1 reshape.151
  20.5 6.7 %collective-permute-done = bf16[4,16,1024]{2,1,0:T(8,128)(2,1)S(1)} collective-permute-done((bf16[4,16,1024]{2,1,0:T(8,128)(2,1)S(1)}, bf16[4,16,1024]{2,1,0:T(8,128)(2,1)S(1)}, u32[]{:S(2)}, u32[]{:S(2)}) %collective-permute-start) | collective-permute-done | bytes 131104 | tf_op jit(solution)/shard_map/ppermute | solution.py:116
  27.2 0.1 broadcast_select_fusion
  27.3 1.4 %gather_fusion.1 = bf16[16,16,1024]{2,1,0:T(8,128)(2,1)} fusion(bf16[4,16,1024]{2,1,0:T(8,128)(2,1)S(1)} %broadcast_select_fusion, s32[1024]{0:T(1024)S(1)} %pad_clamp_fusion), kind=kCustom, calls=%fused_computation.1 | custom fusion | bytes 1048640 | tf_op jit(solution)/shard_map/gather | solution.py:119
  28.7 3.5 %all-to-all-start.1 = ((bf16[8,2,16,1024]{3,2,1,0:T(8,128)(2,1)}), bf16[8,2,16,1024]{3,2,1,0:T(8,128)(2,1)S(1)}, u32[]{:S(2)}, u32[]{:S(2)}) async-start(bf16[8,2,16,1024]{3,2,1,0:T(8,128)(2,1)} %bitcast.3), calls=%async_computation.1 | async-start | bytes 1048576 | tf_op jit(solution)/shard_map/all_to_all | solution.py:120
  32.2 0.1 broadcast_bitcast_fusion
  32.4 0.1 copy.93
  32.5 0.1 copy.94
  32.6 0.1 copy.95
  32.7 1.5 %select_select_fusion.wv_ref = f32[16,4,3,9,128]{4,3,2,1,0:T(8,128)} fusion(f32[16,3,9]{2,1,0:T(4,128)S(1)} %copy.95, f32[16,3,9]{2,1,0:T(4,128)S(1)} %copy.94, f32[16,3,9]{2,1,0:T(4,128)S(1)} %copy.93, pred[4,128]{1,0:T(4,128)(4,1)S(1)} %copy-done.9, pred[4,128]{1,0:T(4,128)(4,1)S(1)} %copy-done.8, pred[4,128]{1,0:T(4,128)(4,1)S(1)} %copy-done.7), kind=kLoop, calls=%fused_computation.3 | loop fusion | flops 663552 | bytes 891456 | tf_op jit(solution)/shard_map/jit(_where)/select_n | solution.py:38
  34.2 10.5 %shard_map.299 = bf16[16,128,1152]{2,1,0:T(8,128)(2,1)} custom-call(f32[16,4,3,9,128]{4,3,2,1,0:T(8,128)} %select_select_fusion.wv_ref), custom_call_target="tpu_custom_call" | custom-call | tf_op jit(solution)/shard_map/pallas_call | solution.py:39
  44.7 0.0 all-to-all-done.1
  44.7 0.0 copy-start.4
  44.7 0.3 fusion.17
  45.1 0.0 copy-start.5
  45.1 0.1 copy.91
  45.2 0.2 multiply_reduce_fusion
  45.4 0.1 sqrt.19
  45.5 0.1 fusion.35
  45.6 0.1 fusion.20
  45.8 0.1 fusion.23
  45.9 0.1 fusion.25
  46.1 0.1 fusion.27
  46.2 0.1 fusion.29
  46.4 0.1 fusion.32
  46.5 9.6 %fusion = f32[4,128,1152]{2,1,0:T(8,128)S(1)} fusion(bf16[2048,1152,1]{1,0,2:T(8,128)(2,1)} %bitcast.59, bf16[4,128,1152]{2,1,0:T(8,128)(2,1)S(1)} %fusion.32, bf16[1152,2048,1]{1,0,2:T(8,128)(2,1)} %bitcast.60, f32[2048]{0:T(1024)S(1)} %broadcast_bitcast_fusion), kind=kOutput, calls=%fused_computation.6 | convolution fusion | flops 4834983936 | bytes 12984320 | tf_op jit(solution)/shard_map/vak,kn->van/dot_general | solution.py:81
  56.0 0.0 copy-start.6
  56.0 0.2 fusion.40
  56.3 0.4 copy-done.6
  56.7 0.3 fusion.11
  57.0 0.1 copy.99
  57.1 0.8 %copy.97 = f32[1,2,128,128]{3,2,1,0:T(8,128)} copy(f32[1,2,128,128]{2,3,1,0:T(8,128)S(1)} %fusion.34) | data formatting | bytes 262144 | tf_op jit(solution)/shard_map/broadcast_in_dim | solution.py:133
  (37 shorter events, 0.4 us)
Async XLA Ops:
  0.0 32.2 %copy-start = (f32[16]{0:T(128)S(1)}, f32[16]{0:T(128)}, u32[]{:S(2)}) copy-start(f32[16]{0:T(128)} %param.39) | copy-start | bytes 196
  0.0 7.8 %copy-start.7 = (pred[4,128]{1,0:T(4,128)(4,1)S(1)}, pred[4,128]{1,0:T(4,128)(4,1)}, u32[]{:S(2)}) copy-start(pred[4,128]{1,0:T(4,128)(4,1)} %constant.132) | copy-start | bytes 1540
  0.0 7.8 %copy-start.8 = (pred[4,128]{1,0:T(4,128)(4,1)S(1)}, pred[4,128]{1,0:T(4,128)(4,1)}, u32[]{:S(2)}) copy-start(pred[4,128]{1,0:T(4,128)(4,1)} %constant.133) | copy-start | bytes 1540
  0.0 7.8 %copy-start.9 = (pred[4,128]{1,0:T(4,128)(4,1)S(1)}, pred[4,128]{1,0:T(4,128)(4,1)}, u32[]{:S(2)}) copy-start(pred[4,128]{1,0:T(4,128)(4,1)} %constant.134) | copy-start | bytes 1540
  0.0 7.7 %copy-start.2 = (bf16[16,1,3,3,3,3]{0,5,4,3,2,1:T(4,128)(2,1)S(1)}, bf16[16,1,3,3,3,3]{0,5,4,3,2,1:T(4,128)(2,1)}, u32[]{:S(2)}) copy-start(bf16[16,1,3,3,3,3]{0,5,4,3,2,1:T(4,128)(2,1)} %param.38) | copy-start | bytes 7780
  0.7 8.3 %copy-start.10 = (s32[4]{0:T(128)S(1)}, s32[4]{0:T(128)}, u32[]{:S(2)}) copy-start(s32[4]{0:T(128)} %param.36) | copy-start | bytes 52
  2.4 14.6 %all-to-all-start = ((bf16[8,16,1152]{2,1,0:T(8,128)(2,1)}), bf16[8,16,1152]{2,1,0:T(8,128)(2,1)S(1)}, u32[]{:S(2)}, u32[]{:S(2)}) async-start(bf16[8,16,1152]{2,1,0:T(8,128)(2,1)} %pad_maximum_fusion), calls=%async_computation | async-start | bytes 589824 | tf_op jit(solution)/shard_map/all_to_all | solution.py:111
  9.0 7.8 %copy-start.1 = (bf16[128,1024]{1,0:T(8,128)(2,1)S(1)}, bf16[128,1024]{1,0:T(8,128)(2,1)}, u32[]{:S(2)}) copy-start(bf16[128,1024]{1,0:T(8,128)(2,1)} %param.34) | copy-start | bytes 786436
  17.6 9.7 %collective-permute-start = (bf16[4,16,1024]{2,1,0:T(8,128)(2,1)S(1)}, bf16[4,16,1024]{2,1,0:T(8,128)(2,1)S(1)}, u32[]{:S(2)}, u32[]{:S(2)}) collective-permute-start(bf16[4,16,1024]{2,1,0:T(8,128)(2,1)S(1)} %gather_fusion), channel_id=1, source_target_pairs={{0,8},{8,0},{1,9},{9,1},{2,10},{10,2},{3,11},{11,3},{4,12},{12,4},... | collective-permute-start | bytes 393224 | tf_op jit(solution)/shard_map/ppermute | solution.py:116
  20.5 11.8 %copy-start.3 = (bf16[1,16,3,3,3,3]{1,5,4,3,2,0:T(4,128)(2,1)S(1)}, bf16[1,16,3,3,3,3]{1,5,4,3,2,0:T(4,128)(2,1)}, u32[]{:S(2)}) copy-start(bf16[1,16,3,3,3,3]{1,5,4,3,2,0:T(4,128)(2,1)} %param.40) | copy-start | bytes 7780
  28.7 16.0 %all-to-all-start.1 = ((bf16[8,2,16,1024]{3,2,1,0:T(8,128)(2,1)}), bf16[8,2,16,1024]{3,2,1,0:T(8,128)(2,1)S(1)}, u32[]{:S(2)}, u32[]{:S(2)}) async-start(bf16[8,2,16,1024]{3,2,1,0:T(8,128)(2,1)} %bitcast.3), calls=%async_computation.1 | async-start | bytes 1048576 | tf_op jit(solution)/shard_map/all_to_all | solution.py:120
  44.7 0.9 %copy-start.4 = (pred[128]{0:T(512)(128)(4,1)S(1)}, pred[128]{0:T(512)(128)(4,1)}, u32[]{:S(2)}) copy-start(pred[128]{0:T(512)(128)(4,1)} %constant.130) | copy-start | bytes 388
  45.1 0.7 %copy-start.5 = (pred[128]{0:T(512)(128)(4,1)S(1)}, pred[128]{0:T(512)(128)(4,1)}, u32[]{:S(2)}) copy-start(pred[128]{0:T(512)(128)(4,1)} %constant.131) | copy-start | bytes 388
  56.0 0.7 %copy-start.6 = (pred[128]{0:T(512)(128)(4,1)S(1)}, pred[128]{0:T(512)(128)(4,1)}, u32[]{:S(2)}) copy-start(pred[128]{0:T(512)(128)(4,1)} %constant.131) | copy-start | bytes 388

commit v11 on v6

--- a/solution.py
+++ b/solution.py
@@ -104,17 +104,17 @@
     named = jnp.where(here, local, mirror)
     parcel = named[picks]
     got = lax.all_to_all(parcel, "sub", 0, 0)
-    return jnp.swapaxes(got, 0, 1).reshape(2, cells, channels), parcel
+    return jnp.swapaxes(got, 0, 1).reshape(2, cells, channels), local
 
 
 def per_device(
     query_maps, source_maps, hubs, pick, weight_first, bias_first, weight_second, bias_second,
     sub,
 ):
-    chosen, parcel = gather_sources(source_maps, hubs, pick, sub)
+    chosen, local = gather_sources(source_maps, hubs, pick, sub)
     correlation = scaled_corr(query_maps, chosen)
     volumes = jnp.concatenate([correlation, jnp.swapaxes(correlation, 1, 2)], axis=0)
-    k1, k2 = band_weights(weight_first, weight_second, parcel)
+    k1, k2 = band_weights(weight_first, weight_second, local)
     filtered = consensus_stack(volumes, k1, k2, bias_first, bias_second)
     return (filtered[:2] + jnp.swapaxes(filtered[2:], 1, 2))[None]
 

time: 57.8 us -> 57.6 us (level)
    ppermute x1, waiting for transfers between devices: 6.73 us -> 5.14 us  [gather_sources(): mirror = lax.ppermute(local, 'half', [(0, 1), (1, 0)])]
    all_to_all x1, waiting for transfers between devices: 0.01 us -> 1.32 us  [gather_sources(): got = lax.all_to_all(parcel, 'sub', 0, 0)]
  transfers between devices with their start and end apart: 3 -> 3, of which waited for: 1 -> 2; matrix products, arithmetic and copies ran while one was open for 36% -> 36% of each run, Pallas kernels for 0% -> 0%
where the time goes in v11:
time: 57.6 us; the launch traced here: 57.1 us
  other arithmetic  22 us (38%)
  starting transfers between devices  11.6 us (20%)
  matrix products  9.86 us (17%)
  waiting for transfers between devices  6.47 us (11%)
  local copies, waits for them, and re-layouts  6.13 us (11%)
  between operations  1.05 us (2%)
    select_n x2, other arithmetic, banded(): band = jnp.where(table[None] == e, spread_w[:, e, None, :], band)  14.5 us
    dot_general x1, matrix products, consensus_stack(): jnp.einsum('vak,kn->van', hidden, k2, preferred_element_type=jnp.float32)  9.55 us
    all_to_all x1, starting transfers between devices, gather_sources(): arrived = lax.all_to_all(payload, 'sub', 0, 0)  5.29 us
    ppermute x1, waiting for transfers between devices, gather_sources(): mirror = lax.ppermute(local, 'half', [(0, 1), (1, 0)])  5.14 us
    all_to_all x1, starting transfers between devices, gather_sources(): got = lax.all_to_all(parcel, 'sub', 0, 0)  3.67 us
    eq x2, other arithmetic, banded(): band = jnp.where(table[None] == e, spread_w[:, e, None, :], band)  3.1 us
    ppermute x1, starting transfers between devices, gather_sources(): mirror = lax.ppermute(local, 'half', [(0, 1), (1, 0)])  2.65 us
    concatenate x1, other arithmetic, gather_sources(): jnp.concatenate([source_maps.reshape(sub, rows, channels), tag], axis=2)  1.69 us
  transfers between devices with their start and end apart: 3, of which 2 were waited for; matrix products, arithmetic and copies ran while one was open for 36% of the time, Pallas kernels for 0%

profile of v11, /device:TPU:0, one launch (start us, length us, event | category | flops | bytes accessed | tf_op | source)
XLA Modules:
  0.0 57.1 jit_solution(12134330745049463043)
XLA Ops:
  0.0 0.0 copy-start
  0.0 0.7 %convert_element_type.44 = bf16[1,2]{1,0:T(2,128)(2,1)S(1)} convert(s32[1,2]{1,0:T(1,128)} %param.31) | non-fusion elementwise | flops 2 | bytes 12 | tf_op jit(solution)/shard_map/convert_element_type | solution.py:95
  0.7 1.7 %pad_maximum_fusion = bf16[8,16,1152]{2,1,0:T(8,128)(2,1)} fusion(bf16[8,16,128]{2,1,0:T(8,128)(2,1)S(1)} %scatter.8, bf16[8,16,1024]{2,1,0:T(8,128)(2,1)} %bitcast.91), kind=kLoop, calls=%fused_computation.59 | loop fusion | flops 589824 | bytes 589824 | tf_op jit(solution)/shard_map/concatenate | solution.py:96
  2.4 5.3 %all-to-all-start = ((bf16[8,16,1152]{2,1,0:T(8,128)(2,1)}), bf16[8,16,1152]{2,1,0:T(8,128)(2,1)S(1)}, u32[]{:S(2)}, u32[]{:S(2)}) async-start(bf16[8,16,1152]{2,1,0:T(8,128)(2,1)} %pad_maximum_fusion), calls=%async_computation | async-start | bytes 589824 | tf_op jit(solution)/shard_map/all_to_all | solution.py:97
  7.8 0.8 %reshape.1187 = bf16[16,9,9]{0,2,1:T(8,128)(2,1)S(1)} reshape(bf16[16,1,3,3,3,3]{0,5,4,3,2,1:T(4,128)(2,1)} %param.32) | data formatting | bytes 5184 | tf_op jit(solution)/shard_map/reshape | solution.py:33
  8.6 0.2 broadcast_in_dim.508
  8.8 0.2 reshape.1188
  9.1 0.0 copy-done.6
  9.1 0.0 copy-done.1
  9.1 0.1 multiply_reduce_fusion.1
  9.3 0.1 broadcast_bitcast_fusion
  9.3 2.3 %broadcast_compare_fusion.4 = (pred[128,2048]{1,0:T(8,128)(4,1)S(1)}, pred[128,2048]{1,0:T(8,128)(4,1)S(1)}, pred[128,2048]{1,0:T(8,128)(4,1)S(1)}, pred[128,204...) fusion(s32[128]{0:T(128)S(1)} %get-tuple-element.72, ...), kind=kLoop, calls=%fused_computation.45 | loop fusion | flops 11796480 | bytes 2380032 | tf_op jit(solution)/shard_map/eq | solution.py:26
  11.7 7.2 %select_select_fusion.1 = bf16[9,128,2048]{2,1,0:T(8,128)(2,1)} fusion(pred[128,2048]{1,0:T(8,128)(4,1)S(1)} %get-tuple-element.61, pred[128,2048]{1,0:T(8,128)(4,1)S(1)} %get-tuple-element.60, pred[128,2048]{1,0:T(8,128)(4,1)S(1)} %get-tuple-element.59, pred[128,2048]{1,0:T(8,128)(4,1)S(1)} %get-tuple-element.58, ...), kind=kLoop, calls=%fused_computation.3 | loop fusion | flops 21233664 | bytes 7409664 | tf_op jit(solution)/shard_map/jit(_where)/select_n | solution.py:26
  19.5 0.4 add_select_fusion.5
  19.9 0.0 all-to-all-done
  20.0 0.6 gather_fusion
  20.5 2.7 %collective-permute-start = (bf16[4,16,1024]{2,1,0:T(8,128)(2,1)S(1)}, bf16[4,16,1024]{2,1,0:T(8,128)(2,1)S(1)}, u32[]{:S(2)}, u32[]{:S(2)}) collective-permute-start(bf16[4,16,1024]{2,1,0:T(8,128)(2,1)S(1)} %gather_fusion), channel_id=1, source_target_pairs={{0,8},{8,0},{1,9},{9,1},{2,10},{10,2},{3,11},{11,3},{4,12},{12,4},... | collective-permute-start | bytes 393224 | tf_op jit(solution)/shard_map/ppermute | solution.py:102
  23.2 0.1 copy.88
  23.3 0.8 %broadcast_compare_fusion.13 = (pred[128,1152]{1,0:T(8,128)(4,1)S(1)}, pred[128,1152]{1,0:T(8,128)(4,1)S(1)}, pred[128,1152]{1,0:T(8,128)(4,1)S(1)}, pred[128,11...) fusion(s32[128,1152]{1,0:T(8,128)S(1)} %add_select_fusion.5), kind=kLoop, calls=%fused_computation.64 | loop fusion | flops 1327104 | bytes 1916928 | tf_op jit(solution)/shard_map/eq | solution.py:26
  24.1 0.1 copy.85
  24.3 0.4 broadcast_in_dim.548
  24.6 0.2 reshape.1190
  24.9 0.1 copy.80
  25.0 0.1 reshape.1210
  25.1 5.1 %collective-permute-done = bf16[4,16,1024]{2,1,0:T(8,128)(2,1)S(1)} collective-permute-done((bf16[4,16,1024]{2,1,0:T(8,128)(2,1)S(1)}, bf16[4,16,1024]{2,1,0:T(8,128)(2,1)S(1)}, u32[]{:S(2)}, u32[]{:S(2)}) %collective-permute-start) | collective-permute-done | bytes 131104 | tf_op jit(solution)/shard_map/ppermute | solution.py:102
  30.2 0.1 broadcast_select_fusion
  30.3 1.4 %gather_fusion.1 = bf16[16,16,1024]{2,1,0:T(8,128)(2,1)} fusion(bf16[4,16,1024]{2,1,0:T(8,128)(2,1)S(1)} %broadcast_select_fusion, s32[1024]{0:T(1024)S(1)} %pad_clamp_fusion), kind=kCustom, calls=%fused_computation.1 | custom fusion | bytes 1048640 | tf_op jit(solution)/shard_map/gather | solution.py:105
  31.7 3.7 %all-to-all-start.1 = ((bf16[8,2,16,1024]{3,2,1,0:T(8,128)(2,1)}), bf16[8,2,16,1024]{3,2,1,0:T(8,128)(2,1)S(1)}, u32[]{:S(2)}, u32[]{:S(2)}) async-start(bf16[8,2,16,1024]{3,2,1,0:T(8,128)(2,1)} %bitcast.3), calls=%async_computation.1 | async-start | bytes 1048576 | tf_op jit(solution)/shard_map/all_to_all | solution.py:106
  35.4 7.3 %select_select_fusion = bf16[16,128,1152]{2,1,0:T(8,128)(2,1)} fusion(pred[128,1152]{1,0:T(8,128)(4,1)S(1)} %get-tuple-element.39, pred[128,1152]{1,0:T(8,128)(4,1)S(1)} %get-tuple-element.40, pred[128,1152]{1,0:T(8,128)(4,1)S(1)} %get-tuple-element.41, pred[128,1152]{1,0:T(8,128)(4,1)S(1)} %get-tuple-element.42, pred[128,1152]{1,0:T(8,128)(4,1)S(1)} %get-tuple-element.43, ...), kind=kLoop, calls=%fused_computation.2 | loop fusion | flops 21233664 | bytes 6377472 | tf_op jit(solution)/shard_map/jit(_where)/select_n | solution.py:26
  42.6 1.3 %all-to-all-done.1 = bf16[8,2,16,1024]{3,2,1,0:T(8,128)(2,1)S(1)} async-done(((bf16[8,2,16,1024]{3,2,1,0:T(8,128)(2,1)}), bf16[8,2,16,1024]{3,2,1,0:T(8,128)(2,1)S(1)}, u32[]{:S(2)}, u32[]{:S(2)}) %all-to-all-start.1) | async-done | bytes 524320 | tf_op jit(solution)/shard_map/all_to_all | solution.py:106
  44.0 0.3 fusion.33
  44.3 0.1 copy.82
  44.4 0.2 multiply_reduce_fusion
  44.6 0.1 sqrt.19
  44.7 0.1 fusion.51
  44.9 0.1 fusion.36
  45.0 0.1 fusion.39
  45.1 0.1 fusion.41
  45.3 0.1 fusion.43
  45.4 0.1 fusion.45
  45.6 0.1 fusion.48
  45.7 9.6 %fusion.8 = f32[4,128,1152]{2,1,0:T(8,128)S(1)} fusion(bf16[2048,1152,1]{1,0,2:T(8,128)(2,1)} %bitcast.87, bf16[4,128,1152]{2,1,0:T(8,128)(2,1)S(1)} %fusion.48, bf16[1152,2048,1]{1,0,2:T(8,128)(2,1)} %bitcast.89, f32[2048]{0:T(1024)S(1)} %broadcast_bitcast_fusion), kind=kOutput, calls=%fused_computation.31 | convolution fusion | flops 4834983936 | bytes 12984320 | tf_op jit(solution)/shard_map/vak,kn->van/dot_general | solution.py:67
  55.3 0.0 copy-start.5
  55.3 0.2 fusion.64
  55.5 0.4 copy-done.5
  55.9 0.3 fusion.27
  56.2 0.1 copy.89
  56.4 0.8 %copy.87 = f32[1,2,128,128]{3,2,1,0:T(8,128)} copy(f32[1,2,128,128]{2,3,1,0:T(8,128)S(1)} %fusion.50) | data formatting | bytes 262144 | tf_op jit(solution)/shard_map/broadcast_in_dim | solution.py:119
  (38 shorter events, 0.5 us)
Async XLA Ops:
  0.0 9.3 %copy-start = (f32[16]{0:T(128)S(1)}, f32[16]{0:T(128)}, u32[]{:S(2)}) copy-start(f32[16]{0:T(128)} %param.33) | copy-start | bytes 196
  0.0 9.1 %copy-start.6 = (s32[4]{0:T(128)S(1)}, s32[4]{0:T(128)}, u32[]{:S(2)}) copy-start(s32[4]{0:T(128)} %param.30) | copy-start | bytes 52
  0.0 9.1 %copy-start.1 = (bf16[128,1024]{1,0:T(8,128)(2,1)S(1)}, bf16[128,1024]{1,0:T(8,128)(2,1)}, u32[]{:S(2)}) copy-start(bf16[128,1024]{1,0:T(8,128)(2,1)} %param.28) | copy-start | bytes 786436
  2.4 17.5 %all-to-all-start = ((bf16[8,16,1152]{2,1,0:T(8,128)(2,1)}), bf16[8,16,1152]{2,1,0:T(8,128)(2,1)S(1)}, u32[]{:S(2)}, u32[]{:S(2)}) async-start(bf16[8,16,1152]{2,1,0:T(8,128)(2,1)} %pad_maximum_fusion), calls=%async_computation | async-start | bytes 589824 | tf_op jit(solution)/shard_map/all_to_all | solution.py:97
  18.8 5.2 %copy-start.2 = (bf16[1,16,3,3,3,3]{1,5,4,3,2,0:T(4,128)(2,1)S(1)}, bf16[1,16,3,3,3,3]{1,5,4,3,2,0:T(4,128)(2,1)}, u32[]{:S(2)}) copy-start(bf16[1,16,3,3,3,3]{1,5,4,3,2,0:T(4,128)(2,1)} %param.34) | copy-start | bytes 7780
  20.5 9.7 %collective-permute-start = (bf16[4,16,1024]{2,1,0:T(8,128)(2,1)S(1)}, bf16[4,16,1024]{2,1,0:T(8,128)(2,1)S(1)}, u32[]{:S(2)}, u32[]{:S(2)}) collective-permute-start(bf16[4,16,1024]{2,1,0:T(8,128)(2,1)S(1)} %gather_fusion), channel_id=1, source_target_pairs={{0,8},{8,0},{1,9},{9,1},{2,10},{10,2},{3,11},{11,3},{4,12},{12,4},... | collective-permute-start | bytes 393224 | tf_op jit(solution)/shard_map/ppermute | solution.py:102
  31.7 12.3 %all-to-all-start.1 = ((bf16[8,2,16,1024]{3,2,1,0:T(8,128)(2,1)}), bf16[8,2,16,1024]{3,2,1,0:T(8,128)(2,1)S(1)}, u32[]{:S(2)}, u32[]{:S(2)}) async-start(bf16[8,2,16,1024]{3,2,1,0:T(8,128)(2,1)} %bitcast.3), calls=%async_computation.1 | async-start | bytes 1048576 | tf_op jit(solution)/shard_map/all_to_all | solution.py:106
  42.6 2.2 %copy-start.3 = (pred[128]{0:T(512)(128)(4,1)S(1)}, pred[128]{0:T(512)(128)(4,1)}, u32[]{:S(2)}) copy-start(pred[128]{0:T(512)(128)(4,1)} %constant.239) | copy-start | bytes 388
  42.6 2.4 %copy-start.4 = (pred[128]{0:T(512)(128)(4,1)S(1)}, pred[128]{0:T(512)(128)(4,1)}, u32[]{:S(2)}) copy-start(pred[128]{0:T(512)(128)(4,1)} %constant.240) | copy-start | bytes 388
  55.3 0.7 %copy-start.5 = (pred[128]{0:T(512)(128)(4,1)S(1)}, pred[128]{0:T(512)(128)(4,1)}, u32[]{:S(2)}) copy-start(pred[128]{0:T(512)(128)(4,1)} %constant.240) | copy-start | bytes 388

commit v12 on v11

--- a/solution.py
+++ b/solution.py
@@ -30,16 +30,17 @@
 def band_weights(weight_first, weight_second, tie):
     hid = weight_first.shape[0]
     cells = HQ * WQ
-    w1 = weight_first.reshape(hid, TAPS, TAPS)
-    k1 = banded(jnp.transpose(w1, (1, 2, 0)), tap_table(cells, hid * cells), cells)
-    k1 = k1.reshape(TAPS * cells, hid * cells)
-    table, weight_second, _ = lax.optimization_barrier(
-        (tap_table(cells, TAPS * cells), weight_second, tie)
-    )
+    split = 5
+    w1 = jnp.transpose(weight_first.reshape(hid, TAPS, TAPS), (1, 2, 0))
+    k1a = banded(w1[:split], tap_table(cells, hid * cells), cells)
+    k1a = k1a.reshape(split * cells, hid * cells)
+    late_w1, weight_second, _ = lax.optimization_barrier((w1[split:], weight_second, tie))
+    k1b = banded(late_w1, tap_table(cells, hid * cells), cells)
+    k1b = k1b.reshape((TAPS - split) * cells, hid * cells)
     w2 = weight_second.reshape(hid, TAPS, TAPS)
-    k2 = banded(jnp.transpose(w2, (0, 2, 1)), table, cells)
+    k2 = banded(jnp.transpose(w2, (0, 2, 1)), tap_table(cells, TAPS * cells), cells)
     k2 = k2.reshape(hid * cells, TAPS * cells)
-    return k1, k2
+    return (k1a, k1b), k2
 
 
 def row_shifts(x):
@@ -61,7 +62,12 @@
     cells = volumes.shape[1]
     hid = bias_first.shape[0]
     stacked = jnp.concatenate(row_shifts(volumes), axis=-1)
-    pre = jnp.einsum("vak,kn->van", stacked, k1, preferred_element_type=jnp.float32)
+    k1a, k1b = k1
+    cut = k1a.shape[0]
+    pre = jnp.einsum("vak,kn->van", stacked[..., :cut], k1a, preferred_element_type=jnp.float32)
+    pre = pre + jnp.einsum(
+        "vak,kn->van", stacked[..., cut:], k1b, preferred_element_type=jnp.float32
+    )
     pre = pre + jnp.repeat(bias_first, cells)[None, None, :]
     hidden = jax.nn.relu(pre).astype(jnp.bfloat16)
     part = jnp.einsum("vak,kn->van", hidden, k2, preferred_element_type=jnp.float32)

time: 57.6 us -> 67.8 us (1.18)
  other arithmetic: 22 us -> 26.6 us
  local copies, waits for them, and re-layouts: 6.13 us -> 10.5 us
  matrix products: 9.86 us -> 13.5 us
  waiting for transfers between devices: 6.47 us -> 3.18 us
    ppermute x1, waiting for transfers between devices: 5.14 us -> 0.01 us  [gather_sources(): mirror = lax.ppermute(local, 'half', [(0, 1), (1, 0)])]
    dot_general x0 -> x1, matrix products: none -> 3.83 us  [consensus_stack(): jnp.einsum('vak,kn->van', stacked[..., :cut], k1a, preferred_element_type...]
    all_to_all x1, waiting for transfers between devices: 1.32 us -> 3.18 us  [gather_sources(): got = lax.all_to_all(parcel, 'sub', 0, 0)]
    broadcast_in_dim x2 -> x3, local copies, waits for them, and re-layouts: 0.08 us -> 1.87 us  [banded(): band = jnp.where(table[None] == e, spread_w[:, e, None, :], band)]
    select_n x2 -> x3, other arithmetic: 14.5 us -> 16.1 us  [banded(): band = jnp.where(table[None] == e, spread_w[:, e, None, :], band)]
    reshape x2 -> x3, local copies, waits for them, and re-layouts: 0.36 us -> 1.82 us  [banded(): spread_w = jnp.repeat(weights, cells, axis=2)]
    eq x2, other arithmetic: 3.1 us -> 4.53 us  [banded(): band = jnp.where(table[None] == e, spread_w[:, e, None, :], band)]
    dot_general x1, matrix products: 9.55 us -> 8.36 us  [consensus_stack(): jnp.einsum('vak,kn->van', hidden, k2, preferred_element_type=jnp.float32)]
  transfers between devices with their start and end apart: 3 -> 3, of which waited for: 2 -> 1; matrix products, arithmetic and copies ran while one was open for 36% -> 42% of each run, Pallas kernels for 0% -> 0%
where the time goes in v12:
time: 67.8 us; the launch traced here: 67 us
  other arithmetic  26.6 us (39%)
  matrix products  13.5 us (20%)
  starting transfers between devices  12.1 us (18%)
  local copies, waits for them, and re-layouts  10.5 us (15%)
  waiting for transfers between devices  3.18 us (5%)
  between operations  1.28 us (2%)
    select_n x3, other arithmetic, banded(): band = jnp.where(table[None] == e, spread_w[:, e, None, :], band)  16.1 us
    dot_general x1, matrix products, consensus_stack(): jnp.einsum('vak,kn->van', hidden, k2, preferred_element_type=jnp.float32)  8.36 us
    all_to_all x1, starting transfers between devices, gather_sources(): arrived = lax.all_to_all(payload, 'sub', 0, 0)  5.29 us
    eq x2, other arithmetic, banded(): band = jnp.where(table[None] == e, spread_w[:, e, None, :], band)  4.53 us
    all_to_all x1, starting transfers between devices, gather_sources(): got = lax.all_to_all(parcel, 'sub', 0, 0)  4.2 us
    dot_general x1, matrix products, consensus_stack(): jnp.einsum('vak,kn->van', stacked[..., :cut], k1a, preferred_element_type...  3.83 us
    all_to_all x1, waiting for transfers between devices, gather_sources(): got = lax.all_to_all(parcel, 'sub', 0, 0)  3.18 us
    ppermute x1, starting transfers between devices, gather_sources(): mirror = lax.ppermute(local, 'half', [(0, 1), (1, 0)])  2.59 us
  transfers between devices with their start and end apart: 3, of which 1 were waited for; matrix products, arithmetic and copies ran while one was open for 42% of the time, Pallas kernels for 0%

profile of v12, /device:TPU:0, one launch (start us, length us, event | category | flops | bytes accessed | tf_op | source)
XLA Modules:
  0.0 67.0 jit_solution(18071059426569097920)
XLA Ops:
  0.0 0.7 %convert_element_type.44 = bf16[1,2]{1,0:T(2,128)(2,1)S(1)} convert(s32[1,2]{1,0:T(1,128)} %param.31) | non-fusion elementwise | flops 2 | bytes 12 | tf_op jit(solution)/shard_map/convert_element_type | solution.py:101
  0.7 1.7 %pad_maximum_fusion = bf16[8,16,1152]{2,1,0:T(8,128)(2,1)} fusion(bf16[8,16,128]{2,1,0:T(8,128)(2,1)S(1)} %scatter.8, bf16[8,16,1024]{2,1,0:T(8,128)(2,1)} %bitcast.119), kind=kLoop, calls=%fused_computation.67 | loop fusion | flops 589824 | bytes 589824 | tf_op jit(solution)/shard_map/concatenate | solution.py:102
  2.4 5.3 %all-to-all-start = ((bf16[8,16,1152]{2,1,0:T(8,128)(2,1)}), bf16[8,16,1152]{2,1,0:T(8,128)(2,1)S(1)}, u32[]{:S(2)}, u32[]{:S(2)}) async-start(bf16[8,16,1152]{2,1,0:T(8,128)(2,1)} %pad_maximum_fusion), calls=%async_computation | async-start | bytes 589824 | tf_op jit(solution)/shard_map/all_to_all | solution.py:103
  7.7 0.0 copy-start.14
  7.8 0.8 %reshape.2211 = bf16[16,9,9]{0,2,1:T(8,128)(2,1)S(1)} reshape(bf16[16,1,3,3,3,3]{0,5,4,3,2,1:T(4,128)(2,1)} %param.32) | data formatting | bytes 5184 | tf_op jit(solution)/shard_map/reshape | solution.py:34
  8.6 0.7 compare_select_fusion.1
  9.3 0.2 broadcast_in_dim.650
  9.5 0.2 reshape.2212
  9.8 0.6 fusion.72
  10.4 0.1 multiply_reduce_fusion.1
  10.5 0.1 broadcast_bitcast_fusion
  11.2 2.3 %broadcast_compare_fusion.4 = (pred[128,2048]{1,0:T(8,128)(4,1)S(1)}, pred[128,2048]{1,0:T(8,128)(4,1)S(1)}, pred[128,2048]{1,0:T(8,128)(4,1)S(1)}, pred[128,204...) fusion(s32[128]{0:T(128)S(1)} %get-tuple-element.87, ...), kind=kLoop, calls=%fused_computation.53 | loop fusion | flops 11796480 | bytes 2380032 | tf_op jit(solution)/shard_map/eq | solution.py:26
  13.7 0.0 copy-start.15
  13.7 3.1 %select_select_fusion.1 = bf16[5,128,2048]{2,1,0:T(8,128)(2,1)S(1)} fusion(pred[128,2048]{1,0:T(8,128)(4,1)S(1)} %get-tuple-element.70, pred[128,2048]{1,0:T(8,128)(4,1)S(1)} %get-tuple-element.69, pred[128,2048]{1,0:T(8,128)(4,1)S(1)} %get-tuple-element.68, pred[128,2048]{1,0:T(8,128)(4,1)S(1)} %get-tuple-element.67, ...), kind=kLoop, calls=%fused_computation.4 | loop fusion | flops 11796480 | bytes 5165056 | tf_op jit(solution)/shard_map/jit(_where)/select_n | solution.py:26
  16.9 2.3 %broadcast_compare_fusion.13 = (pred[128,1152]{1,0:T(8,128)(4,1)}, pred[128,1152]{1,0:T(8,128)(4,1)}, pred[128,1152]{1,0:T(8,128)(4,1)}, pred[128,1152]{1,0:T(8,...) fusion(s32[128]{0:T(128)S(1)} %copy-done.15, ...), kind=kLoop, calls=%fused_computation.72 | loop fusion | flops 6635520 | bytes 1339776 | tf_op jit(solution)/shard_map/eq | solution.py:26
  19.2 1.2 %gather_fusion = bf16[4,16,1024]{2,1,0:T(8,128)(2,1)} fusion(bf16[8,16,1024]{2,1,0:T(8,128)(2,1)S(1)} %slice.265, s32[1024]{0:T(1024)S(1)} %pad_clamp_fusion.1), kind=kCustom, calls=%fused_computation | custom fusion | bytes 262160 | tf_op jit(solution)/shard_map/gather | solution.py:107
  20.4 2.6 %collective-permute-start = (bf16[4,16,1024]{2,1,0:T(8,128)(2,1)}, bf16[4,16,1024]{2,1,0:T(8,128)(2,1)}, u32[]{:S(2)}, u32[]{:S(2)}) collective-permute-start(bf16[4,16,1024]{2,1,0:T(8,128)(2,1)} %gather_fusion), channel_id=1, source_target_pairs={{0,8},{8,0},{1,9},{9,1},{2,10},{10,2},{3,11},{11,3},{4,12},{12,4},... | collective-permute-start | bytes 393224 | tf_op jit(solution)/shard_map/ppermute | solution.py:108
  23.0 0.1 copy.95
  23.1 0.8 %reshape.2214 = bf16[16,9,9]{0,2,1:T(8,128)(2,1)S(1)} reshape(bf16[1,16,3,3,3,3]{1,5,4,3,2,0:T(4,128)(2,1)} %param.34) | data formatting | bytes 5184 | tf_op jit(solution)/shard_map/reshape | solution.py:40
  23.9 0.1 copy.92
  24.0 0.4 broadcast_in_dim.737
  24.4 0.9 %reshape.2215 = bf16[16,9,1152]{2,0,1:T(8,128)(2,1)} reshape(bf16[16,9,9,128]{3,2,0,1:T(8,128)(2,1)S(1)} %broadcast_in_dim.737) | data formatting | bytes 663552 | tf_op jit(solution)/shard_map/reshape | solution.py:23
  25.3 0.9 %slice_bitcast_fusion.9 = (bf16[16,1152]{1,0:T(8,128)(2,1)S(1)}, bf16[16,1152]{1,0:T(8,128)(2,1)S(1)}, bf16[16,1152]{1,0:T(8,128)(2,1)S(1)}, bf16[16,1152]{1,0:T...) fusion(bf16[16,9,1152]{2,0,1:T(8,128)(2,1)} %reshape.2215), kind=kLoop, calls=%fused_computation.129 | loop fusion | bytes 663552 | tf_op jit(solution)/shard_map/jit(_where)/broadcast_in_dim | solution.py:26
  26.3 8.2 %select_select_fusion = bf16[16,128,1152]{2,1,0:T(8,128)(2,1)} fusion(pred[128,1152]{1,0:T(8,128)(4,1)} %get-tuple-element.76, pred[128,1152]{1,0:T(8,128)(4,1)} %get-tuple-element.75, pred[128,1152]{1,0:T(8,128)(4,1)} %get-tuple-element.74, pred[128,1152]{1,0:T(8,128)(4,1)} %get-tuple-element.73, pred[128,1152]{1,0:T(8,128)(4,1)} %get-tuple-element.72, ...), kind=kLoop, calls=%fused_computation.2 | loop fusion | flops 21233664 | bytes 6377472 | tf_op jit(solution)/shard_map/jit(_where)/select_n | solution.py:26
  34.5 0.1 broadcast_in_dim.697
  34.7 0.7 %reshape.2213 = bf16[4,9,2048]{2,0,1:T(4,128)(2,1)} reshape(bf16[4,9,16,128]{3,2,0,1:T(8,128)(2,1)S(1)} %broadcast_in_dim.697) | data formatting | bytes 294912 | tf_op jit(solution)/shard_map/reshape | solution.py:23
  35.4 0.1 copy.86
  35.4 0.1 reshape.2239
  35.6 1.0 %broadcast_select_fusion = bf16[4,16,1024]{2,1,0:T(8,128)(2,1)S(1)} fusion(bf16[4,16,1024]{2,1,0:T(8,128)(2,1)S(1)} %copy-done.10, bf16[4,16,1024]{2,1,0:T(8,128)(2,1)} %collective-permute-done, pred[4]{0:T(512)(128)(4,1)S(1)} %copy-done.21), kind=kLoop, calls=%fused_computation.120 | loop fusion | flops 65536 | bytes 393220 | tf_op jit(solution)/shard_map/jit(_where)/select_n | solution.py:110
  36.6 1.4 %gather_fusion.1 = bf16[16,16,1024]{2,1,0:T(8,128)(2,1)} fusion(bf16[4,16,1024]{2,1,0:T(8,128)(2,1)S(1)} %broadcast_select_fusion, s32[1024]{0:T(1024)S(1)} %pad_clamp_fusion), kind=kCustom, calls=%fused_computation.1 | custom fusion | bytes 1048640 | tf_op jit(solution)/shard_map/gather | solution.py:111
  37.9 4.2 %all-to-all-start.1 = ((bf16[8,2,16,1024]{3,2,1,0:T(8,128)(2,1)}), bf16[8,2,16,1024]{3,2,1,0:T(8,128)(2,1)S(1)}, u32[]{:S(2)}, u32[]{:S(2)}) async-start(bf16[8,2,16,1024]{3,2,1,0:T(8,128)(2,1)} %bitcast.118), calls=%async_computation.1 | async-start | bytes 1048576 | tf_op jit(solution)/shard_map/all_to_all | solution.py:112
  42.1 0.9 %slice_bitcast_fusion.27 = (bf16[4,2048]{1,0:T(4,128)(2,1)S(1)}, bf16[4,2048]{1,0:T(4,128)(2,1)S(1)}, bf16[4,2048]{1,0:T(4,128)(2,1)S(1)}, bf16[4,2048]{1,0:T(4,...) fusion(bf16[4,9,2048]{2,0,1:T(4,128)(2,1)} %reshape.2213), kind=kLoop, calls=%fused_computation.147 | loop fusion | bytes 294912 | tf_op jit(solution)/shard_map/jit(_where)/broadcast_in_dim | solution.py:26
  43.1 4.7 %select_select_fusion.3 = bf16[4,128,2048]{2,1,0:T(8,128)(2,1)} fusion(pred[128,2048]{1,0:T(8,128)(4,1)} %copy-done.8, pred[128,2048]{1,0:T(8,128)(4,1)} %copy-done.7, pred[128,2048]{1,0:T(8,128)(4,1)} %copy-done.6, pred[128,2048]{1,0:T(8,128)(4,1)} %copy-done.5, pred[128,2048]{1,0:T(8,128)(4,1)} %copy-done.4, pred[128,2048]{1,0:T(8,128)(4,1)} %copy-done.3, ...), kind=kLoop, calls=%fused_computation.9 | loop fusion | flops 9437184 | bytes 4603904 | tf_op jit(solution)/shard_map/jit(_where)/select_n | solution.py:26
  47.8 3.2 %all-to-all-done.1 = bf16[8,2,16,1024]{3,2,1,0:T(8,128)(2,1)S(1)} async-done(((bf16[8,2,16,1024]{3,2,1,0:T(8,128)(2,1)}), bf16[8,2,16,1024]{3,2,1,0:T(8,128)(2,1)S(1)}, u32[]{:S(2)}, u32[]{:S(2)}) %all-to-all-start.1) | async-done | bytes 524320 | tf_op jit(solution)/shard_map/all_to_all | solution.py:112
  51.1 1.3 %fusion.47 = f32[2,128,128]{2,1,0:T(8,128)S(1)} fusion(bf16[2,128,1024]{2,1,0:T(8,128)(2,1)S(1)} %bitcast.116, bf16[128,1024]{1,0:T(8,128)(2,1)} %param.28), kind=kOutput, calls=%fused_computation.101 | convolution fusion | flops 67108864 | bytes 917504 | tf_op jit(solution)/shard_map/ac,jbc->jab/dot_general | solution.py:89
  52.3 0.1 copy.88
  52.4 0.2 multiply_reduce_fusion
  52.6 0.1 sqrt.19
  52.7 0.1 fusion.61
  52.9 0.1 fusion.50
  53.0 0.2 fusion.56
  53.2 0.1 fusion.57
  53.4 3.8 %fusion.77 = f32[4,128,2048]{2,1,0:T(8,128)} fusion(bf16[4,128,640]{2,1,0:T(8,128)(2,1)S(1)} %constant_dynamic-update-slice_fusion, bf16[640,2048,1]{1,0,2:T(8,128)(2,1)S(1)} %bitcast.115), kind=kOutput, calls=%fused_computation.184 | convolution fusion | flops 1342177280 | bytes 7471104 | tf_op jit(solution)/shard_map/vak,kn->van/dot_general | solution.py:67
  57.2 8.4 %fusion.8 = f32[4,128,1152]{2,1,0:T(8,128)S(1)} fusion(bf16[2048,1152,1]{1,0,2:T(8,128)(2,1)} %bitcast.113, f32[4,128,2048]{2,1,0:T(8,128)} %fusion.77, bf16[512,2048,1]{1,0,2:T(8,128)(2,1)} %bitcast.117, f32[2048]{0:T(1024)S(1)} %broadcast_bitcast_fusion, bf16[4,128,128]{2,1,0:T(8,128)(2,1)S(1)} %get-tuple-element.58, ...), kind=kOutput, calls=%fused_computation.32 | convolution fusion | flops 3495952384 | bytes 13901824 | tf_op jit(solution)/shard_map/vak,kn->van/dot_general | solution.py:73
  65.6 0.2 fusion.76
  65.9 0.3 fusion.41
  66.2 0.1 copy.96
  66.3 0.8 %copy.94 = f32[1,2,128,128]{3,2,1,0:T(8,128)} copy(f32[1,2,128,128]{2,3,1,0:T(8,128)S(1)} %fusion.60) | data formatting | bytes 262144 | tf_op jit(solution)/shard_map/broadcast_in_dim | solution.py:125
  (73 shorter events, 0.4 us)
Async XLA Ops:
  0.0 10.5 %copy-start = (f32[16]{0:T(128)S(1)}, f32[16]{0:T(128)}, u32[]{:S(2)}) copy-start(f32[16]{0:T(128)} %param.33) | copy-start | bytes 196
  0.0 9.7 %copy-start.22 = (s32[4]{0:T(128)S(1)}, s32[4]{0:T(128)}, u32[]{:S(2)}) copy-start(s32[4]{0:T(128)} %param.30) | copy-start | bytes 52
  0.0 10.4 %copy-start.9 = (bf16[128,1024]{1,0:T(8,128)(2,1)S(1)}, bf16[128,1024]{1,0:T(8,128)(2,1)}, u32[]{:S(2)}) copy-start(bf16[128,1024]{1,0:T(8,128)(2,1)} %param.28) | copy-start | bytes 786436
  2.4 16.8 %all-to-all-start = ((bf16[8,16,1152]{2,1,0:T(8,128)(2,1)}), bf16[8,16,1152]{2,1,0:T(8,128)(2,1)S(1)}, u32[]{:S(2)}, u32[]{:S(2)}) async-start(bf16[8,16,1152]{2,1,0:T(8,128)(2,1)} %pad_maximum_fusion), calls=%async_computation | async-start | bytes 589824 | tf_op jit(solution)/shard_map/all_to_all | solution.py:103
  7.7 5.9 %copy-start.12 = (s32[128]{0:T(128)}, s32[128]{0:T(128)S(1)}, u32[]{:S(2)}) copy-start(s32[128]{0:T(128)S(1)} %get-tuple-element.86) | copy-start | bytes 1540
  7.7 5.9 %copy-start.14 = (s32[128]{0:T(128)}, s32[128]{0:T(128)S(1)}, u32[]{:S(2)}) copy-start(s32[128]{0:T(128)S(1)} %get-tuple-element.87) | copy-start | bytes 1540
  7.8 5.8 %copy-start.16 = (s32[128]{0:T(128)}, s32[128]{0:T(128)S(1)}, u32[]{:S(2)}) copy-start(s32[128]{0:T(128)S(1)} %get-tuple-element.88) | copy-start | bytes 1540
  7.8 5.8 %copy-start.18 = (s32[128]{0:T(128)}, s32[128]{0:T(128)S(1)}, u32[]{:S(2)}) copy-start(s32[128]{0:T(128)S(1)} %get-tuple-element.89) | copy-start | bytes 1540
  13.5 3.3 %copy-start.1 = (pred[128,2048]{1,0:T(8,128)(4,1)}, pred[128,2048]{1,0:T(8,128)(4,1)S(1)}, u32[]{:S(2)}) copy-start(pred[128,2048]{1,0:T(8,128)(4,1)S(1)} %get-tuple-element.63) | copy-start | bytes 786436
  13.5 3.3 %copy-start.2 = (pred[128,2048]{1,0:T(8,128)(4,1)}, pred[128,2048]{1,0:T(8,128)(4,1)S(1)}, u32[]{:S(2)}) copy-start(pred[128,2048]{1,0:T(8,128)(4,1)S(1)} %get-tuple-element.64) | copy-start | bytes 786436
  13.5 3.3 %copy-start.3 = (pred[128,2048]{1,0:T(8,128)(4,1)}, pred[128,2048]{1,0:T(8,128)(4,1)S(1)}, u32[]{:S(2)}) copy-start(pred[128,2048]{1,0:T(8,128)(4,1)S(1)} %get-tuple-element.65) | copy-start | bytes 786436
  13.6 3.3 %copy-start.4 = (pred[128,2048]{1,0:T(8,128)(4,1)}, pred[128,2048]{1,0:T(8,128)(4,1)S(1)}, u32[]{:S(2)}) copy-start(pred[128,2048]{1,0:T(8,128)(4,1)S(1)} %get-tuple-element.66) | copy-start | bytes 786436
  13.6 3.3 %copy-start.5 = (pred[128,2048]{1,0:T(8,128)(4,1)}, pred[128,2048]{1,0:T(8,128)(4,1)S(1)}, u32[]{:S(2)}) copy-start(pred[128,2048]{1,0:T(8,128)(4,1)S(1)} %get-tuple-element.67) | copy-start | bytes 786436
  13.6 3.3 %copy-start.6 = (pred[128,2048]{1,0:T(8,128)(4,1)}, pred[128,2048]{1,0:T(8,128)(4,1)S(1)}, u32[]{:S(2)}) copy-start(pred[128,2048]{1,0:T(8,128)(4,1)S(1)} %get-tuple-element.68) | copy-start | bytes 786436
  13.6 3.3 %copy-start.7 = (pred[128,2048]{1,0:T(8,128)(4,1)}, pred[128,2048]{1,0:T(8,128)(4,1)S(1)}, u32[]{:S(2)}) copy-start(pred[128,2048]{1,0:T(8,128)(4,1)S(1)} %get-tuple-element.69) | copy-start | bytes 786436
  13.6 3.3 %copy-start.8 = (pred[128,2048]{1,0:T(8,128)(4,1)}, pred[128,2048]{1,0:T(8,128)(4,1)S(1)}, u32[]{:S(2)}) copy-start(pred[128,2048]{1,0:T(8,128)(4,1)S(1)} %get-tuple-element.70) | copy-start | bytes 786436
  13.6 3.2 %copy-start.13 = (s32[128]{0:T(128)S(1)}, s32[128]{0:T(128)}, u32[]{:S(2)}) copy-start(s32[128]{0:T(128)} %copy-done.12) | copy-start | bytes 1540
  13.7 3.2 %copy-start.15 = (s32[128]{0:T(128)S(1)}, s32[128]{0:T(128)}, u32[]{:S(2)}) copy-start(s32[128]{0:T(128)} %copy-done.14) | copy-start | bytes 1540
  13.7 3.2 %copy-start.17 = (s32[128]{0:T(128)S(1)}, s32[128]{0:T(128)}, u32[]{:S(2)}) copy-start(s32[128]{0:T(128)} %copy-done.16) | copy-start | bytes 1540
  13.7 3.2 %copy-start.19 = (s32[128]{0:T(128)S(1)}, s32[128]{0:T(128)}, u32[]{:S(2)}) copy-start(s32[128]{0:T(128)} %copy-done.18) | copy-start | bytes 1540
  20.4 15.1 %collective-permute-start = (bf16[4,16,1024]{2,1,0:T(8,128)(2,1)}, bf16[4,16,1024]{2,1,0:T(8,128)(2,1)}, u32[]{:S(2)}, u32[]{:S(2)}) collective-permute-start(bf16[4,16,1024]{2,1,0:T(8,128)(2,1)} %gather_fusion), channel_id=1, source_target_pairs={{0,8},{8,0},{1,9},{9,1},{2,10},{10,2},{3,11},{11,3},{4,12},{12,4},... | collective-permute-start | bytes 393224 | tf_op jit(solution)/shard_map/ppermute | solution.py:108
  26.3 9.3 %copy-start.10 = (bf16[4,16,1024]{2,1,0:T(8,128)(2,1)S(1)}, bf16[4,16,1024]{2,1,0:T(8,128)(2,1)}, u32[]{:S(2)}) copy-start(bf16[4,16,1024]{2,1,0:T(8,128)(2,1)} %gather_fusion) | copy-start | bytes 393220
  26.3 9.3 %copy-start.21 = (pred[4]{0:T(512)(128)(4,1)S(1)}, pred[4]{0:T(512)(128)(4,1)}, u32[]{:S(2)}) copy-start(pred[4]{0:T(512)(128)(4,1)} %fusion.72) | copy-start | bytes 16
  37.9 13.1 %all-to-all-start.1 = ((bf16[8,2,16,1024]{3,2,1,0:T(8,128)(2,1)}), bf16[8,2,16,1024]{3,2,1,0:T(8,128)(2,1)S(1)}, u32[]{:S(2)}, u32[]{:S(2)}) async-start(bf16[8,2,16,1024]{3,2,1,0:T(8,128)(2,1)} %bitcast.118), calls=%async_computation.1 | async-start | bytes 1048576 | tf_op jit(solution)/shard_map/all_to_all | solution.py:112
  47.8 5.1 %copy-start.11 = (pred[128]{0:T(512)(128)(4,1)S(1)}, pred[128]{0:T(512)(128)(4,1)}, u32[]{:S(2)}) copy-start(pred[128]{0:T(512)(128)(4,1)} %constant.253) | copy-start | bytes 388
  47.8 5.2 %copy-start.20 = (pred[128]{0:T(512)(128)(4,1)S(1)}, pred[128]{0:T(512)(128)(4,1)}, u32[]{:S(2)}) copy-start(pred[128]{0:T(512)(128)(4,1)} %constant.254) | copy-start | bytes 388

commit v13 on v8

--- a/solution.py
+++ b/solution.py
@@ -18,23 +18,23 @@
     return jnp.where(inside, e1 * 3 + e2, -1)
 
 
-def banded(weights, table, cells):
+def banded(weights, table, cells, tie=None):
     rows, _, groups = weights.shape
+    masks = tuple(table == e for e in range(TAPS))
+    if tie is not None:
+        masks, weights, _ = lax.optimization_barrier((masks, weights, tie))
     spread_w = jnp.repeat(weights, cells, axis=2)
     band = jnp.zeros((rows, cells, groups * cells), weights.dtype)
     for e in range(TAPS):
-        band = jnp.where(table[None] == e, spread_w[:, e, None, :], band)
+        band = jnp.where(masks[e][None], spread_w[:, e, None, :], band)
     return band
 
 
 def band_first(weight_first, tie):
     hid = weight_first.shape[0]
     cells = HQ * WQ
-    table, weight_first, _ = lax.optimization_barrier(
-        (tap_table(cells, hid * cells), weight_first, tie)
-    )
     w1 = weight_first.reshape(hid, TAPS, TAPS)
-    k1 = banded(jnp.transpose(w1, (1, 2, 0)), table, cells)
+    k1 = banded(jnp.transpose(w1, (1, 2, 0)), tap_table(cells, hid * cells), cells, tie)
     return k1.reshape(TAPS * cells, hid * cells)
 
 

time: 59.5 us -> 57.4 us (0.965)
  waiting for transfers between devices: 2.11 us -> 0.01 us
  local copies, waits for them, and re-layouts: 7.26 us -> 6.62 us
  starting transfers between devices: 11.5 us -> 12.1 us
    all_to_all x1, waiting for transfers between devices: 2.1 us -> 0.01 us  [gather_sources(): arrived = lax.all_to_all(payload, 'sub', 0, 0)]
    eq x2, other arithmetic: 3.13 us -> 3.83 us  [banded(): masks = tuple((table == e for e in range(TAPS)))]
    gather x1, local copies, waits for them, and re-layouts: 1.21 us -> 0.56 us  [gather_sources(): local = chunks[hubs % sub]]
    select_n x2 -> x1, other arithmetic: 1.02 us -> 0.41 us  [tap_table(): return jnp.where(inside, e1 * 3 + e2, -1)]
  transfers between devices with their start and end apart: 3 -> 3, of which waited for: 1 -> 0; matrix products, arithmetic and copies ran while one was open for 41% -> 43% of each run, Pallas kernels for 0% -> 0%
where the time goes in v13:
time: 57.4 us; the launch traced here: 56.9 us
  other arithmetic  27 us (47%)
  starting transfers between devices  12.1 us (21%)
  matrix products  10.1 us (18%)
  local copies, waits for them, and re-layouts  6.62 us (12%)
  between operations  0.99 us (2%)
    select_n x2, other arithmetic, banded(): band = jnp.where(masks[e][None], spread_w[:, e, None, :], band)  15.6 us
    dot_general x1, matrix products, consensus_stack(): jnp.einsum('vak,kn->van', hidden, k2, preferred_element_type=jnp.float32)  9.81 us
    all_to_all x1, starting transfers between devices, gather_sources(): arrived = lax.all_to_all(payload, 'sub', 0, 0)  5.28 us
    all_to_all x1, starting transfers between devices, gather_sources(): got = lax.all_to_all(parcel, 'sub', 0, 0)  4.2 us
    eq x2, other arithmetic, banded(): masks = tuple((table == e for e in range(TAPS)))  3.83 us
    ppermute x1, starting transfers between devices, gather_sources(): mirror = lax.ppermute(local, 'half', [(0, 1), (1, 0)])  2.65 us
    concatenate x1, other arithmetic, gather_sources(): jnp.concatenate([source_maps.reshape(sub, rows, channels), tag], axis=2)  1.68 us
    gather x1, local copies, waits for them, and re-layouts, gather_sources(): parcel = named[picks]  1.39 us
  transfers between devices with their start and end apart: 3, of which 0 were waited for; matrix products, arithmetic and copies ran while one was open for 43% of the time, Pallas kernels for 0%

profile of v13, /device:TPU:0, one launch (start us, length us, event | category | flops | bytes accessed | tf_op | source)
XLA Modules:
  0.0 56.9 jit_solution(10376947424929562586)
XLA Ops:
  0.0 0.7 %convert_element_type.44 = bf16[1,2]{1,0:T(2,128)(2,1)S(1)} convert(s32[1,2]{1,0:T(1,128)} %param.31) | non-fusion elementwise | flops 2 | bytes 12 | tf_op jit(solution)/shard_map/convert_element_type | solution.py:102
  0.7 1.7 %pad_maximum_fusion = bf16[8,16,1152]{2,1,0:T(8,128)(2,1)} fusion(bf16[8,16,128]{2,1,0:T(8,128)(2,1)S(1)} %scatter.8, bf16[8,16,1024]{2,1,0:T(8,128)(2,1)} %bitcast.95), kind=kLoop, calls=%fused_computation.61 | loop fusion | flops 589824 | bytes 589824 | tf_op jit(solution)/shard_map/concatenate | solution.py:103
  2.4 5.3 %all-to-all-start = ((bf16[8,16,1152]{2,1,0:T(8,128)(2,1)}), bf16[8,16,1152]{2,1,0:T(8,128)(2,1)S(1)}, u32[]{:S(2)}, u32[]{:S(2)}) async-start(bf16[8,16,1152]{2,1,0:T(8,128)(2,1)} %pad_maximum_fusion), calls=%async_computation | async-start | bytes 589824 | tf_op jit(solution)/shard_map/all_to_all | solution.py:104
  7.7 0.7 %compare_select_fusion.1 = s32[4]{0:T(128)S(1)} fusion(s32[4]{0:T(128)} %param.30), kind=kLoop, calls=%fused_computation.155 | loop fusion | flops 56 | bytes 32 | tf_op jit(solution)/shard_map/select_n | solution.py:108
  8.4 0.7 %fusion.68 = pred[4]{0:T(512)(128)(4,1)S(1)} fusion(s32[4]{0:T(128)} %param.30, s32[]{:T(128)S(6)} %axis_index.15), kind=kLoop, calls=%fused_computation.167 | loop fusion | flops 64 | bytes 24 | tf_op jit(solution)/shard_map/eq | solution.py:112
  9.1 1.1 %multiply_reduce_fusion.1 = f32[128]{0:T(128)S(1)} fusion(bf16[128,1024]{1,0:T(8,128)(2,1)} %param.28), kind=kLoop, calls=%fused_computation.43 | loop fusion | flops 393088 | bytes 262656 | tf_op jit(solution)/shard_map/reduce_sum | solution.py:88
  10.2 0.0 copy-done
  10.2 0.1 broadcast_bitcast_fusion
  10.3 3.0 %broadcast_compare_fusion = (pred[128,2048]{1,0:T(8,128)(4,1)S(1)}, pred[128,2048]{1,0:T(8,128)(4,1)S(1)}, pred[128,2048]{1,0:T(8,128)(4,1)S(1)}, pred[128,2048]...) fusion(s32[128]{0:T(128)S(1)} %get-tuple-element.96, ...), kind=kLoop, calls=%fused_computation.44 | loop fusion | flops 11796480 | bytes 2380032 | tf_op jit(solution)/shard_map/eq | solution.py:23
  14.0 0.4 add_select_fusion.5
  14.4 0.0 all-to-all-done
  14.4 0.6 gather_fusion
  15.0 2.7 %collective-permute-start = (bf16[4,16,1024]{2,1,0:T(8,128)(2,1)S(1)}, bf16[4,16,1024]{2,1,0:T(8,128)(2,1)}, u32[]{:S(2)}, u32[]{:S(2)}) collective-permute-start(bf16[4,16,1024]{2,1,0:T(8,128)(2,1)S(1)} %gather_fusion), channel_id=1, source_target_pairs={{0,8},{8,0},{1,9},{9,1},{2,10},{10,2},{3,11},{11,3},{4,12},{12,4},... | collective-permute-start | bytes 393224 | tf_op jit(solution)/shard_map/ppermute | solution.py:109
  17.7 0.2 broadcast_in_dim.491
  17.9 0.2 reshape.172
  18.1 0.7 %slice_bitcast_fusion.9 = (bf16[9,2048]{1,0:T(8,128)(2,1)S(1)}, bf16[9,2048]{1,0:T(8,128)(2,1)S(1)}, bf16[9,2048]{1,0:T(8,128)(2,1)S(1)}, bf16[9,2048]{1,0:T(8,1...) fusion(bf16[9,9,2048]{2,0,1:T(8,128)(2,1)S(1)} %reshape.172), kind=kLoop, calls=%fused_computation.127 | loop fusion | bytes 663552 | tf_op jit(solution)/shard_map/jit(_where)/broadcast_in_dim | solution.py:29
  18.8 0.1 copy.88
  18.9 8.3 %select_select_fusion.1 = bf16[9,128,2048]{2,1,0:T(8,128)(2,1)} fusion(pred[128,2048]{1,0:T(8,128)(4,1)S(1)} %get-tuple-element.40, pred[128,2048]{1,0:T(8,128)(4,1)} %get-tuple-element.39, pred[128,2048]{1,0:T(8,128)(4,1)} %get-tuple-element.38, pred[128,2048]{1,0:T(8,128)(4,1)} %get-tuple-element.37, pred[128,2048]{1,0:T(8,128)(4,1)S(1)} %get-tuple-element.36, ...), kind=kLoop, calls=%fused_computation.5 | loop fusion | flops 21233664 | bytes 7409664 | tf_op jit(solution)/shard_map/jit(_where)/select_n | solution.py:29
  27.3 0.1 copy.81
  27.3 0.1 reshape.195
  27.4 0.0 collective-permute-done
  27.4 1.0 %broadcast_select_fusion = bf16[4,16,1024]{2,1,0:T(8,128)(2,1)S(1)} fusion(bf16[4,16,1024]{2,1,0:T(8,128)(2,1)S(1)} %gather_fusion, bf16[4,16,1024]{2,1,0:T(8,128)(2,1)} %collective-permute-done, pred[4]{0:T(512)(128)(4,1)S(1)} %fusion.68), kind=kLoop, calls=%fused_computation.118 | loop fusion | flops 65536 | bytes 393220 | tf_op jit(solution)/shard_map/jit(_where)/select_n | solution.py:113
  28.4 1.4 %gather_fusion.1 = bf16[16,16,1024]{2,1,0:T(8,128)(2,1)} fusion(bf16[4,16,1024]{2,1,0:T(8,128)(2,1)S(1)} %broadcast_select_fusion, s32[1024]{0:T(1024)S(1)} %pad_clamp_fusion), kind=kCustom, calls=%fused_computation.1 | custom fusion | bytes 1048640 | tf_op jit(solution)/shard_map/gather | solution.py:114
  29.8 4.2 %all-to-all-start.1 = ((bf16[8,2,16,1024]{3,2,1,0:T(8,128)(2,1)}), bf16[8,2,16,1024]{3,2,1,0:T(8,128)(2,1)S(1)}, u32[]{:S(2)}, u32[]{:S(2)}) async-start(bf16[8,2,16,1024]{3,2,1,0:T(8,128)(2,1)} %bitcast.14), calls=%async_computation.1 | async-start | bytes 1048576 | tf_op jit(solution)/shard_map/all_to_all | solution.py:115
  34.0 0.8 %broadcast_compare_fusion.13 = (pred[128,1152]{1,0:T(8,128)(4,1)S(1)}, pred[128,1152]{1,0:T(8,128)(4,1)S(1)}, pred[128,1152]{1,0:T(8,128)(4,1)S(1)}, pred[128,11...) fusion(s32[128,1152]{1,0:T(8,128)S(1)} %add_select_fusion.5), kind=kLoop, calls=%fused_computation.66 | loop fusion | flops 1327104 | bytes 1916928 | tf_op jit(solution)/shard_map/eq | solution.py:23
  34.9 0.1 copy.85
  35.0 0.4 broadcast_in_dim.548
  35.4 0.2 reshape.175
  35.6 0.0 copy-start.1
  35.6 7.3 %select_select_fusion = bf16[16,128,1152]{2,1,0:T(8,128)(2,1)} fusion(pred[128,1152]{1,0:T(8,128)(4,1)S(1)} %get-tuple-element.54, pred[128,1152]{1,0:T(8,128)(4,1)S(1)} %get-tuple-element.55, pred[128,1152]{1,0:T(8,128)(4,1)S(1)} %get-tuple-element.56, pred[128,1152]{1,0:T(8,128)(4,1)S(1)} %get-tuple-element.57, pred[128,1152]{1,0:T(8,128)(4,1)S(1)} %get-tuple-element.58, ...), kind=kLoop, calls=%fused_computation.4 | loop fusion | flops 21233664 | bytes 6377472 | tf_op jit(solution)/shard_map/jit(_where)/select_n | solution.py:29
  42.9 0.0 all-to-all-done.1
  43.0 0.3 fusion.39
  43.3 0.1 copy.83
  43.4 0.2 multiply_reduce_fusion
  43.6 0.1 sqrt.19
  43.7 0.1 fusion.57
  43.9 0.1 fusion.42
  44.0 0.1 fusion.45
  44.1 0.1 fusion.47
  44.3 0.1 fusion.49
  44.4 0.1 fusion.51
  44.6 0.1 fusion.54
  44.7 1.0 %copy-done.4 = bf16[4,128,1152]{2,1,0:T(8,128)(2,1)} copy-done((bf16[4,128,1152]{2,1,0:T(8,128)(2,1)}, bf16[4,128,1152]{2,1,0:T(8,128)(2,1)S(1)}, u32[]{:S(2)}) %copy-start.4) | copy-done | bytes 1179672
  45.7 9.8 %fusion.13 = f32[4,128,1152]{2,1,0:T(8,128)S(1)} fusion(bf16[2048,1152,1]{1,0,2:T(8,128)(2,1)} %bitcast.91, bf16[4,128,1152]{2,1,0:T(8,128)(2,1)} %copy-done.4, bf16[1152,2048]{1,0:T(8,128)(2,1)} %bitcast.93, f32[2048]{0:T(1024)S(1)} %broadcast_bitcast_fusion), kind=kOutput, calls=%fused_computation.33 | convolution fusion | flops 4834983936 | bytes 12984320 | tf_op jit(solution)/shard_map/vak,kn->van/dot_general | solution.py:74
  55.5 0.2 fusion.70
  55.7 0.3 fusion.33
  56.0 0.1 copy.89
  56.2 0.8 %copy.87 = f32[1,2,128,128]{3,2,1,0:T(8,128)} copy(f32[1,2,128,128]{2,3,1,0:T(8,128)S(1)} %fusion.56) | data formatting | bytes 262144 | tf_op jit(solution)/shard_map/broadcast_in_dim | solution.py:128
  (38 shorter events, 0.4 us)
Async XLA Ops:
  0.0 10.2 %copy-start = (f32[16]{0:T(128)S(1)}, f32[16]{0:T(128)}, u32[]{:S(2)}) copy-start(f32[16]{0:T(128)} %param.33) | copy-start | bytes 196
  0.0 13.3 %copy-start.2 = (bf16[16,1,3,3,3,3]{0,5,4,3,2,1:T(4,128)(2,1)S(1)}, bf16[16,1,3,3,3,3]{0,5,4,3,2,1:T(4,128)(2,1)}, u32[]{:S(2)}) copy-start(bf16[16,1,3,3,3,3]{0,5,4,3,2,1:T(4,128)(2,1)} %param.32) | copy-start | bytes 7780
  2.4 12.0 %all-to-all-start = ((bf16[8,16,1152]{2,1,0:T(8,128)(2,1)}), bf16[8,16,1152]{2,1,0:T(8,128)(2,1)S(1)}, u32[]{:S(2)}, u32[]{:S(2)}) async-start(bf16[8,16,1152]{2,1,0:T(8,128)(2,1)} %pad_maximum_fusion), calls=%async_computation | async-start | bytes 589824 | tf_op jit(solution)/shard_map/all_to_all | solution.py:104
  15.0 12.4 %collective-permute-start = (bf16[4,16,1024]{2,1,0:T(8,128)(2,1)S(1)}, bf16[4,16,1024]{2,1,0:T(8,128)(2,1)}, u32[]{:S(2)}, u32[]{:S(2)}) collective-permute-start(bf16[4,16,1024]{2,1,0:T(8,128)(2,1)S(1)} %gather_fusion), channel_id=1, source_target_pairs={{0,8},{8,0},{1,9},{9,1},{2,10},{10,2},{3,11},{11,3},{4,12},{12,4},... | collective-permute-start | bytes 393224 | tf_op jit(solution)/shard_map/ppermute | solution.py:109
  27.3 7.6 %copy-start.3 = (bf16[1,16,3,3,3,3]{1,5,4,3,2,0:T(4,128)(2,1)S(1)}, bf16[1,16,3,3,3,3]{1,5,4,3,2,0:T(4,128)(2,1)}, u32[]{:S(2)}) copy-start(bf16[1,16,3,3,3,3]{1,5,4,3,2,0:T(4,128)(2,1)} %param.34) | copy-start | bytes 7780
  29.8 13.1 %all-to-all-start.1 = ((bf16[8,2,16,1024]{3,2,1,0:T(8,128)(2,1)}), bf16[8,2,16,1024]{3,2,1,0:T(8,128)(2,1)S(1)}, u32[]{:S(2)}, u32[]{:S(2)}) async-start(bf16[8,2,16,1024]{3,2,1,0:T(8,128)(2,1)} %bitcast.14), calls=%async_computation.1 | async-start | bytes 1048576 | tf_op jit(solution)/shard_map/all_to_all | solution.py:115
  35.6 7.3 %copy-start.1 = (bf16[128,1024]{1,0:T(8,128)(2,1)S(1)}, bf16[128,1024]{1,0:T(8,128)(2,1)}, u32[]{:S(2)}) copy-start(bf16[128,1024]{1,0:T(8,128)(2,1)} %param.28) | copy-start | bytes 786436
  42.9 0.9 %copy-start.5 = (pred[128]{0:T(512)(128)(4,1)S(1)}, pred[128]{0:T(512)(128)(4,1)}, u32[]{:S(2)}) copy-start(pred[128]{0:T(512)(128)(4,1)} %constant.233) | copy-start | bytes 388
  42.9 1.1 %copy-start.6 = (pred[128]{0:T(512)(128)(4,1)S(1)}, pred[128]{0:T(512)(128)(4,1)}, u32[]{:S(2)}) copy-start(pred[128]{0:T(512)(128)(4,1)} %constant.234) | copy-start | bytes 388
  44.7 1.0 %copy-start.4 = (bf16[4,128,1152]{2,1,0:T(8,128)(2,1)}, bf16[4,128,1152]{2,1,0:T(8,128)(2,1)S(1)}, u32[]{:S(2)}) copy-start(bf16[4,128,1152]{2,1,0:T(8,128)(2,1)S(1)} %fusion.54) | copy-start | bytes 3538948

commit v14 on v13

--- a/solution.py
+++ b/solution.py
@@ -98,8 +98,10 @@
     cells, channels = source_maps.shape
     rows = cells // sub
     lanes = 128
-    tag = jnp.zeros((sub, rows, lanes), source_maps.dtype)
-    tag = tag.at[:, 0, :2].set(pick[0][None, :].astype(source_maps.dtype))
+    row = lax.broadcasted_iota(jnp.int32, (sub, rows, lanes), 1)
+    lane = lax.broadcasted_iota(jnp.int32, (sub, rows, lanes), 2)
+    value = jnp.where(lane == 0, pick[0, 0], pick[0, 1]).astype(source_maps.dtype)
+    tag = jnp.where((row == 0) & (lane < 2), value, jnp.zeros((), source_maps.dtype))
     payload = jnp.concatenate([source_maps.reshape(sub, rows, channels), tag], axis=2)
     arrived = lax.all_to_all(payload, "sub", 0, 0)
     chunks = arrived[:, :, :channels]

time: 57.4 us -> 58.8 us (1.024)
  local copies, waits for them, and re-layouts: 6.62 us -> 7.45 us
  other arithmetic: 27 us -> 27.8 us
    slice x0 -> x1, local copies, waits for them, and re-layouts: none -> 1.39 us  [gather_sources(): pick[0, 0]]
    convert_element_type x1, other arithmetic: 0.68 us -> 1.34 us  [gather_sources(): jnp.where(lane == 0, pick[0, 0], pick[0, 1]).astype(source_maps.dtype)]
    unnamed x18, local copies, waits for them, and re-layouts: 1.31 us -> 0.69 us
  transfers between devices with their start and end apart: 3 -> 3, of which waited for: 0 -> 0; matrix products, arithmetic and copies ran while one was open for 43% -> 42% of each run, Pallas kernels for 0% -> 0%
where the time goes in v14:
time: 58.8 us; the launch traced here: 58.3 us
  other arithmetic  27.8 us (47%)
  starting transfers between devices  12.1 us (21%)
  matrix products  9.86 us (17%)
  local copies, waits for them, and re-layouts  7.45 us (13%)
  between operations  1.01 us (2%)
    select_n x2, other arithmetic, banded(): band = jnp.where(masks[e][None], spread_w[:, e, None, :], band)  15.6 us
    dot_general x1, matrix products, consensus_stack(): jnp.einsum('vak,kn->van', hidden, k2, preferred_element_type=jnp.float32)  9.55 us
    all_to_all x1, starting transfers between devices, gather_sources(): arrived = lax.all_to_all(payload, 'sub', 0, 0)  5.28 us
    all_to_all x1, starting transfers between devices, gather_sources(): got = lax.all_to_all(parcel, 'sub', 0, 0)  4.2 us
    eq x2, other arithmetic, banded(): masks = tuple((table == e for e in range(TAPS)))  3.87 us
    ppermute x1, starting transfers between devices, gather_sources(): mirror = lax.ppermute(local, 'half', [(0, 1), (1, 0)])  2.65 us
    concatenate x1, other arithmetic, gather_sources(): jnp.concatenate([source_maps.reshape(sub, rows, channels), tag], axis=2)  1.68 us
    slice x1, local copies, waits for them, and re-layouts, gather_sources(): pick[0, 0]  1.39 us
  transfers between devices with their start and end apart: 3, of which 0 were waited for; matrix products, arithmetic and copies ran while one was open for 42% of the time, Pallas kernels for 0%

profile of v14, /device:TPU:0, one launch (start us, length us, event | category | flops | bytes accessed | tf_op | source)
XLA Modules:
  0.0 58.3 jit_solution(14750983502746359522)
XLA Ops:
  0.0 1.4 %fusion.72 = (s32[1,1]{1,0:T(1,128)}, s32[1,1]{1,0:T(1,128)}) fusion(s32[1,2]{1,0:T(1,128)} %param.29), kind=kLoop, calls=%fused_computation.177 | loop fusion | bytes 16 | tf_op jit(solution)/shard_map/slice | solution.py:103
  1.4 1.3 %fusion.68 = bf16[128]{0:T(256)(128)(2,1)S(1)} fusion(s32[]{:T(128)} %bitcast.2, s32[]{:T(128)} %bitcast.1), kind=kLoop, calls=%fused_computation.168 | loop fusion | flops 384 | bytes 264 | tf_op jit(solution)/shard_map/convert_element_type | solution.py:103
  2.8 0.1 and_select_fusion
  2.8 1.7 %pad_maximum_fusion = bf16[8,16,1152]{2,1,0:T(8,128)(2,1)} fusion(bf16[8,16,128]{2,1,0:T(8,128)(2,1)S(1)} %and_select_fusion, bf16[8,16,1024]{2,1,0:T(8,128)(2,1)} %bitcast.97), kind=kLoop, calls=%fused_computation.61 | loop fusion | flops 589824 | bytes 589824 | tf_op jit(solution)/shard_map/concatenate | solution.py:105
  4.5 5.3 %all-to-all-start = ((bf16[8,16,1152]{2,1,0:T(8,128)(2,1)}), bf16[8,16,1152]{2,1,0:T(8,128)(2,1)S(1)}, u32[]{:S(2)}, u32[]{:S(2)}) async-start(bf16[8,16,1152]{2,1,0:T(8,128)(2,1)} %pad_maximum_fusion), calls=%async_computation | async-start | bytes 589824 | tf_op jit(solution)/shard_map/all_to_all | solution.py:106
  9.9 0.7 %compare_select_fusion.1 = s32[4]{0:T(128)S(1)} fusion(s32[4]{0:T(128)} %param.28), kind=kLoop, calls=%fused_computation.156 | loop fusion | flops 56 | bytes 32 | tf_op jit(solution)/shard_map/select_n | solution.py:110
  10.6 0.7 %fusion.69 = pred[4]{0:T(512)(128)(4,1)S(1)} fusion(s32[4]{0:T(128)} %param.28, s32[]{:T(128)S(6)} %axis_index.15), kind=kLoop, calls=%fused_computation.172 | loop fusion | flops 64 | bytes 24 | tf_op jit(solution)/shard_map/eq | solution.py:114
  11.2 1.1 %multiply_reduce_fusion.1 = f32[128]{0:T(128)S(1)} fusion(bf16[128,1024]{1,0:T(8,128)(2,1)} %param.26), kind=kLoop, calls=%fused_computation.43 | loop fusion | flops 393088 | bytes 262656 | tf_op jit(solution)/shard_map/reduce_sum | solution.py:88
  12.3 0.1 broadcast_bitcast_fusion
  12.4 3.1 %broadcast_compare_fusion = (pred[128,2048]{1,0:T(8,128)(4,1)S(1)}, pred[128,2048]{1,0:T(8,128)(4,1)S(1)}, pred[128,2048]{1,0:T(8,128)(4,1)S(1)}, pred[128,2048]...) fusion(s32[128]{0:T(128)S(1)} %get-tuple-element.86, ...), kind=kLoop, calls=%fused_computation.44 | loop fusion | flops 11796480 | bytes 2380032 | tf_op jit(solution)/shard_map/eq | solution.py:23
  16.2 0.4 add_select_fusion.5
  16.6 0.0 all-to-all-done
  16.6 0.6 gather_fusion
  17.2 2.7 %collective-permute-start = (bf16[4,16,1024]{2,1,0:T(8,128)(2,1)S(1)}, bf16[4,16,1024]{2,1,0:T(8,128)(2,1)}, u32[]{:S(2)}, u32[]{:S(2)}) collective-permute-start(bf16[4,16,1024]{2,1,0:T(8,128)(2,1)S(1)} %gather_fusion), channel_id=1, source_target_pairs={{0,8},{8,0},{1,9},{9,1},{2,10},{10,2},{3,11},{11,3},{4,12},{12,4},... | collective-permute-start | bytes 393224 | tf_op jit(solution)/shard_map/ppermute | solution.py:111
  19.8 0.2 broadcast_in_dim.502
  20.1 0.2 reshape.130
  20.3 0.7 %slice_bitcast_fusion.9 = (bf16[9,2048]{1,0:T(8,128)(2,1)S(1)}, bf16[9,2048]{1,0:T(8,128)(2,1)S(1)}, bf16[9,2048]{1,0:T(8,128)(2,1)S(1)}, bf16[9,2048]{1,0:T(8,1...) fusion(bf16[9,9,2048]{2,0,1:T(8,128)(2,1)S(1)} %reshape.130), kind=kLoop, calls=%fused_computation.127 | loop fusion | bytes 663552 | tf_op jit(solution)/shard_map/jit(_where)/broadcast_in_dim | solution.py:29
  21.0 0.1 copy.88
  21.1 8.4 %select_select_fusion.1 = bf16[9,128,2048]{2,1,0:T(8,128)(2,1)} fusion(pred[128,2048]{1,0:T(8,128)(4,1)S(1)} %get-tuple-element.28, pred[128,2048]{1,0:T(8,128)(4,1)} %get-tuple-element.27, pred[128,2048]{1,0:T(8,128)(4,1)} %get-tuple-element.26, pred[128,2048]{1,0:T(8,128)(4,1)} %get-tuple-element.25, pred[128,2048]{1,0:T(8,128)(4,1)S(1)} %get-tuple-element.24, ...), kind=kLoop, calls=%fused_computation.5 | loop fusion | flops 21233664 | bytes 7409664 | tf_op jit(solution)/shard_map/jit(_where)/select_n | solution.py:29
  29.5 0.1 copy.81
  29.6 0.1 reshape.153
  29.7 1.0 %broadcast_select_fusion = bf16[4,16,1024]{2,1,0:T(8,128)(2,1)S(1)} fusion(bf16[4,16,1024]{2,1,0:T(8,128)(2,1)S(1)} %gather_fusion, bf16[4,16,1024]{2,1,0:T(8,128)(2,1)} %collective-permute-done, pred[4]{0:T(512)(128)(4,1)S(1)} %fusion.69), kind=kLoop, calls=%fused_computation.118 | loop fusion | flops 65536 | bytes 393220 | tf_op jit(solution)/shard_map/jit(_where)/select_n | solution.py:115
  30.6 1.4 %gather_fusion.1 = bf16[16,16,1024]{2,1,0:T(8,128)(2,1)} fusion(bf16[4,16,1024]{2,1,0:T(8,128)(2,1)S(1)} %broadcast_select_fusion, s32[1024]{0:T(1024)S(1)} %pad_clamp_fusion), kind=kCustom, calls=%fused_computation.1 | custom fusion | bytes 1048640 | tf_op jit(solution)/shard_map/gather | solution.py:116
  32.0 4.2 %all-to-all-start.1 = ((bf16[8,2,16,1024]{3,2,1,0:T(8,128)(2,1)}), bf16[8,2,16,1024]{3,2,1,0:T(8,128)(2,1)S(1)}, u32[]{:S(2)}, u32[]{:S(2)}) async-start(bf16[8,2,16,1024]{3,2,1,0:T(8,128)(2,1)} %bitcast.16), calls=%async_computation.1 | async-start | bytes 1048576 | tf_op jit(solution)/shard_map/all_to_all | solution.py:117
  36.2 0.8 %broadcast_compare_fusion.13 = (pred[128,1152]{1,0:T(8,128)(4,1)S(1)}, pred[128,1152]{1,0:T(8,128)(4,1)S(1)}, pred[128,1152]{1,0:T(8,128)(4,1)S(1)}, pred[128,11...) fusion(s32[128,1152]{1,0:T(8,128)S(1)} %add_select_fusion.5), kind=kLoop, calls=%fused_computation.66 | loop fusion | flops 1327104 | bytes 1916928 | tf_op jit(solution)/shard_map/eq | solution.py:23
  37.1 0.1 copy.85
  37.2 0.4 broadcast_in_dim.559
  37.6 0.2 reshape.133
  37.8 0.0 copy-start.1
  37.8 7.3 %select_select_fusion = bf16[16,128,1152]{2,1,0:T(8,128)(2,1)} fusion(pred[128,1152]{1,0:T(8,128)(4,1)S(1)} %get-tuple-element.42, pred[128,1152]{1,0:T(8,128)(4,1)S(1)} %get-tuple-element.43, pred[128,1152]{1,0:T(8,128)(4,1)S(1)} %get-tuple-element.44, pred[128,1152]{1,0:T(8,128)(4,1)S(1)} %get-tuple-element.45, pred[128,1152]{1,0:T(8,128)(4,1)S(1)} %get-tuple-element.46, ...), kind=kLoop, calls=%fused_computation.4 | loop fusion | flops 21233664 | bytes 6377472 | tf_op jit(solution)/shard_map/jit(_where)/select_n | solution.py:29
  45.2 0.3 fusion.39
  45.5 0.1 copy.83
  45.6 0.2 multiply_reduce_fusion
  45.8 0.1 sqrt.19
  45.9 0.1 fusion.57
  46.1 0.1 fusion.42
  46.2 0.1 fusion.45
  46.3 0.1 fusion.47
  46.5 0.1 fusion.49
  46.6 0.1 fusion.51
  46.8 0.1 fusion.54
  46.9 9.6 %fusion.13 = f32[4,128,1152]{2,1,0:T(8,128)S(1)} fusion(bf16[2048,1152,1]{1,0,2:T(8,128)(2,1)} %bitcast.93, bf16[4,128,1152]{2,1,0:T(8,128)(2,1)S(1)} %fusion.54, bf16[1152,2048]{1,0:T(8,128)(2,1)} %bitcast.95, f32[2048]{0:T(1024)S(1)} %broadcast_bitcast_fusion), kind=kOutput, calls=%fused_computation.33 | convolution fusion | flops 4834983936 | bytes 12984320 | tf_op jit(solution)/shard_map/vak,kn->van/dot_general | solution.py:74
  56.5 0.0 copy-start.6
  56.5 0.2 fusion.71
  56.7 0.4 copy-done.6
  57.1 0.3 fusion.33
  57.4 0.1 copy.89
  57.5 0.8 %copy.87 = f32[1,2,128,128]{3,2,1,0:T(8,128)} copy(f32[1,2,128,128]{2,3,1,0:T(8,128)S(1)} %fusion.56) | data formatting | bytes 262144 | tf_op jit(solution)/shard_map/broadcast_in_dim | solution.py:130
  (40 shorter events, 0.4 us)
Async XLA Ops:
  0.0 12.3 %copy-start = (f32[16]{0:T(128)S(1)}, f32[16]{0:T(128)}, u32[]{:S(2)}) copy-start(f32[16]{0:T(128)} %param.31) | copy-start | bytes 196
  0.0 15.5 %copy-start.2 = (bf16[16,1,3,3,3,3]{0,5,4,3,2,1:T(4,128)(2,1)S(1)}, bf16[16,1,3,3,3,3]{0,5,4,3,2,1:T(4,128)(2,1)}, u32[]{:S(2)}) copy-start(bf16[16,1,3,3,3,3]{0,5,4,3,2,1:T(4,128)(2,1)} %param.30) | copy-start | bytes 7780
  4.5 12.1 %all-to-all-start = ((bf16[8,16,1152]{2,1,0:T(8,128)(2,1)}), bf16[8,16,1152]{2,1,0:T(8,128)(2,1)S(1)}, u32[]{:S(2)}, u32[]{:S(2)}) async-start(bf16[8,16,1152]{2,1,0:T(8,128)(2,1)} %pad_maximum_fusion), calls=%async_computation | async-start | bytes 589824 | tf_op jit(solution)/shard_map/all_to_all | solution.py:106
  17.2 12.5 %collective-permute-start = (bf16[4,16,1024]{2,1,0:T(8,128)(2,1)S(1)}, bf16[4,16,1024]{2,1,0:T(8,128)(2,1)}, u32[]{:S(2)}, u32[]{:S(2)}) collective-permute-start(bf16[4,16,1024]{2,1,0:T(8,128)(2,1)S(1)} %gather_fusion), channel_id=1, source_target_pairs={{0,8},{8,0},{1,9},{9,1},{2,10},{10,2},{3,11},{11,3},{4,12},{12,4},... | collective-permute-start | bytes 393224 | tf_op jit(solution)/shard_map/ppermute | solution.py:111
  29.5 7.6 %copy-start.3 = (bf16[1,16,3,3,3,3]{1,5,4,3,2,0:T(4,128)(2,1)S(1)}, bf16[1,16,3,3,3,3]{1,5,4,3,2,0:T(4,128)(2,1)}, u32[]{:S(2)}) copy-start(bf16[1,16,3,3,3,3]{1,5,4,3,2,0:T(4,128)(2,1)} %param.32) | copy-start | bytes 7780
  32.0 13.1 %all-to-all-start.1 = ((bf16[8,2,16,1024]{3,2,1,0:T(8,128)(2,1)}), bf16[8,2,16,1024]{3,2,1,0:T(8,128)(2,1)S(1)}, u32[]{:S(2)}, u32[]{:S(2)}) async-start(bf16[8,2,16,1024]{3,2,1,0:T(8,128)(2,1)} %bitcast.16), calls=%async_computation.1 | async-start | bytes 1048576 | tf_op jit(solution)/shard_map/all_to_all | solution.py:117
  37.8 7.4 %copy-start.1 = (bf16[128,1024]{1,0:T(8,128)(2,1)S(1)}, bf16[128,1024]{1,0:T(8,128)(2,1)}, u32[]{:S(2)}) copy-start(bf16[128,1024]{1,0:T(8,128)(2,1)} %param.26) | copy-start | bytes 786436
  45.1 0.9 %copy-start.4 = (pred[128]{0:T(512)(128)(4,1)S(1)}, pred[128]{0:T(512)(128)(4,1)}, u32[]{:S(2)}) copy-start(pred[128]{0:T(512)(128)(4,1)} %constant.204) | copy-start | bytes 388
  45.1 1.1 %copy-start.5 = (pred[128]{0:T(512)(128)(4,1)S(1)}, pred[128]{0:T(512)(128)(4,1)}, u32[]{:S(2)}) copy-start(pred[128]{0:T(512)(128)(4,1)} %constant.205) | copy-start | bytes 388
  56.5 0.7 %copy-start.6 = (pred[128]{0:T(512)(128)(4,1)S(1)}, pred[128]{0:T(512)(128)(4,1)}, u32[]{:S(2)}) copy-start(pred[128]{0:T(512)(128)(4,1)} %constant.205) | copy-start | bytes 388

commit v15 on v13

--- a/solution.py
+++ b/solution.py
@@ -2,6 +2,7 @@
 import jax
 import jax.numpy as jnp
 from jax import lax
+from jax.experimental.layout import Layout, with_layout_constraint
 from jax.sharding import PartitionSpec as P
 
 HQ = 4
@@ -125,7 +126,9 @@
     volumes = jnp.concatenate([correlation, jnp.swapaxes(correlation, 1, 2)], axis=0)
     k2 = band_second(weight_second, parcel)
     filtered = consensus_stack(volumes, k1, k2, bias_first, bias_second)
-    return (filtered[:2] + jnp.swapaxes(filtered[2:], 1, 2))[None]
+    total = filtered[:2] + jnp.swapaxes(filtered[2:], 1, 2)
+    total = with_layout_constraint(total, Layout(major_to_minor=(0, 1, 2)))
+    return total[None]
 
 
 def solution(mesh):

time: 57.4 us -> 57.6 us (level)
  other arithmetic: 27 us -> 28.1 us
    broadcast_in_dim x1 -> x0, local copies, waits for them, and re-layouts: 0.76 us -> none  [per_device(): return (filtered[:2] + jnp.swapaxes(filtered[2:], 1, 2))[None]]
    broadcast_in_dim x1, other arithmetic: 0.02 us -> 0.67 us  [per_device(): return total[None]]
    unnamed x18 -> x17, local copies, waits for them, and re-layouts: 1.31 us -> 1.4 us
where the time goes in v15:
time: 57.6 us; the launch traced here: 57.1 us
  other arithmetic  28.1 us (49%)
  starting transfers between devices  12.1 us (21%)
  matrix products  9.8 us (17%)
  local copies, waits for them, and re-layouts  6.05 us (11%)
  between operations  1 us (2%)
    select_n x2, other arithmetic, banded(): band = jnp.where(masks[e][None], spread_w[:, e, None, :], band)  15.6 us
    dot_general x1, matrix products, consensus_stack(): jnp.einsum('vak,kn->van', hidden, k2, preferred_element_type=jnp.float32)  9.5 us
    all_to_all x1, starting transfers between devices, gather_sources(): arrived = lax.all_to_all(payload, 'sub', 0, 0)  5.28 us
    all_to_all x1, starting transfers between devices, gather_sources(): got = lax.all_to_all(parcel, 'sub', 0, 0)  4.2 us
    eq x2, other arithmetic, banded(): masks = tuple((table == e for e in range(TAPS)))  3.83 us
    ppermute x1, starting transfers between devices, gather_sources(): mirror = lax.ppermute(local, 'half', [(0, 1), (1, 0)])  2.65 us
    concatenate x1, other arithmetic, gather_sources(): jnp.concatenate([source_maps.reshape(sub, rows, channels), tag], axis=2)  1.68 us
    unnamed x17, local copies, waits for them, and re-layouts  1.4 us
  transfers between devices with their start and end apart: 3, of which 0 were waited for; matrix products, arithmetic and copies ran while one was open for 43% of the time, Pallas kernels for 0%

profile of v15, /device:TPU:0, one launch (start us, length us, event | category | flops | bytes accessed | tf_op | source)
XLA Modules:
  0.0 57.1 jit_solution(3282558196987666148)
XLA Ops:
  0.0 0.7 %convert_element_type.44 = bf16[1,2]{1,0:T(2,128)(2,1)S(1)} convert(s32[1,2]{1,0:T(1,128)} %param.31) | non-fusion elementwise | flops 2 | bytes 12 | tf_op jit(solution)/shard_map/convert_element_type | solution.py:103
  0.7 1.7 %pad_maximum_fusion = bf16[8,16,1152]{2,1,0:T(8,128)(2,1)} fusion(bf16[8,16,128]{2,1,0:T(8,128)(2,1)S(1)} %scatter.8, bf16[8,16,1024]{2,1,0:T(8,128)(2,1)} %bitcast.95), kind=kLoop, calls=%fused_computation.69 | loop fusion | flops 589824 | bytes 589824 | tf_op jit(solution)/shard_map/concatenate | solution.py:104
  2.4 5.3 %all-to-all-start = ((bf16[8,16,1152]{2,1,0:T(8,128)(2,1)}), bf16[8,16,1152]{2,1,0:T(8,128)(2,1)S(1)}, u32[]{:S(2)}, u32[]{:S(2)}) async-start(bf16[8,16,1152]{2,1,0:T(8,128)(2,1)} %pad_maximum_fusion), calls=%async_computation | async-start | bytes 589824 | tf_op jit(solution)/shard_map/all_to_all | solution.py:105
  7.7 0.7 %compare_select_fusion.1 = s32[4]{0:T(128)S(1)} fusion(s32[4]{0:T(128)} %param.30), kind=kLoop, calls=%fused_computation.155 | loop fusion | flops 56 | bytes 32 | tf_op jit(solution)/shard_map/select_n | solution.py:109
  8.4 0.7 %fusion.68 = pred[4]{0:T(512)(128)(4,1)S(1)} fusion(s32[4]{0:T(128)} %param.30, s32[]{:T(128)S(6)} %axis_index.15), kind=kLoop, calls=%fused_computation.167 | loop fusion | flops 64 | bytes 24 | tf_op jit(solution)/shard_map/eq | solution.py:113
  9.1 1.1 %multiply_reduce_fusion.1 = f32[128]{0:T(128)S(1)} fusion(bf16[128,1024]{1,0:T(8,128)(2,1)} %param.28), kind=kLoop, calls=%fused_computation.51 | loop fusion | flops 393088 | bytes 262656 | tf_op jit(solution)/shard_map/reduce_sum | solution.py:89
  10.2 0.1 broadcast_bitcast_fusion
  10.3 3.0 %broadcast_compare_fusion = (pred[128,2048]{1,0:T(8,128)(4,1)S(1)}, pred[128,2048]{1,0:T(8,128)(4,1)S(1)}, pred[128,2048]{1,0:T(8,128)(4,1)S(1)}, pred[128,2048]...) fusion(s32[128]{0:T(128)S(1)} %get-tuple-element.96, ...), kind=kLoop, calls=%fused_computation.52 | loop fusion | flops 11796480 | bytes 2380032 | tf_op jit(solution)/shard_map/eq | solution.py:24
  14.0 0.4 add_select_fusion.5
  14.4 0.0 all-to-all-done
  14.4 0.6 gather_fusion
  15.0 2.7 %collective-permute-start = (bf16[4,16,1024]{2,1,0:T(8,128)(2,1)S(1)}, bf16[4,16,1024]{2,1,0:T(8,128)(2,1)}, u32[]{:S(2)}, u32[]{:S(2)}) collective-permute-start(bf16[4,16,1024]{2,1,0:T(8,128)(2,1)S(1)} %gather_fusion), channel_id=1, source_target_pairs={{0,8},{8,0},{1,9},{9,1},{2,10},{10,2},{3,11},{11,3},{4,12},{12,4},... | collective-permute-start | bytes 393224 | tf_op jit(solution)/shard_map/ppermute | solution.py:110
  17.7 0.2 broadcast_in_dim.491
  17.9 0.2 reshape.172
  18.1 0.7 %slice_bitcast_fusion.9 = (bf16[9,2048]{1,0:T(8,128)(2,1)S(1)}, bf16[9,2048]{1,0:T(8,128)(2,1)S(1)}, bf16[9,2048]{1,0:T(8,128)(2,1)S(1)}, bf16[9,2048]{1,0:T(8,1...) fusion(bf16[9,9,2048]{2,0,1:T(8,128)(2,1)S(1)} %reshape.172), kind=kLoop, calls=%fused_computation.127 | loop fusion | bytes 663552 | tf_op jit(solution)/shard_map/jit(_where)/broadcast_in_dim | solution.py:30
  18.8 0.1 copy.151
  18.9 8.3 %select_select_fusion.1 = bf16[9,128,2048]{2,1,0:T(8,128)(2,1)} fusion(pred[128,2048]{1,0:T(8,128)(4,1)S(1)} %get-tuple-element.40, pred[128,2048]{1,0:T(8,128)(4,1)} %get-tuple-element.39, pred[128,2048]{1,0:T(8,128)(4,1)} %get-tuple-element.38, pred[128,2048]{1,0:T(8,128)(4,1)} %get-tuple-element.37, pred[128,2048]{1,0:T(8,128)(4,1)S(1)} %get-tuple-element.36, ...), kind=kLoop, calls=%fused_computation.5 | loop fusion | flops 21233664 | bytes 7409664 | tf_op jit(solution)/shard_map/jit(_where)/select_n | solution.py:30
  27.3 0.1 copy.133
  27.3 0.1 reshape.195
  27.4 0.0 collective-permute-done
  27.4 1.0 %broadcast_select_fusion = bf16[4,16,1024]{2,1,0:T(8,128)(2,1)S(1)} fusion(bf16[4,16,1024]{2,1,0:T(8,128)(2,1)S(1)} %gather_fusion, bf16[4,16,1024]{2,1,0:T(8,128)(2,1)} %collective-permute-done, pred[4]{0:T(512)(128)(4,1)S(1)} %fusion.68), kind=kLoop, calls=%fused_computation.118 | loop fusion | flops 65536 | bytes 393220 | tf_op jit(solution)/shard_map/jit(_where)/select_n | solution.py:114
  28.4 1.4 %gather_fusion.1 = bf16[16,16,1024]{2,1,0:T(8,128)(2,1)} fusion(bf16[4,16,1024]{2,1,0:T(8,128)(2,1)S(1)} %broadcast_select_fusion, s32[1024]{0:T(1024)S(1)} %pad_clamp_fusion), kind=kCustom, calls=%fused_computation.1 | custom fusion | bytes 1048640 | tf_op jit(solution)/shard_map/gather | solution.py:115
  29.8 4.2 %all-to-all-start.1 = ((bf16[8,2,16,1024]{3,2,1,0:T(8,128)(2,1)}), bf16[8,2,16,1024]{3,2,1,0:T(8,128)(2,1)S(1)}, u32[]{:S(2)}, u32[]{:S(2)}) async-start(bf16[8,2,16,1024]{3,2,1,0:T(8,128)(2,1)} %bitcast.14), calls=%async_computation.1 | async-start | bytes 1048576 | tf_op jit(solution)/shard_map/all_to_all | solution.py:116
  34.0 0.8 %broadcast_compare_fusion.13 = (pred[128,1152]{1,0:T(8,128)(4,1)S(1)}, pred[128,1152]{1,0:T(8,128)(4,1)S(1)}, pred[128,1152]{1,0:T(8,128)(4,1)S(1)}, pred[128,11...) fusion(s32[128,1152]{1,0:T(8,128)S(1)} %add_select_fusion.5), kind=kLoop, calls=%fused_computation.74 | loop fusion | flops 1327104 | bytes 1916928 | tf_op jit(solution)/shard_map/eq | solution.py:24
  34.9 0.1 copy.138
  35.0 0.4 broadcast_in_dim.548
  35.4 0.2 reshape.175
  35.6 0.0 copy-start.1
  35.6 7.3 %select_select_fusion = bf16[16,128,1152]{2,1,0:T(8,128)(2,1)} fusion(pred[128,1152]{1,0:T(8,128)(4,1)S(1)} %get-tuple-element.54, pred[128,1152]{1,0:T(8,128)(4,1)S(1)} %get-tuple-element.55, pred[128,1152]{1,0:T(8,128)(4,1)S(1)} %get-tuple-element.56, pred[128,1152]{1,0:T(8,128)(4,1)S(1)} %get-tuple-element.57, pred[128,1152]{1,0:T(8,128)(4,1)S(1)} %get-tuple-element.58, ...), kind=kLoop, calls=%fused_computation.4 | loop fusion | flops 21233664 | bytes 6377472 | tf_op jit(solution)/shard_map/jit(_where)/select_n | solution.py:30
  43.0 0.3 fusion.39
  43.3 0.1 copy.136
  43.4 0.2 multiply_reduce_fusion
  43.6 0.1 sqrt.19
  43.7 0.1 fusion.57
  43.9 0.1 fusion.42
  44.0 0.1 fusion.43
  44.1 0.1 fusion.45
  44.3 0.1 fusion.47
  44.4 0.1 fusion.49
  44.6 0.1 fusion.51
  44.7 0.1 fusion.52
  44.8 0.1 fusion.54
  45.0 1.0 %copy-done.4 = bf16[4,128,1152]{1,2,0:T(8,128)(2,1)} copy-done((bf16[4,128,1152]{1,2,0:T(8,128)(2,1)}, bf16[4,128,1152]{1,2,0:T(8,128)(2,1)S(1)}, u32[]{:S(2)}) %copy-start.4) | copy-done | bytes 1179672
  46.0 9.5 %fusion.13 = f32[4,128,1152]{1,2,0:T(8,128)S(1)} fusion(bf16[2048,1152,1]{1,0,2:T(8,128)(2,1)} %bitcast.91, bf16[4,128,1152]{1,2,0:T(8,128)(2,1)} %copy-done.4, bf16[1152,2048]{1,0:T(8,128)(2,1)} %bitcast.93, f32[2048]{0:T(1024)S(1)} %broadcast_bitcast_fusion), kind=kOutput, calls=%fused_computation.33 | convolution fusion | flops 4834983936 | bytes 12984320 | tf_op jit(solution)/shard_map/vak,kn->van/dot_general | solution.py:75
  55.5 0.2 fusion.70
  55.7 0.6 %fusion.33 = f32[4,128,128]{1,2,0:T(8,128)S(1)} fusion(f32[4,128,128]{1,2,0:T(8,128)S(1)} %get-tuple-element.52, f32[4,128,128]{1,2,0:T(8,128)S(1)} %get-tuple-element.51, f32[4,128,128]{1,2,0:T(8,128)S(1)} %get-tuple-element.50, f32[4,128,128]{1,2,0:T(8,128)S(1)} %get-tuple-element.49, f32[4,128,128]{1,2,0:T(8,128)S(1)} %get-tuple-element.48, ...), kind=kLoop, calls=%fused_computation.89 | loop fusion | flops 1048576 | bytes 2621700 | tf_op jit(solution)/shard_map/jit(relu)/max | solution.py:83
  56.3 0.1 copy.148
  56.4 0.7 %fusion.56 = f32[1,2,128,128]{3,2,1,0:T(8,128)} fusion(f32[2,128,128]{2,1,0:T(8,128)S(1)} %copy.148, f32[4,128,128]{1,2,0:T(8,128)S(1)} %fusion.33), kind=kLoop, calls=%fused_computation.113 | loop fusion | flops 32768 | bytes 393216 | tf_op jit(solution)/shard_map/broadcast_in_dim | solution.py:131
  (37 shorter events, 0.3 us)
Async XLA Ops:
  0.0 10.2 %copy-start = (f32[16]{0:T(128)S(1)}, f32[16]{0:T(128)}, u32[]{:S(2)}) copy-start(f32[16]{0:T(128)} %param.33) | copy-start | bytes 196
  0.0 13.3 %copy-start.2 = (bf16[16,1,3,3,3,3]{0,5,4,3,2,1:T(4,128)(2,1)S(1)}, bf16[16,1,3,3,3,3]{0,5,4,3,2,1:T(4,128)(2,1)}, u32[]{:S(2)}) copy-start(bf16[16,1,3,3,3,3]{0,5,4,3,2,1:T(4,128)(2,1)} %param.32) | copy-start | bytes 7780
  2.4 12.0 %all-to-all-start = ((bf16[8,16,1152]{2,1,0:T(8,128)(2,1)}), bf16[8,16,1152]{2,1,0:T(8,128)(2,1)S(1)}, u32[]{:S(2)}, u32[]{:S(2)}) async-start(bf16[8,16,1152]{2,1,0:T(8,128)(2,1)} %pad_maximum_fusion), calls=%async_computation | async-start | bytes 589824 | tf_op jit(solution)/shard_map/all_to_all | solution.py:105
  15.0 12.4 %collective-permute-start = (bf16[4,16,1024]{2,1,0:T(8,128)(2,1)S(1)}, bf16[4,16,1024]{2,1,0:T(8,128)(2,1)}, u32[]{:S(2)}, u32[]{:S(2)}) collective-permute-start(bf16[4,16,1024]{2,1,0:T(8,128)(2,1)S(1)} %gather_fusion), channel_id=1, source_target_pairs={{0,8},{8,0},{1,9},{9,1},{2,10},{10,2},{3,11},{11,3},{4,12},{12,4},... | collective-permute-start | bytes 393224 | tf_op jit(solution)/shard_map/ppermute | solution.py:110
  27.3 7.6 %copy-start.3 = (bf16[1,16,3,3,3,3]{1,5,4,3,2,0:T(4,128)(2,1)S(1)}, bf16[1,16,3,3,3,3]{1,5,4,3,2,0:T(4,128)(2,1)}, u32[]{:S(2)}) copy-start(bf16[1,16,3,3,3,3]{1,5,4,3,2,0:T(4,128)(2,1)} %param.34) | copy-start | bytes 7780
  29.8 13.1 %all-to-all-start.1 = ((bf16[8,2,16,1024]{3,2,1,0:T(8,128)(2,1)}), bf16[8,2,16,1024]{3,2,1,0:T(8,128)(2,1)S(1)}, u32[]{:S(2)}, u32[]{:S(2)}) async-start(bf16[8,2,16,1024]{3,2,1,0:T(8,128)(2,1)} %bitcast.14), calls=%async_computation.1 | async-start | bytes 1048576 | tf_op jit(solution)/shard_map/all_to_all | solution.py:116
  35.6 7.3 %copy-start.1 = (bf16[128,1024]{1,0:T(8,128)(2,1)S(1)}, bf16[128,1024]{1,0:T(8,128)(2,1)}, u32[]{:S(2)}) copy-start(bf16[128,1024]{1,0:T(8,128)(2,1)} %param.28) | copy-start | bytes 786436
  42.9 0.9 %copy-start.5 = (pred[128]{0:T(512)(128)(4,1)S(1)}, pred[128]{0:T(512)(128)(4,1)}, u32[]{:S(2)}) copy-start(pred[128]{0:T(512)(128)(4,1)} %constant.233) | copy-start | bytes 388
  42.9 1.2 %copy-start.6 = (pred[128]{0:T(512)(128)(4,1)S(1)}, pred[128]{0:T(512)(128)(4,1)}, u32[]{:S(2)}) copy-start(pred[128]{0:T(512)(128)(4,1)} %constant.234) | copy-start | bytes 388
  45.0 1.0 %copy-start.4 = (bf16[4,128,1152]{1,2,0:T(8,128)(2,1)}, bf16[4,128,1152]{1,2,0:T(8,128)(2,1)S(1)}, u32[]{:S(2)}) copy-start(bf16[4,128,1152]{1,2,0:T(8,128)(2,1)S(1)} %fusion.54) | copy-start | bytes 3538948

commit v16 on v13

--- a/solution.py
+++ b/solution.py
@@ -41,11 +41,8 @@
 def band_second(weight_second, tie):
     hid = weight_second.shape[1]
     cells = HQ * WQ
-    table, weight_second, _ = lax.optimization_barrier(
-        (tap_table(cells, TAPS * cells), weight_second, tie)
-    )
     w2 = weight_second.reshape(hid, TAPS, TAPS)
-    k2 = banded(jnp.transpose(w2, (0, 2, 1)), table, cells)
+    k2 = banded(jnp.transpose(w2, (0, 2, 1)), tap_table(cells, TAPS * cells), cells, tie)
     return k2.reshape(hid * cells, TAPS * cells)
 
 

time: 57.4 us -> 61.2 us (1.066)
  local copies, waits for them, and re-layouts: 6.62 us -> 8.83 us
  other arithmetic: 27 us -> 28 us
  waiting for transfers between devices: 0.01 us -> 0.74 us
    eq x2, other arithmetic: 3.83 us -> 5.28 us  [banded(): masks = tuple((table == e for e in range(TAPS)))]
    reshape x1, local copies, waits for them, and re-layouts: 0.03 us -> 1.39 us  [band_second(): w2 = weight_second.reshape(hid, TAPS, TAPS)]
    reshape x1, local copies, waits for them, and re-layouts: 0.02 us -> 0.77 us  [band_first(): w1 = weight_first.reshape(hid, TAPS, TAPS)]
    all_to_all x1, waiting for transfers between devices: 0.01 us -> 0.73 us  [gather_sources(): got = lax.all_to_all(parcel, 'sub', 0, 0)]
    gather x1, local copies, waits for them, and re-layouts: 0.56 us -> 1.21 us  [gather_sources(): local = chunks[hubs % sub]]
    unnamed x18 -> x32, local copies, waits for them, and re-layouts: 1.31 us -> 0.72 us
  transfers between devices with their start and end apart: 3 -> 3, of which waited for: 0 -> 1; matrix products, arithmetic and copies ran while one was open for 43% -> 45% of each run, Pallas kernels for 0% -> 0%
where the time goes in v16:
time: 61.2 us; the launch traced here: 60.6 us
  other arithmetic  28 us (46%)
  starting transfers between devices  12.1 us (20%)
  matrix products  9.85 us (16%)
  local copies, waits for them, and re-layouts  8.83 us (14%)
  between operations  1.09 us (2%)
  waiting for transfers between devices  0.74 us (1%)
    select_n x2, other arithmetic, banded(): band = jnp.where(masks[e][None], spread_w[:, e, None, :], band)  15.4 us
    dot_general x1, matrix products, consensus_stack(): jnp.einsum('vak,kn->van', hidden, k2, preferred_element_type=jnp.float32)  9.55 us
    all_to_all x1, starting transfers between devices, gather_sources(): arrived = lax.all_to_all(payload, 'sub', 0, 0)  5.28 us
    eq x2, other arithmetic, banded(): masks = tuple((table == e for e in range(TAPS)))  5.28 us
    all_to_all x1, starting transfers between devices, gather_sources(): got = lax.all_to_all(parcel, 'sub', 0, 0)  4.2 us
    ppermute x1, starting transfers between devices, gather_sources(): mirror = lax.ppermute(local, 'half', [(0, 1), (1, 0)])  2.59 us
    concatenate x1, other arithmetic, gather_sources(): jnp.concatenate([source_maps.reshape(sub, rows, channels), tag], axis=2)  1.69 us
    reshape x1, local copies, waits for them, and re-layouts, band_second(): w2 = weight_second.reshape(hid, TAPS, TAPS)  1.39 us
  transfers between devices with their start and end apart: 3, of which 1 were waited for; matrix products, arithmetic and copies ran while one was open for 45% of the time, Pallas kernels for 0%

profile of v16, /device:TPU:0, one launch (start us, length us, event | category | flops | bytes accessed | tf_op | source)
XLA Modules:
  0.0 60.6 jit_solution(17241674613057903074)
XLA Ops:
  0.0 0.7 %convert_element_type.44 = bf16[1,2]{1,0:T(2,128)(2,1)S(1)} convert(s32[1,2]{1,0:T(1,128)} %param.31) | non-fusion elementwise | flops 2 | bytes 12 | tf_op jit(solution)/shard_map/convert_element_type | solution.py:99
  0.7 1.7 %pad_maximum_fusion = bf16[8,16,1152]{2,1,0:T(8,128)(2,1)} fusion(bf16[8,16,128]{2,1,0:T(8,128)(2,1)S(1)} %scatter.8, bf16[8,16,1024]{2,1,0:T(8,128)(2,1)} %bitcast.95), kind=kLoop, calls=%fused_computation.61 | loop fusion | flops 589824 | bytes 589824 | tf_op jit(solution)/shard_map/concatenate | solution.py:100
  2.4 5.3 %all-to-all-start = ((bf16[8,16,1152]{2,1,0:T(8,128)(2,1)}), bf16[8,16,1152]{2,1,0:T(8,128)(2,1)S(1)}, u32[]{:S(2)}, u32[]{:S(2)}) async-start(bf16[8,16,1152]{2,1,0:T(8,128)(2,1)} %pad_maximum_fusion), calls=%async_computation | async-start | bytes 589824 | tf_op jit(solution)/shard_map/all_to_all | solution.py:101
  7.7 0.7 %compare_select_fusion.1 = s32[4]{0:T(128)S(1)} fusion(s32[4]{0:T(128)} %param.30), kind=kLoop, calls=%fused_computation.155 | loop fusion | flops 56 | bytes 32 | tf_op jit(solution)/shard_map/select_n | solution.py:105
  8.4 0.8 %reshape.171 = bf16[16,9,9]{0,2,1:T(8,128)(2,1)S(1)} reshape(bf16[16,1,3,3,3,3]{0,5,4,3,2,1:T(4,128)(2,1)} %param.32) | data formatting | bytes 5184 | tf_op jit(solution)/shard_map/reshape | solution.py:36
  9.2 0.7 %fusion.68 = pred[4]{0:T(512)(128)(4,1)S(1)} fusion(s32[4]{0:T(128)} %param.30, s32[]{:T(128)S(6)} %axis_index.15), kind=kLoop, calls=%fused_computation.167 | loop fusion | flops 64 | bytes 24 | tf_op jit(solution)/shard_map/eq | solution.py:109
  9.9 1.1 %multiply_reduce_fusion.1 = f32[128]{0:T(128)S(1)} fusion(bf16[128,1024]{1,0:T(8,128)(2,1)} %param.28), kind=kLoop, calls=%fused_computation.43 | loop fusion | flops 393088 | bytes 262656 | tf_op jit(solution)/shard_map/reduce_sum | solution.py:85
  11.0 1.4 %reshape.174 = bf16[16,9,9]{0,2,1:T(8,128)(2,1)} reshape(bf16[1,16,3,3,3,3]{1,5,4,3,2,0:T(4,128)(2,1)} %param.34) | data formatting | bytes 5184 | tf_op jit(solution)/shard_map/reshape | solution.py:44
  12.4 0.1 broadcast_bitcast_fusion
  13.1 3.0 %broadcast_compare_fusion = (pred[128,2048]{1,0:T(8,128)(4,1)S(1)}, pred[128,2048]{1,0:T(8,128)(4,1)S(1)}, pred[128,2048]{1,0:T(8,128)(4,1)S(1)}, pred[128,2048]...) fusion(s32[128]{0:T(128)S(1)} %get-tuple-element.112, ...), kind=kLoop, calls=%fused_computation.44 | loop fusion | flops 11796480 | bytes 2380032 | tf_op jit(solution)/shard_map/eq | solution.py:23
  16.1 2.3 %broadcast_compare_fusion.9 = (pred[128,1152]{1,0:T(8,128)(4,1)S(1)}, pred[128,1152]{1,0:T(8,128)(4,1)}, pred[128,1152]{1,0:T(8,128)(4,1)}, pred[128,1152]{1,0:T...) fusion(s32[128]{0:T(128)S(1)} %get-tuple-element.112, ...), kind=kLoop, calls=%fused_computation.62 | loop fusion | flops 6635520 | bytes 1339776 | tf_op jit(solution)/shard_map/eq | solution.py:23
  18.4 1.2 %gather_fusion = bf16[4,16,1024]{2,1,0:T(8,128)(2,1)} fusion(bf16[8,16,1024]{2,1,0:T(8,128)(2,1)S(1)} %slice.217, s32[1024]{0:T(1024)S(1)} %pad_clamp_fusion.1), kind=kCustom, calls=%fused_computation | custom fusion | bytes 262160 | tf_op jit(solution)/shard_map/gather | solution.py:105
  19.6 2.6 %collective-permute-start = (bf16[4,16,1024]{2,1,0:T(8,128)(2,1)}, bf16[4,16,1024]{2,1,0:T(8,128)(2,1)}, u32[]{:S(2)}, u32[]{:S(2)}) collective-permute-start(bf16[4,16,1024]{2,1,0:T(8,128)(2,1)} %gather_fusion), channel_id=1, source_target_pairs={{0,8},{8,0},{1,9},{9,1},{2,10},{10,2},{3,11},{11,3},{4,12},{12,4},... | collective-permute-start | bytes 393224 | tf_op jit(solution)/shard_map/ppermute | solution.py:106
  22.2 0.2 broadcast_in_dim.491
  22.4 0.2 reshape.172
  22.6 0.7 %slice_bitcast_fusion.9 = (bf16[9,2048]{1,0:T(8,128)(2,1)S(1)}, bf16[9,2048]{1,0:T(8,128)(2,1)S(1)}, bf16[9,2048]{1,0:T(8,128)(2,1)S(1)}, bf16[9,2048]{1,0:T(8,1...) fusion(bf16[9,9,2048]{2,0,1:T(8,128)(2,1)S(1)} %reshape.172), kind=kLoop, calls=%fused_computation.127 | loop fusion | bytes 663552 | tf_op jit(solution)/shard_map/jit(_where)/broadcast_in_dim | solution.py:29
  23.3 0.1 copy.88
  23.4 8.2 %select_select_fusion.1 = bf16[9,128,2048]{2,1,0:T(8,128)(2,1)} fusion(pred[128,2048]{1,0:T(8,128)(4,1)} %get-tuple-element.48, pred[128,2048]{1,0:T(8,128)(4,1)S(1)} %get-tuple-element.47, pred[128,2048]{1,0:T(8,128)(4,1)S(1)} %get-tuple-element.46, pred[128,2048]{1,0:T(8,128)(4,1)S(1)} %get-tuple-element.45, pred[128,2048]{1,0:T(8,128)(4,1)S(1)} %get-tuple-element.44, ...), kind=kLoop, calls=%fused_computation.5 | loop fusion | flops 21233664 | bytes 7409664 | tf_op jit(solution)/shard_map/jit(_where)/select_n | solution.py:29
  31.6 0.1 copy.81
  31.7 0.1 reshape.195
  31.8 0.0 collective-permute-done
  31.9 1.2 %broadcast_select_fusion = bf16[4,16,1024]{2,1,0:T(8,128)(2,1)S(1)} fusion(bf16[4,16,1024]{2,1,0:T(8,128)(2,1)} %gather_fusion, bf16[4,16,1024]{2,1,0:T(8,128)(2,1)} %collective-permute-done, pred[4]{0:T(512)(128)(4,1)S(1)} %fusion.68), kind=kLoop, calls=%fused_computation.118 | loop fusion | flops 65536 | bytes 393220 | tf_op jit(solution)/shard_map/jit(_where)/select_n | solution.py:110
  33.0 1.4 %gather_fusion.1 = bf16[16,16,1024]{2,1,0:T(8,128)(2,1)} fusion(bf16[4,16,1024]{2,1,0:T(8,128)(2,1)S(1)} %broadcast_select_fusion, s32[1024]{0:T(1024)S(1)} %pad_clamp_fusion), kind=kCustom, calls=%fused_computation.1 | custom fusion | bytes 1048640 | tf_op jit(solution)/shard_map/gather | solution.py:111
  34.4 4.2 %all-to-all-start.1 = ((bf16[8,2,16,1024]{3,2,1,0:T(8,128)(2,1)}), bf16[8,2,16,1024]{3,2,1,0:T(8,128)(2,1)S(1)}, u32[]{:S(2)}, u32[]{:S(2)}) async-start(bf16[8,2,16,1024]{3,2,1,0:T(8,128)(2,1)} %bitcast.14), calls=%async_computation.1 | async-start | bytes 1048576 | tf_op jit(solution)/shard_map/all_to_all | solution.py:112
  38.6 0.1 copy.85
  38.8 0.4 broadcast_in_dim.548
  39.1 0.2 reshape.175
  39.5 0.0 copy-start.1
  39.5 7.3 %select_select_fusion = bf16[16,128,1152]{2,1,0:T(8,128)(2,1)} fusion(pred[128,1152]{1,0:T(8,128)(4,1)S(1)} %copy-done.6, pred[128,1152]{1,0:T(8,128)(4,1)S(1)} %copy-done.7, pred[128,1152]{1,0:T(8,128)(4,1)S(1)} %copy-done.8, pred[128,1152]{1,0:T(8,128)(4,1)S(1)} %copy-done.9, pred[128,1152]{1,0:T(8,128)(4,1)S(1)} %copy-done.2, ...), kind=kLoop, calls=%fused_computation.4 | loop fusion | flops 21233664 | bytes 6377472 | tf_op jit(solution)/shard_map/jit(_where)/select_n | solution.py:29
  46.7 0.7 %all-to-all-done.1 = bf16[8,2,16,1024]{3,2,1,0:T(8,128)(2,1)S(1)} async-done(((bf16[8,2,16,1024]{3,2,1,0:T(8,128)(2,1)}), bf16[8,2,16,1024]{3,2,1,0:T(8,128)(2,1)S(1)}, u32[]{:S(2)}, u32[]{:S(2)}) %all-to-all-start.1) | async-done | bytes 524320 | tf_op jit(solution)/shard_map/all_to_all | solution.py:112
  47.5 0.3 fusion.39
  47.8 0.1 copy.83
  47.9 0.2 multiply_reduce_fusion
  48.1 0.1 sqrt.19
  48.2 0.1 fusion.57
  48.4 0.1 fusion.42
  48.6 0.1 fusion.45
  48.7 0.1 fusion.47
  48.8 0.1 fusion.49
  49.0 0.1 fusion.51
  49.1 0.1 fusion.54
  49.2 9.6 %fusion.13 = f32[4,128,1152]{2,1,0:T(8,128)S(1)} fusion(bf16[2048,1152,1]{1,0,2:T(8,128)(2,1)} %bitcast.91, bf16[4,128,1152]{2,1,0:T(8,128)(2,1)S(1)} %fusion.54, bf16[1152,2048]{1,0:T(8,128)(2,1)} %bitcast.93, f32[2048]{0:T(1024)S(1)} %broadcast_bitcast_fusion), kind=kOutput, calls=%fused_computation.33 | convolution fusion | flops 4834983936 | bytes 12984320 | tf_op jit(solution)/shard_map/vak,kn->van/dot_general | solution.py:71
  58.8 0.0 copy-start.13
  58.8 0.2 fusion.70
  59.1 0.4 copy-done.13
  59.5 0.3 fusion.33
  59.7 0.1 copy.89
  59.9 0.8 %copy.87 = f32[1,2,128,128]{3,2,1,0:T(8,128)} copy(f32[1,2,128,128]{2,3,1,0:T(8,128)S(1)} %fusion.56) | data formatting | bytes 262144 | tf_op jit(solution)/shard_map/broadcast_in_dim | solution.py:125
  (51 shorter events, 0.4 us)
Async XLA Ops:
  0.0 12.4 %copy-start = (f32[16]{0:T(128)S(1)}, f32[16]{0:T(128)}, u32[]{:S(2)}) copy-start(f32[16]{0:T(128)} %param.33) | copy-start | bytes 196
  2.4 16.0 %all-to-all-start = ((bf16[8,16,1152]{2,1,0:T(8,128)(2,1)}), bf16[8,16,1152]{2,1,0:T(8,128)(2,1)S(1)}, u32[]{:S(2)}, u32[]{:S(2)}) async-start(bf16[8,16,1152]{2,1,0:T(8,128)(2,1)} %pad_maximum_fusion), calls=%async_computation | async-start | bytes 589824 | tf_op jit(solution)/shard_map/all_to_all | solution.py:101
  19.6 12.2 %collective-permute-start = (bf16[4,16,1024]{2,1,0:T(8,128)(2,1)}, bf16[4,16,1024]{2,1,0:T(8,128)(2,1)}, u32[]{:S(2)}, u32[]{:S(2)}) collective-permute-start(bf16[4,16,1024]{2,1,0:T(8,128)(2,1)} %gather_fusion), channel_id=1, source_target_pairs={{0,8},{8,0},{1,9},{9,1},{2,10},{10,2},{3,11},{11,3},{4,12},{12,4},... | collective-permute-start | bytes 393224 | tf_op jit(solution)/shard_map/ppermute | solution.py:106
  31.6 7.0 %copy-start.10 = (bf16[16,9,9]{0,2,1:T(8,128)(2,1)S(1)}, bf16[16,9,9]{0,2,1:T(8,128)(2,1)}, u32[]{:S(2)}) copy-start(bf16[16,9,9]{0,2,1:T(8,128)(2,1)} %reshape.174) | copy-start | bytes 7780
  31.8 7.6 %copy-start.2 = (pred[128,1152]{1,0:T(8,128)(4,1)S(1)}, pred[128,1152]{1,0:T(8,128)(4,1)}, u32[]{:S(2)}) copy-start(pred[128,1152]{1,0:T(8,128)(4,1)} %get-tuple-element.56) | copy-start | bytes 442372
  31.8 7.6 %copy-start.3 = (pred[128,1152]{1,0:T(8,128)(4,1)S(1)}, pred[128,1152]{1,0:T(8,128)(4,1)}, u32[]{:S(2)}) copy-start(pred[128,1152]{1,0:T(8,128)(4,1)} %get-tuple-element.55) | copy-start | bytes 442372
  31.8 7.6 %copy-start.4 = (pred[128,1152]{1,0:T(8,128)(4,1)S(1)}, pred[128,1152]{1,0:T(8,128)(4,1)}, u32[]{:S(2)}) copy-start(pred[128,1152]{1,0:T(8,128)(4,1)} %get-tuple-element.54) | copy-start | bytes 442372
  31.8 7.6 %copy-start.5 = (pred[128,1152]{1,0:T(8,128)(4,1)S(1)}, pred[128,1152]{1,0:T(8,128)(4,1)}, u32[]{:S(2)}) copy-start(pred[128,1152]{1,0:T(8,128)(4,1)} %get-tuple-element.53) | copy-start | bytes 442372
  31.8 7.6 %copy-start.6 = (pred[128,1152]{1,0:T(8,128)(4,1)S(1)}, pred[128,1152]{1,0:T(8,128)(4,1)}, u32[]{:S(2)}) copy-start(pred[128,1152]{1,0:T(8,128)(4,1)} %get-tuple-element.60) | copy-start | bytes 442372
  31.8 7.6 %copy-start.7 = (pred[128,1152]{1,0:T(8,128)(4,1)S(1)}, pred[128,1152]{1,0:T(8,128)(4,1)}, u32[]{:S(2)}) copy-start(pred[128,1152]{1,0:T(8,128)(4,1)} %get-tuple-element.59) | copy-start | bytes 442372
  31.9 7.6 %copy-start.8 = (pred[128,1152]{1,0:T(8,128)(4,1)S(1)}, pred[128,1152]{1,0:T(8,128)(4,1)}, u32[]{:S(2)}) copy-start(pred[128,1152]{1,0:T(8,128)(4,1)} %get-tuple-element.58) | copy-start | bytes 442372
  31.9 7.6 %copy-start.9 = (pred[128,1152]{1,0:T(8,128)(4,1)S(1)}, pred[128,1152]{1,0:T(8,128)(4,1)}, u32[]{:S(2)}) copy-start(pred[128,1152]{1,0:T(8,128)(4,1)} %get-tuple-element.57) | copy-start | bytes 442372
  34.4 13.1 %all-to-all-start.1 = ((bf16[8,2,16,1024]{3,2,1,0:T(8,128)(2,1)}), bf16[8,2,16,1024]{3,2,1,0:T(8,128)(2,1)S(1)}, u32[]{:S(2)}, u32[]{:S(2)}) async-start(bf16[8,2,16,1024]{3,2,1,0:T(8,128)(2,1)} %bitcast.14), calls=%async_computation.1 | async-start | bytes 1048576 | tf_op jit(solution)/shard_map/all_to_all | solution.py:112
  39.5 8.1 %copy-start.1 = (bf16[128,1024]{1,0:T(8,128)(2,1)S(1)}, bf16[128,1024]{1,0:T(8,128)(2,1)}, u32[]{:S(2)}) copy-start(bf16[128,1024]{1,0:T(8,128)(2,1)} %param.28) | copy-start | bytes 786436
  46.7 1.7 %copy-start.11 = (pred[128]{0:T(512)(128)(4,1)S(1)}, pred[128]{0:T(512)(128)(4,1)}, u32[]{:S(2)}) copy-start(pred[128]{0:T(512)(128)(4,1)} %constant.233) | copy-start | bytes 388
  46.7 1.8 %copy-start.12 = (pred[128]{0:T(512)(128)(4,1)S(1)}, pred[128]{0:T(512)(128)(4,1)}, u32[]{:S(2)}) copy-start(pred[128]{0:T(512)(128)(4,1)} %constant.234) | copy-start | bytes 388
  58.8 0.7 %copy-start.13 = (pred[128]{0:T(512)(128)(4,1)S(1)}, pred[128]{0:T(512)(128)(4,1)}, u32[]{:S(2)}) copy-start(pred[128]{0:T(512)(128)(4,1)} %constant.234) | copy-start | bytes 388
